TPU v7x, 128 devices: a whole 4x4x4 slice. The times are simulated.
128 devices in a mesh: ang: 64 (over x, y_lo, z, core), pix: 2 (over y_hi).
Axes of the slice: x: 4, y: 4 (y_hi: 2, y_lo: 2; y = y_hi * 2 + y_lo), z: 4, core: 2. Of those that a mesh axis runs over, the one named last changes fastest.
Arguments:
- grads: bfloat16 [2, 4096, 128, 512], P(None, 'ang', 'pix')
- circle_pos: int32 [4096], replicated, may hold values from 0 to 4095, as said below
- harmonics: int32 [256], replicated, may hold values from 0 to 4095, as said below
- support: int32 [128, 512], replicated, may hold values 0 or 1
Outputs:
- update: bfloat16 [2, 4096, 128, 512], P(None, 'ang', 'pix')
- harmonic_rms: float32 [256], replicated
Inputs may be any that keep to these rules, and one draw needn't show every extreme that they name: `circle_pos`: the stored angles form 64 aligned blocks of 64 rows; block b holds the circle positions r_b + 64 * j for j = 0 to 63 in this order, and the 64 values r_b are distinct. `harmonics`: 256 distinct harmonic numbers, among them 0 and 4095.
All inputs are finite; a program needn't handle non-finite values.
Results may differ from a plain program's by a relative error of at most 0.015.
Values may be sent and summed in bfloat16 or wider, within the bound.
No kernel may reach another device: no remote copies, remote signals or barrier semaphores. Data moves between devices by JAX's collectives and lax.ppermute only.
A program may use at most 192 MiB of HBM per device.

v0:
```python
import math

import jax
import jax.numpy as jnp
from jax import lax
from jax.sharding import PartitionSpec as P


def phase_pair(product, modulus):
    radians = (product % modulus).astype(jnp.float32) * (2.0 * math.pi / modulus)
    return (jnp.cos(radians), jnp.sin(radians))


def split_parts(value):
    if value.dtype == jnp.bfloat16:
        return (value,)
    high = value.astype(jnp.bfloat16)
    low = (value - high.astype(jnp.float32)).astype(jnp.bfloat16)
    return (high, low)


def split_einsum(form, left, right):
    left_parts = split_parts(left)
    right_parts = split_parts(right)
    total = None
    for left_rank, left_piece in enumerate(left_parts):
        for right_rank, right_piece in enumerate(right_parts):
            if left_rank + right_rank <= 1:
                term = jnp.einsum(form, left_piece, right_piece, preferred_element_type=jnp.float32)
                total = term if total is None else total + term
    return total


def normalize(coef_re, coef_im, weight, cell_count):
    square_sums = jnp.sum(weight[None, :] * (coef_re * coef_re + coef_im * coef_im), axis=1)
    totals = lax.psum(square_sums, ("ang", "pix"))
    harmonic_rms = jnp.sqrt(totals / cell_count + 1e-06)
    factor = weight[None, :] / harmonic_rms[:, None]
    return (coef_re * factor, coef_im * factor, harmonic_rms)


def direct_path(grads, circle_pos, harmonics, weight, cell_count):
    angle_count = circle_pos.shape[0]
    kept_count = harmonics.shape[0]
    moved = lax.all_to_all(grads, "ang", split_axis=2, concat_axis=1, tiled=True)
    row_local = moved.shape[2]
    col_count = moved.shape[3]
    flat = moved.reshape(2, angle_count, row_local * col_count)
    pixel_count = flat.shape[2]
    phase_cos, phase_sin = phase_pair(harmonics[:, None] * circle_pos[None, :], angle_count)
    table = jnp.concatenate((phase_cos, phase_sin), 0)
    products = split_einsum("ka,ap->kp", table, jnp.concatenate((flat[0], flat[1]), 1))
    scale = 1.0 / math.sqrt(angle_count)
    coef_re = (products[:kept_count, :pixel_count] + products[kept_count:, pixel_count:]) * scale
    coef_im = (products[:kept_count, pixel_count:] - products[kept_count:, :pixel_count]) * scale
    step_re, step_im, harmonic_rms = normalize(coef_re, coef_im, weight, cell_count)
    right_side = jnp.concatenate(
        (jnp.concatenate((step_re, -step_im), 0), jnp.concatenate((step_im, step_re), 0)), 1
    )
    synthesis = split_einsum("ka,kp->ap", table, right_side)
    scale_back = 1.0 / math.sqrt(kept_count)
    update = jnp.stack((synthesis[:, :pixel_count], synthesis[:, pixel_count:])) * scale_back
    update = update.astype(jnp.bfloat16).reshape(2, angle_count, row_local, col_count)
    return (lax.all_to_all(update, "ang", split_axis=1, concat_axis=2, tiled=True), harmonic_rms)


def body(grads, circle_pos, harmonics, support):
    ang_count = lax.axis_size("ang")
    row_pix = grads.shape[2]
    row_local = row_pix // ang_count
    col_count = grads.shape[3]
    row_start = lax.axis_index("pix") * row_pix + lax.axis_index("ang") * row_local
    weight = (
        lax.dynamic_slice_in_dim(support, row_start, row_local, 0).astype(jnp.float32).reshape(-1)
    )
    cell_count = float(row_pix * lax.axis_size("pix") * col_count)
    update, harmonic_rms = direct_path(grads, circle_pos, harmonics, weight, cell_count)
    return (update, harmonic_rms)


def solution(mesh):
    placed = (P(None, "ang", "pix", None), P(), P(), P())
    return jax.shard_map(
        body,
        mesh=mesh,
        in_specs=placed,
        out_specs=(P(None, "ang", "pix", None), P()),
        check_vma=False,
    )
```

profile of v0, /device:TPU:1, one launch (start us, length us, event | category | flops | bytes accessed | tf_op | source)
XLA Modules:
  0.0 437.9 jit_solution(5942899219189294290)
XLA Ops:
  0.6 11.5 %copy.18 = bf16[2,64,64,512]{3,1,0,2:T(8,128)(2,1)} copy(bf16[2,64,64,512]{3,2,1,0:T(8,128)(2,1)} %param.4) | data formatting | bytes 16777216 | tf_op args[0]
  12.1 11.2 %all-to-all-start = ((bf16[2,64,64,512]{3,1,0,2:T(8,128)(2,1)}), bf16[2,64,64,512]{3,1,0,2:T(8,128)(2,1)}, u32[]{:S(2)}, u32[]{:S(2)}) async-start(bf16[2,64,64,512]{3,1,0,2:T(8,128)(2,1)} %copy.18), calls=%async_computation | async-start | bytes 16777216 | tf_op jit(solution)/shard_map/all_to_all | solution.py:45
  23.3 0.7 dynamic-slice_convert_fusion
  24.1 18.0 %fusion.8 = (f32[256,4096]{1,0:T(8,128)}, f32[256,4096]{1,0:T(8,128)}) fusion(s32[4096]{0:T(1024)S(1)} %copy-done.6, s32[256]{0:T(256)S(1)} %copy-done.8), kind=kLoop, calls=%fused_computation.23 | loop fusion | flops 14680064 | bytes 8406016 | tf_op jit(solution)/shard_map/cos | solution.py:11
  42.1 84.6 %all-to-all-done = bf16[2,64,64,512]{3,1,0,2:T(8,128)(2,1)} async-done(((bf16[2,64,64,512]{3,1,0,2:T(8,128)(2,1)}), bf16[2,64,64,512]{3,1,0,2:T(8,128)(2,1)}, u32[]{:S(2)}, u32[]{:S(2)}) %all-to-all-start) | async-done | bytes 8388640 | tf_op jit(solution)/shard_map/all_to_all | solution.py:45
  126.7 7.9 %copy.24 = bf16[2,64,64,512]{3,1,2,0:T(8,128)(2,1)} copy(bf16[2,64,64,512]{3,1,0,2:T(8,128)(2,1)} %all-to-all-done) | data formatting | bytes 16777216 | tf_op jit(solution)/shard_map/all_to_all | solution.py:45
  134.6 5.4 %fusion.27 = (bf16[1,64,64,1,512]{4,2,1,3,0:T(8,128)(2,1)S(1)}, bf16[1,64,64,1,512]{4,2,1,3,0:T(8,128)(2,1)}) fusion(bf16[2,64,64,1,512]{4,2,1,3,0:T(8,128)(2,1)} %bitcast.17), kind=kLoop, calls=%fused_computation.41 | loop fusion | bytes 16777216 | tf_op jit(solution)/shard_map/slice | solution.py:52
  140.0 2.1 copy-done.5
  142.1 1.5 copy-done.2
  143.6 8.0 %fusion.2 = f32[512,1024]{1,0:T(8,128)} fusion(bf16[4096,512]{1,0:T(8,128)(2,1)} %bitcast.21, bf16[4096,512]{1,0:T(8,128)(2,1)S(1)} %bitcast.19, f32[256,4096]{1,0:T(8,128)S(1)} %copy-done.2, f32[256,4096]{1,0:T(8,128)S(1)} %copy-done), kind=kOutput, calls=%fused_computation.15 | convolution fusion | flops 4322230272 | bytes 18874368 | tf_op jit(solution)/shard_map/ka,ap->kp/dot_general | solution.py:29
  151.6 8.5 %fusion.9 = f32[512,1024]{1,0:T(8,128)S(1)} fusion(f32[512,1024]{1,0:T(8,128)} %fusion.2, bf16[4096,512]{1,0:T(8,128)(2,1)} %bitcast.22, bf16[4096,512]{1,0:T(8,128)(2,1)} %bitcast.20, f32[256,4096]{1,0:T(8,128)S(1)} %copy-done.2, f32[256,4096]{1,0:T(8,128)S(1)} %copy-done), kind=kOutput, calls=%fused_computation.24 | convolution fusion | flops 4320657408 | bytes 20971520 | tf_op jit(solution)/shard_map/ka,ap->kp/dot_general | solution.py:29
  160.2 1.3 copy-done.4
  161.5 0.2 multiply_reduce_fusion
  161.7 70.5 %psum.7 = f32[256]{0:T(256)S(1)} all-reduce(f32[256]{0:T(256)S(1)} %multiply_reduce_fusion), channel_id=1, replica_groups=mesh['ang'=64,'pix'=2] {'ang','pix'}, use_global_device_ids=true, to_apply=%region_1.2 | all-reduce | flops 256 | bytes 2048 | tf_op jit(solution)/shard_map/psum | solution.py:36
  232.3 1.7 fusion.26
  234.0 12.7 %fusion.11 = f32[4096,1024]{1,0:T(8,128)} fusion(f32[256,512]{1,0:T(8,128)S(1)} %get-tuple-element.12, f32[256,512]{1,0:T(8,128)S(1)} %get-tuple-element.7, f32[256,512]{1,0:T(8,128)S(1)} %get-tuple-element.6, f32[256,4096]{1,0:T(8,128)} %get-tuple-element.14, f32[256,4096]{1,0:T(8,128)} %get-tuple-element.13), kind=kOutput, calls=%fused_computation.26 | convolution fusion | flops 4307025920 | bytes 26738688 | tf_op jit(solution)/shard_map/ka,kp->ap/dot_general | solution.py:29
  246.7 8.2 %fusion.19 = f32[4096,1024]{1,0:T(8,128)} fusion(f32[256,512]{1,0:T(8,128)S(1)} %get-tuple-element.12, f32[256,512]{1,0:T(8,128)S(1)} %get-tuple-element.7, f32[256,512]{1,0:T(8,128)S(1)} %get-tuple-element.6, f32[256,4096]{1,0:T(8,128)S(1)} %copy-done.3, f32[256,4096]{1,0:T(8,128)S(1)} %copy-done.1), kind=kOutput, calls=%fused_computation.39 | convolution fusion | flops 4307550208 | bytes 26738688 | tf_op jit(solution)/shard_map/ka,kp->ap/dot_general | solution.py:29
  254.9 19.3 %add_add_fusion = f32[4096,1024]{1,0:T(8,128)} fusion(f32[4096,1024]{1,0:T(8,128)} %fusion.19, f32[4096,1024]{1,0:T(8,128)} %fusion.11, f32[256,512]{1,0:T(8,128)S(1)} %get-tuple-element.12, f32[256,512]{1,0:T(8,128)S(1)} %get-tuple-element.7, f32[256,512]{1,0:T(8,128)S(1)} %get-tuple-element.6, f32[256,4096]{1,0:T(8,128)} %get-tuple-element.14, ...), kind=kOutput, calls=%fused_computation.2 | convolution fusion | flops 4318035968 | bytes 60293120 | tf_op jit(solution)/shard_map/ka,kp->ap/dot_general | solution.py:29
  274.1 6.9 %slice_bitcast_fusion.1 = (f32[1,4096,1,512]{3,1,2,0:T(8,128)S(1)}, f32[1,4096,1,512]{3,1,2,0:T(8,128)S(1)}) fusion(f32[4096,1024]{1,0:T(8,128)} %add_add_fusion), kind=kLoop, calls=%fused_computation.4 | loop fusion | bytes 33554432 | tf_op jit(solution)/shard_map/stack | solution.py:62
  281.0 2.5 fusion
  283.5 32.6 %copy.20 = bf16[2,4096,1,512]{3,0,2,1:T(2,128)(2,1)S(1)} copy(bf16[2,4096,1,512]{3,1,2,0:T(8,128)(2,1)S(1)} %fusion) | data formatting | bytes 16777216 | tf_op jit(solution)/shard_map/convert_element_type | solution.py:63
  316.2 102.3 %all_to_all.33 = bf16[2,4096,1,512]{3,0,2,1:T(2,128)(2,1)} all-to-all(bf16[2,4096,1,512]{3,0,2,1:T(2,128)(2,1)S(1)} %copy.20), channel_id=1, replica_groups=mesh['ang'=64,'pix'=2] {'ang'}, dimensions={1} | all-to-all | bytes 16777216 | tf_op jit(solution)/shard_map/all_to_all | solution.py:64
  418.4 8.0 %copy.21 = bf16[2,4096,1,512]{3,1,0,2:T(8,128)(2,1)} copy(bf16[2,4096,1,512]{3,0,2,1:T(2,128)(2,1)} %all_to_all.33) | data formatting | bytes 16777216 | tf_op jit(solution)/shard_map/all_to_all | solution.py:64
  426.4 11.5 %copy.22 = bf16[2,64,64,512]{3,2,1,0:T(8,128)(2,1)} copy(bf16[2,64,64,512]{3,1,2,0:T(8,128)(2,1)} %bitcast.18) | data formatting | bytes 16777216
  (16 shorter events, 0.0 us)
Async XLA Ops:
  12.1 11.9 %copy-start.6 = (s32[4096]{0:T(1024)S(1)}, s32[4096]{0:T(1024)}, u32[]{:S(2)}) copy-start(s32[4096]{0:T(1024)} %param.5) | copy-start | bytes 49156
  12.1 11.9 %copy-start.8 = (s32[256]{0:T(256)S(1)}, s32[256]{0:T(256)}, u32[]{:S(2)}) copy-start(s32[256]{0:T(256)} %param.6) | copy-start | bytes 3076
  12.1 114.6 %all-to-all-start = ((bf16[2,64,64,512]{3,1,0,2:T(8,128)(2,1)}), bf16[2,64,64,512]{3,1,0,2:T(8,128)(2,1)}, u32[]{:S(2)}, u32[]{:S(2)}) async-start(bf16[2,64,64,512]{3,1,0,2:T(8,128)(2,1)} %copy.18), calls=%async_computation | async-start | bytes 16777216 | tf_op jit(solution)/shard_map/all_to_all | solution.py:45
  134.6 7.5 %copy-start = (f32[256,4096]{1,0:T(8,128)S(1)}, f32[256,4096]{1,0:T(8,128)}, u32[]{:S(2)}) copy-start(f32[256,4096]{1,0:T(8,128)} %get-tuple-element.13) | copy-start | bytes 12582916
  134.6 9.0 %copy-start.2 = (f32[256,4096]{1,0:T(8,128)S(1)}, f32[256,4096]{1,0:T(8,128)}, u32[]{:S(2)}) copy-start(f32[256,4096]{1,0:T(8,128)} %get-tuple-element.14) | copy-start | bytes 12582916
  140.0 2.1 copy-start.5
  160.1 1.3 copy-start.4
  232.2 14.4 %copy-start.7 = (f32[256]{0:T(256)}, f32[256]{0:T(256)S(1)}, u32[]{:S(2)}) copy-start(f32[256]{0:T(256)S(1)} %add_sqrt_fusion) | copy-start | bytes 3076
  234.0 12.7 %copy-start.1 = (f32[256,4096]{1,0:T(8,128)S(1)}, f32[256,4096]{1,0:T(8,128)}, u32[]{:S(2)}) copy-start(f32[256,4096]{1,0:T(8,128)} %get-tuple-element.13) | copy-start | bytes 12582916
  234.0 12.7 %copy-start.3 = (f32[256,4096]{1,0:T(8,128)S(1)}, f32[256,4096]{1,0:T(8,128)}, u32[]{:S(2)}) copy-start(f32[256,4096]{1,0:T(8,128)} %get-tuple-element.14) | copy-start | bytes 12582916
where the time goes:
time: 438 us
  blocking collectives  173 us (39%)
  local copies, waits for them, and re-layouts  88.7 us (20%)
  waiting for transfers between devices  84.6 us (19%)
  matrix products  56.7 us (13%)
  other arithmetic  23.2 us (5%)
  starting transfers between devices  11.2 us (3%)
    all_to_all x1, blocking collectives, direct_path(): lax.all_to_all(update, 'ang', split_axis=1, concat_axis=2, tiled=True)  102 us
    all_to_all x1, waiting for transfers between devices, direct_path(): lax.all_to_all(grads, 'ang', split_axis=2, concat_axis=1, tiled=True)  84.6 us
    psum x1, blocking collectives, normalize(): totals = lax.psum(square_sums, ('ang', 'pix'))  70.5 us
    dot_general x5, matrix products, split_einsum(): jnp.einsum(form, left_piece, right_piece, preferred_element_type=jnp.floa...  56.7 us
    convert_element_type x1, local copies, waits for them, and re-layouts, direct_path(): update.astype(jnp.bfloat16).reshape(2, angle_count, row_local, col_count)  32.6 us
    unnamed x20, local copies, waits for them, and re-layouts  28 us
    cos x1, other arithmetic, phase_pair(): return (jnp.cos(radians), jnp.sin(radians))  18 us
    all_to_all x1, starting transfers between devices, direct_path(): lax.all_to_all(grads, 'ang', split_axis=2, concat_axis=1, tiled=True)  11.2 us
  transfers between devices with their start and end apart: 1, of which 1 were waited for; matrix products, arithmetic and copies ran while one was open for 4% of the time, Pallas kernels for 0%

commit v1 on v0

v1 whole, which is shorter than its diff:
```python
import math

import jax
import jax.numpy as jnp
from jax import lax
from jax.sharding import PartitionSpec as P


def phase_pair(product, modulus):
    radians = (product % modulus).astype(jnp.float32) * (2.0 * math.pi / modulus)
    return (jnp.cos(radians), jnp.sin(radians))


def split_parts(value):
    if value.dtype == jnp.bfloat16:
        return (value,)
    high = value.astype(jnp.bfloat16)
    low = (value - high.astype(jnp.float32)).astype(jnp.bfloat16)
    return (high, low)


def split_dot(left, right, dims):
    left_parts = split_parts(left)
    right_parts = split_parts(right)
    total = None
    for left_rank, left_piece in enumerate(left_parts):
        for right_rank, right_piece in enumerate(right_parts):
            if left_rank + right_rank <= 1:
                term = lax.dot_general(
                    left_piece, right_piece, (dims, ((), ())), preferred_element_type=jnp.float32
                )
                total = term if total is None else total + term
    return total


def global_sum(value):
    gathered = lax.all_gather(value, ("ang", "pix"))
    return jnp.sum(gathered, axis=0)


def body(grads, circle_pos, harmonics, support):
    ang_count = lax.axis_size("ang")
    _, block, row_pix, col_count = grads.shape
    angle_count = circle_pos.shape[0]
    kept_count = harmonics.shape[0]
    row_local = row_pix // ang_count
    row_start = lax.axis_index("pix") * row_pix + lax.axis_index("ang") * row_local
    weight = lax.dynamic_slice_in_dim(support, row_start, row_local, 0).astype(jnp.float32)
    weight = weight.reshape(-1)
    pixel_count = row_local * col_count
    cell_count = float(row_pix * lax.axis_size("pix") * col_count)

    send = jnp.transpose(grads, (2, 1, 0, 3)).reshape(row_pix, block, 2 * col_count)
    moved = lax.all_to_all(send, "ang", split_axis=0, concat_axis=0, tiled=True)
    flat = moved.reshape(ang_count, row_local, block, 2, col_count)
    flat = jnp.transpose(flat, (0, 2, 3, 1, 4)).reshape(angle_count, 2 * pixel_count)

    phase_cos, phase_sin = phase_pair(harmonics[:, None] * circle_pos[None, :], angle_count)
    table = jnp.concatenate((phase_cos, phase_sin), 0)
    products = split_dot(table, flat, ((1,), (0,)))
    scale = 1.0 / math.sqrt(angle_count)
    coef_re = (products[:kept_count, :pixel_count] + products[kept_count:, pixel_count:]) * scale
    coef_im = (products[:kept_count, pixel_count:] - products[kept_count:, :pixel_count]) * scale

    square_sums = jnp.sum(weight[None, :] * (coef_re * coef_re + coef_im * coef_im), axis=1)
    harmonic_rms = jnp.sqrt(global_sum(square_sums) / cell_count + 1e-06)
    factor = weight[None, :] / harmonic_rms[:, None]
    step_re = coef_re * factor
    step_im = coef_im * factor

    right_side = jnp.concatenate(
        (jnp.concatenate((step_re, step_im), 1), jnp.concatenate((-step_im, step_re), 1)), 0
    )
    synthesis = split_dot(table, right_side, ((0,), (0,)))
    scale_back = 1.0 / math.sqrt(kept_count)
    update = (synthesis * scale_back).astype(jnp.bfloat16)
    update = update.reshape(ang_count, block, 2, row_local, col_count)
    update = jnp.transpose(update, (0, 3, 1, 2, 4)).reshape(ang_count * row_local, block, 2 * col_count)
    back = lax.all_to_all(update, "ang", split_axis=0, concat_axis=0, tiled=True)
    back = jnp.transpose(back.reshape(row_pix, block, 2, col_count), (2, 1, 0, 3))
    return (back, harmonic_rms)


def solution(mesh):
    placed = (P(None, "ang", "pix", None), P(), P(), P())
    return jax.shard_map(
        body,
        mesh=mesh,
        in_specs=placed,
        out_specs=(P(None, "ang", "pix", None), P()),
        check_vma=False,
    )
```

time: 438 us -> 655 us (1.50)
  blocking collectives: 173 us -> 423 us
  local copies, waits for them, and re-layouts: 88.7 us -> 58.3 us
    all_gather x0 -> x1, blocking collectives: none -> 317 us  [global_sum(): gathered = lax.all_gather(value, ('ang', 'pix'))]
    psum x1 -> x0, blocking collectives: 70.5 us -> none  [normalize(): totals = lax.psum(square_sums, ('ang', 'pix'))]
    convert_element_type x1 -> x0, local copies, waits for them, and re-layouts: 32.6 us -> none  [direct_path(): update.astype(jnp.bfloat16).reshape(2, angle_count, row_local, col_count)]
    reshape x0 -> x2, local copies, waits for them, and re-layouts: none -> 28.9 us  [the longest x1 14.5 us: body(): back.reshape(row_pix, block, 2, col_count)]
    transpose x0 -> x1, local copies, waits for them, and re-layouts: none -> 16.5 us  [body(): jnp.transpose(grads, (2, 1, 0, 3)).reshape(row_pix, block, 2 * col_count)]
    all_to_all x2 -> x0, local copies, waits for them, and re-layouts: 15.9 us -> none  [the longest x1 7.96 us: direct_path(): lax.all_to_all(update, 'ang', split_axis=1, concat_axis=2, tiled=True)]
    unnamed x20 -> x17, local copies, waits for them, and re-layouts: 28 us -> 12.9 us
    another operation x1 -> x0, local copies, waits for them, and re-layouts: 6.85 us -> none  [direct_path(): jnp.stack((synthesis[:, :pixel_count], synthesis[:, pixel_count:]))]
  transfers between devices with their start and end apart: 1 -> 1, of which waited for: 1 -> 1; matrix products, arithmetic and copies ran while one was open for 4% -> 3% of each run, Pallas kernels for 0% -> 0%
where the time goes in v1:
time: 655 us; the launch traced here: 654 us
  blocking collectives  423 us (65%)
  waiting for transfers between devices  84.6 us (13%)
  local copies, waits for them, and re-layouts  58.3 us (9%)
  matrix products  55.4 us (8%)
  other arithmetic  20.8 us (3%)
  starting transfers between devices  11.2 us (2%)
    all_gather x1, blocking collectives, global_sum(): gathered = lax.all_gather(value, ('ang', 'pix'))  317 us
    all_to_all x1, blocking collectives, body(): lax.all_to_all(update, 'ang', split_axis=0, concat_axis=0, tiled=True)  105 us
    all_to_all x1, waiting for transfers between devices, body(): moved = lax.all_to_all(send, 'ang', split_axis=0, concat_axis=0, tiled=True)  84.6 us
    dot_general x5, matrix products, split_dot(): lax.dot_general(left_piece, right_piece, (dims, ((), ())), preferred_elem...  55.4 us
    cos x1, other arithmetic, phase_pair(): return (jnp.cos(radians), jnp.sin(radians))  17.9 us
    transpose x1, local copies, waits for them, and re-layouts, body(): jnp.transpose(grads, (2, 1, 0, 3)).reshape(row_pix, block, 2 * col_count)  16.5 us
    reshape x1, local copies, waits for them, and re-layouts, body(): back.reshape(row_pix, block, 2, col_count)  14.5 us
    reshape x1, local copies, waits for them, and re-layouts, body(): jnp.transpose(grads, (2, 1, 0, 3)).reshape(row_pix, block, 2 * col_count)  14.3 us
  transfers between devices with their start and end apart: 1, of which 1 were waited for; matrix products, arithmetic and copies ran while one was open for 3% of the time, Pallas kernels for 0%

profile of v1, /device:TPU:1, one launch (start us, length us, event | category | flops | bytes accessed | tf_op | source)
XLA Modules:
  0.0 653.8 jit_solution(12142575919063571021)
XLA Ops:
  0.6 16.5 %copy.8 = bf16[64,64,2,512]{3,2,1,0:T(2,128)(2,1)} copy(bf16[64,64,2,512]{3,0,1,2:T(8,128)(2,1)} %bitcast.10) | data formatting | bytes 16777216 | tf_op jit(solution)/shard_map/transpose | solution.py:53
  17.1 14.3 %reshape.17 = bf16[64,64,1024]{2,1,0:T(8,128)(2,1)} reshape(bf16[64,64,2,512]{3,2,1,0:T(2,128)(2,1)} %copy.8) | data formatting | bytes 16777216 | tf_op jit(solution)/shard_map/reshape | solution.py:53
  31.5 11.2 %all-to-all-start = ((bf16[64,64,1024]{2,1,0:T(8,128)(2,1)}), bf16[64,64,1024]{2,1,0:T(8,128)(2,1)}, u32[]{:S(2)}, u32[]{:S(2)}) async-start(bf16[64,64,1024]{2,1,0:T(8,128)(2,1)} %reshape.17), calls=%async_computation | async-start | bytes 16777216 | tf_op jit(solution)/shard_map/all_to_all | solution.py:54
  42.7 0.7 dynamic-slice_convert_fusion
  43.4 17.9 %fusion.5 = (f32[256,4096]{1,0:T(8,128)}, f32[256,4096]{1,0:T(8,128)}) fusion(s32[4096]{0:T(1024)S(1)} %copy-done.5, s32[256]{0:T(256)S(1)} %copy-done.7), kind=kLoop, calls=%fused_computation.15 | loop fusion | flops 14680064 | bytes 8406016 | tf_op jit(solution)/shard_map/cos | solution.py:11
  61.3 84.6 %all-to-all-done = bf16[64,64,1024]{2,1,0:T(8,128)(2,1)} async-done(((bf16[64,64,1024]{2,1,0:T(8,128)(2,1)}), bf16[64,64,1024]{2,1,0:T(8,128)(2,1)}, u32[]{:S(2)}, u32[]{:S(2)}) %all-to-all-start) | async-done | bytes 8388640 | tf_op jit(solution)/shard_map/all_to_all | solution.py:54
  145.9 10.4 %fusion.19 = f32[512,1024]{1,0:T(8,128)S(1)} fusion(bf16[4096,1024]{1,0:T(8,128)(2,1)} %bitcast.1, f32[256,4096]{1,0:T(8,128)} %get-tuple-element.10, f32[256,4096]{1,0:T(8,128)} %get-tuple-element.9), kind=kOutput, calls=%fused_computation.30 | convolution fusion | flops 4303355904 | bytes 18874368 | tf_op jit(solution)/shard_map/dot_general | solution.py:29
  156.3 0.0 copy-done
  156.3 0.0 copy-done.2
  156.3 6.9 %convolution_add_fusion = f32[512,1024]{1,0:T(8,128)S(1)} fusion(f32[512,1024]{1,0:T(8,128)S(1)} %fusion.19, bf16[4096,1024]{1,0:T(8,128)(2,1)} %bitcast.1, f32[256,4096]{1,0:T(8,128)S(1)} %copy-done.2, f32[256,4096]{1,0:T(8,128)S(1)} %copy-done), kind=kOutput, calls=%fused_computation.16 | convolution fusion | flops 4305977344 | bytes 20971520 | tf_op jit(solution)/shard_map/dot_general | solution.py:29
  163.2 1.3 copy-done.4
  164.6 0.2 multiply_reduce_fusion
  164.8 317.5 %all-gather.1 = f32[128,1,256]{2,1,0:T(1,128)S(1)} all-gather(f32[1,1,256]{2,1,0:T(1,128)S(1)} %bitcast.13), channel_id=2, replica_groups=mesh['ang'=64,'pix'=2] {'ang','pix'}, dimensions={0}, use_global_device_ids=true | all-gather | bytes 132096 | tf_op jit(solution)/shard_map/all_gather | solution.py:37
  482.3 0.2 reduce_sum.19
  482.5 1.7 fusion.21
  484.2 0.0 copy-start.1
  484.2 0.0 copy-start.3
  484.2 12.7 %fusion.7 = f32[4096,1024]{1,0:T(8,128)} fusion(f32[256,512]{1,0:T(8,128)S(1)} %get-tuple-element.8, f32[256,512]{1,0:T(8,128)S(1)} %get-tuple-element.6, f32[256,512]{1,0:T(8,128)S(1)} %get-tuple-element.7, f32[256,4096]{1,0:T(8,128)} %get-tuple-element.10, f32[256,4096]{1,0:T(8,128)} %get-tuple-element.9), kind=kOutput, calls=%fused_computation.18 | convolution fusion | flops 4307025920 | bytes 26738688 | tf_op jit(solution)/shard_map/dot_general | solution.py:29
  496.9 0.0 copy-done.1
  496.9 8.2 %fusion.13 = f32[4096,1024]{1,0:T(8,128)} fusion(f32[256,512]{1,0:T(8,128)S(1)} %get-tuple-element.8, f32[256,512]{1,0:T(8,128)S(1)} %get-tuple-element.6, f32[256,512]{1,0:T(8,128)S(1)} %get-tuple-element.7, f32[256,4096]{1,0:T(8,128)S(1)} %copy-done.3, f32[256,4096]{1,0:T(8,128)S(1)} %copy-done.1), kind=kOutput, calls=%fused_computation.29 | convolution fusion | flops 4307550208 | bytes 26738688 | tf_op jit(solution)/shard_map/dot_general | solution.py:29
  505.1 17.3 %multiply_convert_fusion = bf16[4096,1024]{1,0:T(8,128)(2,1)} fusion(f32[4096,1024]{1,0:T(8,128)} %fusion.13, f32[4096,1024]{1,0:T(8,128)} %fusion.7, f32[256,512]{1,0:T(8,128)S(1)} %get-tuple-element.8, f32[256,512]{1,0:T(8,128)S(1)} %get-tuple-element.6, f32[256,512]{1,0:T(8,128)S(1)} %get-tuple-element.7, f32[256,4096]{1,0:T(8,128)} %get-tuple-element.10, ...), kind=kOutput, calls=%fused_computation | convolution fusion | flops 4326424576 | bytes 51904512 | tf_op jit(solution)/shard_map/dot_general | solution.py:29
  522.4 105.4 %all_to_all.10 = bf16[64,64,1024]{2,1,0:T(8,128)(2,1)} all-to-all(bf16[64,64,1024]{2,1,0:T(8,128)(2,1)} %bitcast.8), channel_id=1, replica_groups=mesh['ang'=64,'pix'=2] {'ang'}, dimensions={0} | all-to-all | bytes 16777216 | tf_op jit(solution)/shard_map/all_to_all | solution.py:79
  627.7 14.5 %reshape.18 = bf16[64,64,2,512]{3,2,1,0:T(2,128)(2,1)} reshape(bf16[64,64,1024]{2,1,0:T(8,128)(2,1)} %all_to_all.10) | data formatting | bytes 16777216 | tf_op jit(solution)/shard_map/reshape | solution.py:80
  642.3 11.5 %copy.9 = bf16[2,64,64,512]{3,2,1,0:T(8,128)(2,1)} copy(bf16[2,64,64,512]{3,0,1,2:T(2,128)(2,1)} %bitcast.9) | data formatting | bytes 16777216
  (11 shorter events, 0.0 us)
Async XLA Ops:
  31.5 11.9 %copy-start.5 = (s32[4096]{0:T(1024)S(1)}, s32[4096]{0:T(1024)}, u32[]{:S(2)}) copy-start(s32[4096]{0:T(1024)} %param.5) | copy-start | bytes 49156
  31.5 11.9 %copy-start.7 = (s32[256]{0:T(256)S(1)}, s32[256]{0:T(256)}, u32[]{:S(2)}) copy-start(s32[256]{0:T(256)} %param.6) | copy-start | bytes 3076
  31.5 114.4 %all-to-all-start = ((bf16[64,64,1024]{2,1,0:T(8,128)(2,1)}), bf16[64,64,1024]{2,1,0:T(8,128)(2,1)}, u32[]{:S(2)}, u32[]{:S(2)}) async-start(bf16[64,64,1024]{2,1,0:T(8,128)(2,1)} %reshape.17), calls=%async_computation | async-start | bytes 16777216 | tf_op jit(solution)/shard_map/all_to_all | solution.py:54
  145.9 10.4 %copy-start = (f32[256,4096]{1,0:T(8,128)S(1)}, f32[256,4096]{1,0:T(8,128)}, u32[]{:S(2)}) copy-start(f32[256,4096]{1,0:T(8,128)} %get-tuple-element.9) | copy-start | bytes 12582916
  145.9 10.4 %copy-start.2 = (f32[256,4096]{1,0:T(8,128)S(1)}, f32[256,4096]{1,0:T(8,128)}, u32[]{:S(2)}) copy-start(f32[256,4096]{1,0:T(8,128)} %get-tuple-element.10) | copy-start | bytes 12582916
  163.2 1.4 copy-start.4
  482.5 14.4 %copy-start.6 = (f32[256]{0:T(256)}, f32[256]{0:T(256)S(1)}, u32[]{:S(2)}) copy-start(f32[256]{0:T(256)S(1)} %add_sqrt_fusion) | copy-start | bytes 3076
  484.2 12.7 %copy-start.1 = (f32[256,4096]{1,0:T(8,128)S(1)}, f32[256,4096]{1,0:T(8,128)}, u32[]{:S(2)}) copy-start(f32[256,4096]{1,0:T(8,128)} %get-tuple-element.9) | copy-start | bytes 12582916
  484.2 12.7 %copy-start.3 = (f32[256,4096]{1,0:T(8,128)S(1)}, f32[256,4096]{1,0:T(8,128)}, u32[]{:S(2)}) copy-start(f32[256,4096]{1,0:T(8,128)} %get-tuple-element.10) | copy-start | bytes 12582916

commit v2 on v1

v2 whole, which is shorter than its diff:
```python
import math

import jax
import jax.numpy as jnp
from jax import lax
from jax.sharding import Mesh
from jax.sharding import PartitionSpec as P

ANG = ("x", "yl", "z", "c")
ALL = ANG + ("pix",)


def phase_pair(product, modulus):
    radians = (product % modulus).astype(jnp.float32) * (2.0 * math.pi / modulus)
    return (jnp.cos(radians), jnp.sin(radians))


def split_parts(value):
    if value.dtype == jnp.bfloat16:
        return (value,)
    high = value.astype(jnp.bfloat16)
    low = (value - high.astype(jnp.float32)).astype(jnp.bfloat16)
    return (high, low)


def split_dot(left, right, dims):
    left_parts = split_parts(left)
    right_parts = split_parts(right)
    total = None
    for left_rank, left_piece in enumerate(left_parts):
        for right_rank, right_piece in enumerate(right_parts):
            if left_rank + right_rank <= 1:
                term = lax.dot_general(
                    left_piece, right_piece, (dims, ((), ())), preferred_element_type=jnp.float32
                )
                total = term if total is None else total + term
    return total


def global_sum(value):
    for axis in ("c", "pix", "yl", "x", "z"):
        size = lax.axis_size(axis)
        shift = 1
        while shift < size:
            perm = [(i, (i + shift) % size) for i in range(size)]
            value = value + lax.ppermute(value, axis, perm)
            shift *= 2
    return value


def body(grads, circle_pos, harmonics, support):
    ang_count = lax.axis_size(ANG)
    _, block, row_pix, col_count = grads.shape
    angle_count = circle_pos.shape[0]
    kept_count = harmonics.shape[0]
    row_start = lax.axis_index("pix") * row_pix + lax.axis_index(ANG)
    weight = lax.dynamic_slice_in_dim(support, row_start, 1, 0).astype(jnp.float32).reshape(-1)
    cell_count = float(row_pix * lax.axis_size("pix") * col_count)

    send = jnp.transpose(grads, (2, 0, 1, 3))
    moved = lax.all_to_all(send, ANG, split_axis=0, concat_axis=0, tiled=True)
    flat = moved.reshape(ang_count * 2 * block, col_count)

    phase_cos, phase_sin = phase_pair(harmonics[:, None] * circle_pos[None, :], angle_count)
    phase_cos = phase_cos.reshape(kept_count, ang_count, 1, block)
    phase_sin = phase_sin.reshape(kept_count, ang_count, 1, block)
    table = jnp.concatenate(
        (
            jnp.concatenate((phase_cos, phase_sin), 2),
            jnp.concatenate((-phase_sin, phase_cos), 2),
        ),
        0,
    ).reshape(2 * kept_count, ang_count * 2 * block)

    coef = split_dot(table, flat, ((1,), (0,))) * (1.0 / math.sqrt(angle_count))
    coef_re = coef[:kept_count]
    coef_im = coef[kept_count:]
    square_sums = jnp.sum(weight[None, :] * (coef_re * coef_re + coef_im * coef_im), axis=1)
    harmonic_rms = jnp.sqrt(global_sum(square_sums) / cell_count + 1e-06)
    factor = weight[None, :] / harmonic_rms[:, None]
    step = coef * jnp.concatenate((factor, factor), 0)

    synthesis = split_dot(table, step, ((0,), (0,)))
    update = (synthesis * (1.0 / math.sqrt(kept_count))).astype(jnp.bfloat16)
    update = update.reshape(ang_count, 2, block, col_count)
    back = lax.all_to_all(update, ANG, split_axis=0, concat_axis=0, tiled=True)
    back = jnp.transpose(back, (1, 2, 0, 3))
    return (back, harmonic_rms)


def solution(mesh):
    devices = mesh.devices.reshape(4, 2, 4, 2, mesh.shape["pix"])
    physical = Mesh(devices, ALL)
    placed = (P(None, ANG, "pix", None), P(), P(), P())
    return jax.shard_map(
        body,
        mesh=physical,
        in_specs=placed,
        out_specs=(P(None, ANG, "pix", None), P()),
        check_vma=False,
    )
```

time: 655 us -> 340 us (0.52)
  blocking collectives: 423 us -> 106 us
  local copies, waits for them, and re-layouts: 58.3 us -> 23.1 us
  other arithmetic: 20.8 us -> 34.1 us
  starting transfers between devices: 11.2 us -> 23.5 us
  waiting for transfers between devices: 84.6 us -> 94.9 us
    all_gather x1 -> x0, blocking collectives: 317 us -> none  [global_sum(): gathered = lax.all_gather(value, ('ang', 'pix'))]
    reshape x2 -> x0, local copies, waits for them, and re-layouts: 28.9 us -> none  [the longest x1 14.5 us: body(): back.reshape(row_pix, block, 2, col_count)]
    sin x0 -> x1, other arithmetic: none -> 19.7 us  [phase_pair(): return (jnp.cos(radians), jnp.sin(radians))]
    cos x1 -> x0, other arithmetic: 17.9 us -> none  [phase_pair(): return (jnp.cos(radians), jnp.sin(radians))]
    transpose x1 -> x0, local copies, waits for them, and re-layouts: 16.5 us -> none  [body(): jnp.transpose(grads, (2, 1, 0, 3)).reshape(row_pix, block, 2 * col_count)]
    ppermute x0 -> x7, starting transfers between devices: none -> 12.4 us  [global_sum(): value = value + lax.ppermute(value, axis, perm)]
    ppermute x0 -> x7, waiting for transfers between devices: none -> 12.1 us  [global_sum(): value = value + lax.ppermute(value, axis, perm)]
    unnamed x17 -> x12, local copies, waits for them, and re-layouts: 12.9 us -> 23.1 us
  transfers between devices with their start and end apart: 1 -> 8, of which waited for: 1 -> 6; matrix products, arithmetic and copies ran while one was open for 3% -> 10% of each run, Pallas kernels for 0% -> 0%
where the time goes in v2:
time: 340 us
  blocking collectives  106 us (31%)
  waiting for transfers between devices  94.9 us (28%)
  matrix products  57.7 us (17%)
  other arithmetic  34.1 us (10%)
  starting transfers between devices  23.5 us (7%)
  local copies, waits for them, and re-layouts  23.1 us (7%)
    all_to_all x1, blocking collectives, body(): back = lax.all_to_all(update, ANG, split_axis=0, concat_axis=0, tiled=True)  106 us
    all_to_all x1, waiting for transfers between devices, body(): moved = lax.all_to_all(send, ANG, split_axis=0, concat_axis=0, tiled=True)  82.8 us
    dot_general x5, matrix products, split_dot(): lax.dot_general(left_piece, right_piece, (dims, ((), ())), preferred_elem...  57.7 us
    unnamed x12, local copies, waits for them, and re-layouts  23.1 us
    sin x1, other arithmetic, phase_pair(): return (jnp.cos(radians), jnp.sin(radians))  19.7 us
    ppermute x7, starting transfers between devices, global_sum(): value = value + lax.ppermute(value, axis, perm)  12.4 us
    ppermute x7, waiting for transfers between devices, global_sum(): value = value + lax.ppermute(value, axis, perm)  12.1 us
    all_to_all x1, starting transfers between devices, body(): moved = lax.all_to_all(send, ANG, split_axis=0, concat_axis=0, tiled=True)  11.2 us
  transfers between devices with their start and end apart: 8, of which 6 were waited for; matrix products, arithmetic and copies ran while one was open for 10% of the time, Pallas kernels for 0%

profile of v2, /device:TPU:1, one launch (start us, length us, event | category | flops | bytes accessed | tf_op | source)
XLA Modules:
  0.0 339.8 jit_solution(9507998770758033457)
XLA Ops:
  0.6 11.5 %copy.13 = bf16[2,64,64,512]{3,1,0,2:T(8,128)(2,1)} copy(bf16[2,64,64,512]{3,2,1,0:T(8,128)(2,1)} %param.4) | data formatting | bytes 16777216 | tf_op args[0]
  12.1 11.2 %all-to-all-start = ((bf16[64,2,64,512]{3,2,1,0:T(8,128)(2,1)}), bf16[64,2,64,512]{3,2,1,0:T(8,128)(2,1)}, u32[]{:S(2)}, u32[]{:S(2)}) async-start(bf16[64,2,64,512]{3,2,1,0:T(8,128)(2,1)} %bitcast.30), calls=%async_computation | async-start | bytes 16777216 | tf_op jit(solution)/shard_map/all_to_all | solution.py:61
  23.4 0.7 dynamic-slice_convert_fusion
  24.2 19.7 %fusion.8 = (f32[256,64,1,64]{0,3,2,1:T(8,128)}, f32[256,64,1,64]{0,3,2,1:T(8,128)}, f32[256,64,1,64]{0,3,2,1:T(8,128)}) fusion(s32[64,64]{1,0:T(8,128)S(1)} %mul.93, s32[256]{0:T(256)S(1)} %copy-done.4), kind=kLoop, calls=%fused_computation.19 | loop fusion | flops 15728640 | bytes 12600320 | tf_op jit(solution)/shard_map/sin | solution.py:15
  43.9 82.8 %all-to-all-done = bf16[64,2,64,512]{3,2,1,0:T(8,128)(2,1)} async-done(((bf16[64,2,64,512]{3,2,1,0:T(8,128)(2,1)}), bf16[64,2,64,512]{3,2,1,0:T(8,128)(2,1)}, u32[]{:S(2)}, u32[]{:S(2)}) %all-to-all-start) | async-done | bytes 8388640 | tf_op jit(solution)/shard_map/all_to_all | solution.py:61
  126.7 10.7 %fusion.19 = f32[512,512]{0,1:T(8,128)S(1)} fusion(bf16[64,2,64,512]{3,2,1,0:T(8,128)(2,1)} %all-to-all-done, f32[256,64,1,64]{0,3,2,1:T(8,128)} %get-tuple-element.8, f32[256,64,1,64]{0,3,2,1:T(8,128)} %get-tuple-element.7, f32[256,64,1,64]{0,3,2,1:T(8,128)} %get-tuple-element.6), kind=kOutput, calls=%fused_computation.24 | convolution fusion | flops 4324327424 | bytes 22020096 | tf_op jit(solution)/shard_map/dot_general | solution.py:33
  137.4 12.8 %fusion.16 = f32[512,512]{0,1:T(8,128)S(1)} fusion(f32[512,512]{0,1:T(8,128)S(1)} %fusion.19, bf16[64,2,64,512]{3,2,1,0:T(8,128)(2,1)} %all-to-all-done, f32[256,64,1,64]{0,3,2,1:T(8,128)} %get-tuple-element.8, f32[256,64,1,64]{0,3,2,1:T(8,128)} %get-tuple-element.7, f32[256,64,1,64]{0,3,2,1:T(8,128)} %get-tuple-element.6), kind=kOutput, calls=%fused_computation.23 | convolution fusion | flops 4329046016 | bytes 23068672 | tf_op jit(solution)/shard_map/dot_general | solution.py:33
  150.2 0.1 fusion.25
  150.3 5.1 %collective-permute-start = (f32[256]{0:T(256)S(1)}, f32[256]{0:T(256)S(1)}, u32[]{:S(2)}, u32[]{:S(2)}) collective-permute-start(f32[256]{0:T(256)S(1)} %fusion.25), channel_id=1, source_target_pairs={{0,2},{2,0},{1,3},{3,1},{4,6},{6,4},{5,7},{7,5},{8,10},{10,8},{9,1... | collective-permute-start | bytes 3080 | tf_op jit(solution)/shard_map/ppermute | solution.py:46
  155.4 0.8 collective-permute-done
  156.3 2.6 collective-permute-start.1
  158.9 1.3 collective-permute-done.1
  160.2 2.4 collective-permute-done.2
  162.6 3.6 %collective-permute-done.3 = f32[256]{0:T(256)S(1)} collective-permute-done((f32[256]{0:T(256)S(1)}, f32[256]{0:T(256)S(1)}, u32[]{:S(2)}, u32[]{:S(2)}) %collective-permute-start.3) | collective-permute-done | bytes 1056 | tf_op jit(solution)/shard_map/ppermute | solution.py:46
  166.3 3.9 %collective-permute-done.4 = f32[256]{0:T(256)S(1)} collective-permute-done((f32[256]{0:T(256)S(1)}, f32[256]{0:T(256)S(1)}, u32[]{:S(2)}, u32[]{:S(2)}) %collective-permute-start.4) | collective-permute-done | bytes 1056 | tf_op jit(solution)/shard_map/ppermute | solution.py:46
  170.2 2.2 collective-permute-start.5
  172.4 7.7 %maximum_maximum_fusion = f32[512,64,2,64]{0,3,2,1:T(8,128)S(1)} fusion(f32[256,64,1,64]{0,3,2,1:T(8,128)} %get-tuple-element.8, f32[256,64,1,64]{0,3,2,1:T(8,128)} %get-tuple-element.7, f32[256,64,1,64]{0,3,2,1:T(8,128)} %get-tuple-element.6), kind=kLoop, calls=%fused_computation | loop fusion | flops 12582912 | bytes 29360128 | tf_op jit(solution)/shard_map/concatenate | solution.py:67
  180.1 2.4 collective-permute-start.6
  182.6 5.6 %fusion = (bf16[512,8192]{0,1:T(8,128)(2,1)}, bf16[512,8192]{0,1:T(8,128)(2,1)S(1)}) fusion(f32[512,64,2,64]{0,3,2,1:T(8,128)S(1)} %maximum_maximum_fusion), kind=kLoop, calls=%fused_computation.3 | loop fusion | flops 16777216 | bytes 33554432 | tf_op jit(solution)/shard_map/convert_element_type | solution.py:22
  188.4 9.4 %fusion.22 = f32[8192,512]{1,0:T(8,128)} fusion(bf16[512,8192]{0,1:T(8,128)(2,1)S(1)} %get-tuple-element.5, f32[512,512]{0,1:T(8,128)} %copy-done, f32[256,512]{0,1:T(8,128)S(1)} %broadcast_divide_fusion), kind=kOutput, calls=%fused_computation.29 | convolution fusion | flops 4296540160 | bytes 26738688 | tf_op jit(solution)/shard_map/dot_general | solution.py:33
  197.8 8.1 %fusion.29 = f32[8192,512]{1,0:T(8,128)} fusion(bf16[512,8192]{0,1:T(8,128)(2,1)S(1)} %get-tuple-element.5, f32[512,512]{0,1:T(8,128)S(1)} %copy-done.1, f32[256,512]{0,1:T(8,128)S(1)} %broadcast_divide_fusion), kind=kOutput, calls=%fused_computation.39 | convolution fusion | flops 4295753728 | bytes 26738688 | tf_op jit(solution)/shard_map/dot_general | solution.py:33
  205.9 16.7 %multiply_convert_fusion = bf16[8192,512]{1,0:T(8,128)(2,1)S(1)} fusion(f32[8192,512]{1,0:T(8,128)} %fusion.29, f32[8192,512]{1,0:T(8,128)} %fusion.22, bf16[512,8192]{0,1:T(8,128)(2,1)} %get-tuple-element.4, f32[512,512]{0,1:T(8,128)S(1)} %copy-done.1, f32[256,512]{0,1:T(8,128)S(1)} %broadcast_divide_fusion), kind=kOutput, calls=%fused_computation.4 | convolution fusion | flops 4312530944 | bytes 51904512 | tf_op jit(solution)/shard_map/dot_general | solution.py:33
  222.6 105.6 %all_to_all.10 = bf16[64,2,64,512]{3,2,1,0:T(8,128)(2,1)} all-to-all(bf16[64,2,64,512]{3,2,1,0:T(8,128)(2,1)S(1)} %bitcast.29), channel_id=1, replica_groups=mesh['x'=4,'yl'=2,'z'=4,'c'=2,'pix'=2] {'x','yl','z','c'}, dimensions={0} | all-to-all | bytes 16777216 | tf_op jit(solution)/shard_map/all_to_all | solution.py:86
  328.2 11.5 %copy.9 = bf16[2,64,64,512]{3,2,1,0:T(8,128)(2,1)} copy(bf16[2,64,64,512]{3,1,0,2:T(8,128)(2,1)} %bitcast.31) | data formatting | bytes 16777216
  (24 shorter events, 0.3 us)
Async XLA Ops:
  12.1 11.2 %copy-start.2 = (s32[4096]{0:T(1024)S(1)}, s32[4096]{0:T(1024)}, u32[]{:S(2)}) copy-start(s32[4096]{0:T(1024)} %param.5) | copy-start | bytes 49156
  12.1 12.0 %copy-start.4 = (s32[256]{0:T(256)S(1)}, s32[256]{0:T(256)}, u32[]{:S(2)}) copy-start(s32[256]{0:T(256)} %param.6) | copy-start | bytes 3076
  12.1 114.6 %all-to-all-start = ((bf16[64,2,64,512]{3,2,1,0:T(8,128)(2,1)}), bf16[64,2,64,512]{3,2,1,0:T(8,128)(2,1)}, u32[]{:S(2)}, u32[]{:S(2)}) async-start(bf16[64,2,64,512]{3,2,1,0:T(8,128)(2,1)} %bitcast.30), calls=%async_computation | async-start | bytes 16777216 | tf_op jit(solution)/shard_map/all_to_all | solution.py:61
  150.2 20.0 %copy-start = (f32[512,512]{0,1:T(8,128)}, f32[512,512]{0,1:T(8,128)S(1)}, u32[]{:S(2)}) copy-start(f32[512,512]{0,1:T(8,128)S(1)} %fusion.16) | copy-start | bytes 3145732
  150.3 5.9 %collective-permute-start = (f32[256]{0:T(256)S(1)}, f32[256]{0:T(256)S(1)}, u32[]{:S(2)}, u32[]{:S(2)}) collective-permute-start(f32[256]{0:T(256)S(1)} %fusion.25), channel_id=1, source_target_pairs={{0,2},{2,0},{1,3},{3,1},{4,6},{6,4},{5,7},{7,5},{8,10},{10,8},{9,1... | collective-permute-start | bytes 3080 | tf_op jit(solution)/shard_map/ppermute | solution.py:46
  156.3 3.9 %collective-permute-start.1 = (f32[256]{0:T(256)S(1)}, f32[256]{0:T(256)S(1)}, u32[]{:S(2)}, u32[]{:S(2)}) collective-permute-start(f32[256]{0:T(256)S(1)} %add.84), channel_id=1, source_target_pairs={{0,1},{1,0},{2,3},{3,2},{4,5},{5,4},{6,7},{7,6},{8,9},{9,8},{10,11... | collective-permute-start | bytes 3080 | tf_op jit(solution)/shard_map/ppermute | solution.py:46
  160.2 2.4 collective-permute-start.2
  162.6 3.6 %collective-permute-start.3 = (f32[256]{0:T(256)S(1)}, f32[256]{0:T(256)S(1)}, u32[]{:S(2)}, u32[]{:S(2)}) collective-permute-start(f32[256]{0:T(256)S(1)} %add.86), channel_id=1, source_target_pairs={{0,32},{32,64},{64,96},{96,0},{1,33},{33,65},{65,97},{97,1},{2,34}... | collective-permute-start | bytes 3080 | tf_op jit(solution)/shard_map/ppermute | solution.py:46
  166.2 3.9 %collective-permute-start.4 = (f32[256]{0:T(256)S(1)}, f32[256]{0:T(256)S(1)}, u32[]{:S(2)}, u32[]{:S(2)}) collective-permute-start(f32[256]{0:T(256)S(1)} %add.87), channel_id=1, source_target_pairs={{0,64},{32,96},{64,0},{96,32},{1,65},{33,97},{65,1},{97,33},{2,66}... | collective-permute-start | bytes 3080 | tf_op jit(solution)/shard_map/ppermute | solution.py:46
  170.2 9.9 %collective-permute-start.5 = (f32[256]{0:T(256)S(1)}, f32[256]{0:T(256)S(1)}, u32[]{:S(2)}, u32[]{:S(2)}) collective-permute-start(f32[256]{0:T(256)S(1)} %add.88), channel_id=1, source_target_pairs={{0,4},{4,8},{8,12},{12,0},{1,5},{5,9},{9,13},{13,1},{2,6},{6,10},{... | collective-permute-start | bytes 3080 | tf_op jit(solution)/shard_map/ppermute | solution.py:46
  180.1 8.0 %collective-permute-start.6 = (f32[256]{0:T(256)S(1)}, f32[256]{0:T(256)S(1)}, u32[]{:S(2)}, u32[]{:S(2)}) collective-permute-start(f32[256]{0:T(256)S(1)} %add.89), channel_id=1, source_target_pairs={{0,8},{4,12},{8,0},{12,4},{1,9},{5,13},{9,1},{13,5},{2,10},{6,14},... | collective-permute-start | bytes 3080 | tf_op jit(solution)/shard_map/ppermute | solution.py:46
  188.2 9.6 %copy-start.3 = (f32[256]{0:T(256)}, f32[256]{0:T(256)S(1)}, u32[]{:S(2)}) copy-start(f32[256]{0:T(256)S(1)} %add_sqrt_fusion) | copy-start | bytes 3076
  188.4 9.5 %copy-start.1 = (f32[512,512]{0,1:T(8,128)S(1)}, f32[512,512]{0,1:T(8,128)}, u32[]{:S(2)}) copy-start(f32[512,512]{0,1:T(8,128)} %copy-done) | copy-start | bytes 3145732

commit v3 on v2

--- a/solution.py
+++ b/solution.py
@@ -48,6 +48,37 @@
     return value
 
 
+def phase_table(circle_pos, harmonics, ang_count, block):
+    angle_count = circle_pos.shape[0]
+    residues = circle_pos.reshape(ang_count, block)[:, 0]
+    outer = phase_pair(harmonics[:, None] * residues[None, :], angle_count)
+    steps = jnp.arange(block, dtype=jnp.int32)
+    inner = phase_pair(harmonics[:, None] * steps[None, :], block)
+    return (outer, inner)
+
+
+def real_table(outer, inner, transposed):
+    outer_cos, outer_sin = outer
+    inner_cos, inner_sin = inner
+    if transposed:
+        outer_cos, outer_sin = outer_cos.T[:, None, None, :], outer_sin.T[:, None, None, :]
+        inner_cos, inner_sin = inner_cos.T[None, None, :, :], inner_sin.T[None, None, :, :]
+        axis_ri, axis_k = 1, 3
+    else:
+        outer_cos, outer_sin = outer_cos[:, :, None, None], outer_sin[:, :, None, None]
+        inner_cos, inner_sin = inner_cos[:, None, None, :], inner_sin[:, None, None, :]
+        axis_ri, axis_k = 2, 0
+    phase_cos = outer_cos * inner_cos - outer_sin * inner_sin
+    phase_sin = outer_sin * inner_cos + outer_cos * inner_sin
+    return jnp.concatenate(
+        (
+            jnp.concatenate((phase_cos, phase_sin), axis_ri),
+            jnp.concatenate((-phase_sin, phase_cos), axis_ri),
+        ),
+        axis_k,
+    )
+
+
 def body(grads, circle_pos, harmonics, support):
     ang_count = lax.axis_size(ANG)
     _, block, row_pix, col_count = grads.shape
@@ -56,23 +87,22 @@
     row_start = lax.axis_index("pix") * row_pix + lax.axis_index(ANG)
     weight = lax.dynamic_slice_in_dim(support, row_start, 1, 0).astype(jnp.float32).reshape(-1)
     cell_count = float(row_pix * lax.axis_size("pix") * col_count)
+    depth = ang_count * 2 * block
 
     send = jnp.transpose(grads, (2, 0, 1, 3))
     moved = lax.all_to_all(send, ANG, split_axis=0, concat_axis=0, tiled=True)
-    flat = moved.reshape(ang_count * 2 * block, col_count)
+    flat = moved.reshape(depth, col_count)
 
-    phase_cos, phase_sin = phase_pair(harmonics[:, None] * circle_pos[None, :], angle_count)
-    phase_cos = phase_cos.reshape(kept_count, ang_count, 1, block)
-    phase_sin = phase_sin.reshape(kept_count, ang_count, 1, block)
-    table = jnp.concatenate(
-        (
-            jnp.concatenate((phase_cos, phase_sin), 2),
-            jnp.concatenate((-phase_sin, phase_cos), 2),
-        ),
-        0,
-    ).reshape(2 * kept_count, ang_count * 2 * block)
+    outer, inner = phase_table(circle_pos, harmonics, ang_count, block)
+    forward_parts = split_parts(real_table(outer, inner, False).reshape(2 * kept_count, depth))
+    backward_parts = split_parts(real_table(outer, inner, True).reshape(depth, 2 * kept_count))
+    forward_parts, backward_parts = lax.optimization_barrier((forward_parts, backward_parts))
 
-    coef = split_dot(table, flat, ((1,), (0,))) * (1.0 / math.sqrt(angle_count))
+    coef = None
+    for piece in forward_parts:
+        term = jnp.dot(piece, flat, preferred_element_type=jnp.float32)
+        coef = term if coef is None else coef + term
+    coef = coef * (1.0 / math.sqrt(angle_count))
     coef_re = coef[:kept_count]
     coef_im = coef[kept_count:]
     square_sums = jnp.sum(weight[None, :] * (coef_re * coef_re + coef_im * coef_im), axis=1)
@@ -80,7 +110,13 @@
     factor = weight[None, :] / harmonic_rms[:, None]
     step = coef * jnp.concatenate((factor, factor), 0)
 
-    synthesis = split_dot(table, step, ((0,), (0,)))
+    step_parts = split_parts(step)
+    synthesis = None
+    for left_rank, left_piece in enumerate(backward_parts):
+        for right_rank, right_piece in enumerate(step_parts):
+            if left_rank + right_rank <= 1:
+                term = jnp.dot(left_piece, right_piece, preferred_element_type=jnp.float32)
+                synthesis = term if synthesis is None else synthesis + term
     update = (synthesis * (1.0 / math.sqrt(kept_count))).astype(jnp.bfloat16)
     update = update.reshape(ang_count, 2, block, col_count)
     back = lax.all_to_all(update, ANG, split_axis=0, concat_axis=0, tiled=True)

time: 340 us -> 327 us (0.962)
  waiting for transfers between devices: 94.9 us -> 86.5 us
  matrix products: 57.7 us -> 52.1 us
    sin x1 -> x0, other arithmetic: 19.7 us -> none  [phase_pair(): return (jnp.cos(radians), jnp.sin(radians))]
    all_to_all x1, waiting for transfers between devices: 82.8 us -> 69.1 us  [body(): moved = lax.all_to_all(send, ANG, split_axis=0, concat_axis=0, tiled=True)]
    convert_element_type x1 -> x2, other arithmetic: 5.64 us -> 14.9 us  [split_parts(): low = (value - high.astype(jnp.float32)).astype(jnp.bfloat16)]
    add x0 -> x2, other arithmetic: none -> 7.6 us  [real_table(): phase_sin = outer_sin * inner_cos + outer_cos * inner_sin]
    dot_general x5, matrix products: 57.7 us -> 52.1 us  [the longest x3 33 us: body(): term = jnp.dot(left_piece, right_piece, preferred_element_type=jnp.float32)]
    ppermute x7, waiting for transfers between devices: 12.1 us -> 17.5 us  [global_sum(): value = value + lax.ppermute(value, axis, perm)]
    concatenate x1 -> x2, other arithmetic: 7.72 us -> 9.77 us  [real_table(): jnp.concatenate((jnp.concatenate((phase_cos, phase_sin), axis_ri), jnp.co...]
  transfers between devices with their start and end apart: 8 -> 8, of which waited for: 6 -> 8; matrix products, arithmetic and copies ran while one was open for 10% -> 10% of each run, Pallas kernels for 0% -> 0%
where the time goes in v3:
time: 327 us
  blocking collectives  108 us (33%)
  waiting for transfers between devices  86.5 us (26%)
  matrix products  52.1 us (16%)
  other arithmetic  34.4 us (11%)
  local copies, waits for them, and re-layouts  23.1 us (7%)
  starting transfers between devices  21.8 us (7%)
    all_to_all x1, blocking collectives, body(): back = lax.all_to_all(update, ANG, split_axis=0, concat_axis=0, tiled=True)  108 us
    all_to_all x1, waiting for transfers between devices, body(): moved = lax.all_to_all(send, ANG, split_axis=0, concat_axis=0, tiled=True)  69.1 us
    dot_general x3, matrix products, body(): term = jnp.dot(left_piece, right_piece, preferred_element_type=jnp.float32)  33 us
    unnamed x12, local copies, waits for them, and re-layouts  22.9 us
    dot_general x2, matrix products, body(): term = jnp.dot(piece, flat, preferred_element_type=jnp.float32)  19.2 us
    ppermute x7, waiting for transfers between devices, global_sum(): value = value + lax.ppermute(value, axis, perm)  17.5 us
    convert_element_type x2, other arithmetic, split_parts(): low = (value - high.astype(jnp.float32)).astype(jnp.bfloat16)  14.9 us
    all_to_all x1, starting transfers between devices, body(): moved = lax.all_to_all(send, ANG, split_axis=0, concat_axis=0, tiled=True)  11.2 us
  transfers between devices with their start and end apart: 8, of which 8 were waited for; matrix products, arithmetic and copies ran while one was open for 10% of the time, Pallas kernels for 0%

profile of v3, /device:TPU:1, one launch (start us, length us, event | category | flops | bytes accessed | tf_op | source)
XLA Modules:
  0.0 326.6 jit_solution(4020324372293136915)
XLA Ops:
  0.6 11.4 %copy.14 = bf16[2,64,64,512]{3,1,0,2:T(8,128)(2,1)} copy(bf16[2,64,64,512]{3,2,1,0:T(8,128)(2,1)} %param.4) | data formatting | bytes 16777216 | tf_op args[0]
  12.0 11.2 %all-to-all-start = ((bf16[64,2,64,512]{3,2,1,0:T(8,128)(2,1)}), bf16[64,2,64,512]{3,2,1,0:T(8,128)(2,1)}, u32[]{:S(2)}, u32[]{:S(2)}) async-start(bf16[64,2,64,512]{3,2,1,0:T(8,128)(2,1)} %bitcast.29), calls=%async_computation | async-start | bytes 16777216 | tf_op jit(solution)/shard_map/all_to_all | solution.py:93
  23.9 1.8 multiply_add_fusion
  26.3 5.8 %multiply_add_fusion.1 = (f32[256,64,1,64]{0,3,2,1:T(8,128)}, f32[256,64,1,64]{0,3,2,1:T(8,128)}, f32[256,64,1,64]{0,3,2,1:T(8,128)}) fusion(f32[256,64]{0,1:T(8,128)S(1)} %get-tuple-element.28, f32[256,64]{0,1:T(8,128)S(1)} %get-tuple-element.25, f32[256,64]{0,1:T(8,128)S(1)} %get-tuple-element.29, f32[256,64]{0,1:T(8,128)S(1)} %get-tuple-element.24), kind=kLoop, calls=%fused_computation.12 | loop fusion | flops 7340032 | bytes 12845056 | tf_op jit(solution)/shard_map/add | solution.py:72
  32.1 2.2 maximum_maximum_fusion.1
  34.3 7.6 %maximum_maximum_fusion = f32[512,64,2,64]{0,3,2,1:T(8,128)S(1)} fusion(f32[256,64,1,64]{0,3,2,1:T(8,128)} %get-tuple-element.21, f32[256,64,1,64]{0,3,2,1:T(8,128)} %get-tuple-element.20, f32[256,64,1,64]{0,3,2,1:T(8,128)} %get-tuple-element.19), kind=kLoop, calls=%fused_computation | loop fusion | flops 12582912 | bytes 29360128 | tf_op jit(solution)/shard_map/concatenate | solution.py:73
  41.9 7.4 %fusion = (bf16[8192,512]{1,0:T(8,128)(2,1)}, bf16[8192,512]{1,0:T(8,128)(2,1)}) fusion(f32[64,2,64,512]{3,2,1,0:T(8,128)S(1)} %maximum_maximum_fusion.1), kind=kLoop, calls=%fused_computation.4 | loop fusion | flops 16777216 | bytes 33554432 | tf_op jit(solution)/shard_map/convert_element_type | solution.py:22
  49.3 7.4 %fusion.1 = (bf16[512,8192]{0,1:T(8,128)(2,1)}, bf16[512,8192]{0,1:T(8,128)(2,1)}) fusion(f32[512,64,2,64]{0,3,2,1:T(8,128)S(1)} %maximum_maximum_fusion), kind=kLoop, calls=%fused_computation.7 | loop fusion | flops 16777216 | bytes 33554432 | tf_op jit(solution)/shard_map/convert_element_type | solution.py:22
  57.5 69.1 %all-to-all-done = bf16[64,2,64,512]{3,2,1,0:T(8,128)(2,1)} async-done(((bf16[64,2,64,512]{3,2,1,0:T(8,128)(2,1)}), bf16[64,2,64,512]{3,2,1,0:T(8,128)(2,1)}, u32[]{:S(2)}, u32[]{:S(2)}) %all-to-all-start) | async-done | bytes 8388640 | tf_op jit(solution)/shard_map/all_to_all | solution.py:93
  126.6 9.6 %fusion.41 = f32[512,512]{0,1:T(8,128)S(1)} fusion(bf16[512,8192]{0,1:T(8,128)(2,1)} %get-tuple-element.7, bf16[8192,512]{1,0:T(8,128)(2,1)} %bitcast.3), kind=kOutput, calls=%fused_computation.75 | convolution fusion | flops 4294967296 | bytes 17825792 | tf_op jit(solution)/shard_map/dot_general | solution.py:103
  136.1 9.6 %fusion.2 = f32[512,512]{0,1:T(8,128)S(1)} fusion(f32[512,512]{0,1:T(8,128)S(1)} %fusion.41, bf16[512,8192]{0,1:T(8,128)(2,1)} %get-tuple-element.8, bf16[8192,512]{1,0:T(8,128)(2,1)} %bitcast.3), kind=kOutput, calls=%fused_computation.15 | convolution fusion | flops 4295491584 | bytes 18874368 | tf_op jit(solution)/shard_map/dot_general | solution.py:103
  145.9 5.1 %collective-permute-start = (f32[256]{0:T(256)S(1)}, f32[256]{0:T(256)S(1)}, u32[]{:S(2)}, u32[]{:S(2)}) collective-permute-start(f32[256]{0:T(256)S(1)} %fusion.9), channel_id=1, source_target_pairs={{0,2},{2,0},{1,3},{3,1},{4,6},{6,4},{5,7},{7,5},{8,10},{10,8},{9,1... | collective-permute-start | bytes 3080 | tf_op jit(solution)/shard_map/ppermute | solution.py:46
  151.8 2.6 collective-permute-start.1
  155.8 2.4 collective-permute-done.2
  158.2 3.6 %collective-permute-done.3 = f32[256]{0:T(256)S(1)} collective-permute-done((f32[256]{0:T(256)S(1)}, f32[256]{0:T(256)S(1)}, u32[]{:S(2)}, u32[]{:S(2)}) %collective-permute-start.3) | collective-permute-done | bytes 1056 | tf_op jit(solution)/shard_map/ppermute | solution.py:46
  161.8 3.9 %collective-permute-done.4 = f32[256]{0:T(256)S(1)} collective-permute-done((f32[256]{0:T(256)S(1)}, f32[256]{0:T(256)S(1)}, u32[]{:S(2)}, u32[]{:S(2)}) %collective-permute-start.4) | collective-permute-done | bytes 1056 | tf_op jit(solution)/shard_map/ppermute | solution.py:46
  165.7 2.2 collective-permute-start.5
  168.0 2.2 collective-permute-done.5
  170.8 3.2 collective-permute-done.6
  174.2 8.1 %fusion.6 = f32[8192,512]{1,0:T(8,128)} fusion(bf16[8192,512]{1,0:T(8,128)(2,1)S(1)} %bitcast.27, f32[512,512]{0,1:T(8,128)S(1)} %fusion.2, f32[256,512]{0,1:T(8,128)S(1)} %broadcast_divide_fusion), kind=kOutput, calls=%fused_computation.21 | convolution fusion | flops 4296540160 | bytes 26738688 | tf_op jit(solution)/shard_map/dot_general | solution.py:118
  182.4 8.1 %fusion.39 = f32[8192,512]{1,0:T(8,128)} fusion(bf16[8192,512]{1,0:T(8,128)(2,1)S(1)} %bitcast.27, f32[512,512]{0,1:T(8,128)S(1)} %fusion.2, f32[256,512]{0,1:T(8,128)S(1)} %broadcast_divide_fusion), kind=kOutput, calls=%fused_computation.74 | convolution fusion | flops 4295753728 | bytes 26738688 | tf_op jit(solution)/shard_map/dot_general | solution.py:118
  190.5 16.7 %multiply_convert_fusion = bf16[8192,512]{1,0:T(8,128)(2,1)S(1)} fusion(f32[8192,512]{1,0:T(8,128)} %fusion.39, f32[8192,512]{1,0:T(8,128)} %fusion.6, bf16[8192,512]{1,0:T(8,128)(2,1)} %get-tuple-element.9, f32[512,512]{0,1:T(8,128)S(1)} %fusion.2, f32[256,512]{0,1:T(8,128)S(1)} %broadcast_divide_fusion), kind=kOutput, calls=%fused_computation.8 | convolution fusion | flops 4312530944 | bytes 51904512 | tf_op jit(solution)/shard_map/dot_general | solution.py:118
  207.2 107.9 %all_to_all.10 = bf16[64,2,64,512]{3,2,1,0:T(8,128)(2,1)} all-to-all(bf16[64,2,64,512]{3,2,1,0:T(8,128)(2,1)S(1)} %bitcast.28), channel_id=1, replica_groups=mesh['x'=4,'yl'=2,'z'=4,'c'=2,'pix'=2] {'x','yl','z','c'}, dimensions={0} | all-to-all | bytes 16777216 | tf_op jit(solution)/shard_map/all_to_all | solution.py:122
  315.1 11.5 %copy.12 = bf16[2,64,64,512]{3,2,1,0:T(8,128)(2,1)} copy(bf16[2,64,64,512]{3,1,0,2:T(8,128)(2,1)} %bitcast.30) | data formatting | bytes 16777216
  (31 shorter events, 5.2 us)
Async XLA Ops:
  12.0 11.2 %copy-start = (s32[4096]{0:T(1024)S(1)}, s32[4096]{0:T(1024)}, u32[]{:S(2)}) copy-start(s32[4096]{0:T(1024)} %param.5) | copy-start | bytes 49156
  12.0 11.4 %copy-start.1 = (s32[256]{0:T(256)S(1)}, s32[256]{0:T(256)}, u32[]{:S(2)}) copy-start(s32[256]{0:T(256)} %param.6) | copy-start | bytes 3076
  12.0 114.6 %all-to-all-start = ((bf16[64,2,64,512]{3,2,1,0:T(8,128)(2,1)}), bf16[64,2,64,512]{3,2,1,0:T(8,128)(2,1)}, u32[]{:S(2)}, u32[]{:S(2)}) async-start(bf16[64,2,64,512]{3,2,1,0:T(8,128)(2,1)} %bitcast.29), calls=%async_computation | async-start | bytes 16777216 | tf_op jit(solution)/shard_map/all_to_all | solution.py:93
  126.5 47.7 %slice-start = ((s8[8388608]{0:T(1024)(128)(4,1)}), s8[4194304]{0:T(1024)(128)(4,1)S(1)}, s32[]{:S(2)}) async-start(s8[8388608]{0:T(1024)(128)(4,1)} %bitcast.26), calls=%async_computation.2 | async-start | bytes 8388608
  136.1 38.1 %slice-start.1 = ((s8[8388608]{0:T(1024)(128)(4,1)}), s8[4194304]{0:T(1024)(128)(4,1)S(1)}, s32[]{:S(2)}) async-start(s8[8388608]{0:T(1024)(128)(4,1)} %bitcast.26), calls=%async_computation.3 | async-start | bytes 8388608
  145.9 5.9 %collective-permute-start = (f32[256]{0:T(256)S(1)}, f32[256]{0:T(256)S(1)}, u32[]{:S(2)}, u32[]{:S(2)}) collective-permute-start(f32[256]{0:T(256)S(1)} %fusion.9), channel_id=1, source_target_pairs={{0,2},{2,0},{1,3},{3,1},{4,6},{6,4},{5,7},{7,5},{8,10},{10,8},{9,1... | collective-permute-start | bytes 3080 | tf_op jit(solution)/shard_map/ppermute | solution.py:46
  151.8 3.9 %collective-permute-start.1 = (f32[256]{0:T(256)S(1)}, f32[256]{0:T(256)S(1)}, u32[]{:S(2)}, u32[]{:S(2)}) collective-permute-start(f32[256]{0:T(256)S(1)} %add.143), channel_id=1, source_target_pairs={{0,1},{1,0},{2,3},{3,2},{4,5},{5,4},{6,7},{7,6},{8,9},{9,8},{10,11... | collective-permute-start | bytes 3080 | tf_op jit(solution)/shard_map/ppermute | solution.py:46
  155.8 2.4 collective-permute-start.2
  158.2 3.6 %collective-permute-start.3 = (f32[256]{0:T(256)S(1)}, f32[256]{0:T(256)S(1)}, u32[]{:S(2)}, u32[]{:S(2)}) collective-permute-start(f32[256]{0:T(256)S(1)} %add.145), channel_id=1, source_target_pairs={{0,32},{32,64},{64,96},{96,0},{1,33},{33,65},{65,97},{97,1},{2,34}... | collective-permute-start | bytes 3080 | tf_op jit(solution)/shard_map/ppermute | solution.py:46
  161.8 3.9 %collective-permute-start.4 = (f32[256]{0:T(256)S(1)}, f32[256]{0:T(256)S(1)}, u32[]{:S(2)}, u32[]{:S(2)}) collective-permute-start(f32[256]{0:T(256)S(1)} %add.146), channel_id=1, source_target_pairs={{0,64},{32,96},{64,0},{96,32},{1,65},{33,97},{65,1},{97,33},{2,66}... | collective-permute-start | bytes 3080 | tf_op jit(solution)/shard_map/ppermute | solution.py:46
  165.7 4.4 %collective-permute-start.5 = (f32[256]{0:T(256)S(1)}, f32[256]{0:T(256)S(1)}, u32[]{:S(2)}, u32[]{:S(2)}) collective-permute-start(f32[256]{0:T(256)S(1)} %add.147), channel_id=1, source_target_pairs={{0,4},{4,8},{8,12},{12,0},{1,5},{5,9},{9,13},{13,1},{2,6},{6,10},{... | collective-permute-start | bytes 3080 | tf_op jit(solution)/shard_map/ppermute | solution.py:46
  170.1 3.9 %collective-permute-start.6 = (f32[256]{0:T(256)S(1)}, f32[256]{0:T(256)S(1)}, u32[]{:S(2)}, u32[]{:S(2)}) collective-permute-start(f32[256]{0:T(256)S(1)} %add.148), channel_id=1, source_target_pairs={{0,8},{4,12},{8,0},{12,4},{1,9},{5,13},{9,1},{13,5},{2,10},{6,14},... | collective-permute-start | bytes 3080 | tf_op jit(solution)/shard_map/ppermute | solution.py:46
  174.1 8.3 %copy-start.2 = (f32[256]{0:T(256)}, f32[256]{0:T(256)S(1)}, u32[]{:S(2)}) copy-start(f32[256]{0:T(256)S(1)} %add_sqrt_fusion) | copy-start | bytes 3076

commit v4 on v3

--- a/solution.py
+++ b/solution.py
@@ -94,15 +94,14 @@
     flat = moved.reshape(depth, col_count)
 
     outer, inner = phase_table(circle_pos, harmonics, ang_count, block)
-    forward_parts = split_parts(real_table(outer, inner, False).reshape(2 * kept_count, depth))
-    backward_parts = split_parts(real_table(outer, inner, True).reshape(depth, 2 * kept_count))
-    forward_parts, backward_parts = lax.optimization_barrier((forward_parts, backward_parts))
+    forward_high, forward_low = split_parts(real_table(outer, inner, False).reshape(2 * kept_count, depth))
+    backward_high, backward_low = split_parts(real_table(outer, inner, True).reshape(depth, 2 * kept_count))
+    forward_table = jnp.concatenate((forward_high, forward_low), 0)
+    backward_table = jnp.concatenate((backward_high, backward_low, backward_high), 1)
+    forward_table, backward_table = lax.optimization_barrier((forward_table, backward_table))
 
-    coef = None
-    for piece in forward_parts:
-        term = jnp.dot(piece, flat, preferred_element_type=jnp.float32)
-        coef = term if coef is None else coef + term
-    coef = coef * (1.0 / math.sqrt(angle_count))
+    stacked = jnp.dot(forward_table, flat, preferred_element_type=jnp.float32)
+    coef = (stacked[: 2 * kept_count] + stacked[2 * kept_count:]) * (1.0 / math.sqrt(angle_count))
     coef_re = coef[:kept_count]
     coef_im = coef[kept_count:]
     square_sums = jnp.sum(weight[None, :] * (coef_re * coef_re + coef_im * coef_im), axis=1)
@@ -110,13 +109,9 @@
     factor = weight[None, :] / harmonic_rms[:, None]
     step = coef * jnp.concatenate((factor, factor), 0)
 
-    step_parts = split_parts(step)
-    synthesis = None
-    for left_rank, left_piece in enumerate(backward_parts):
-        for right_rank, right_piece in enumerate(step_parts):
-            if left_rank + right_rank <= 1:
-                term = jnp.dot(left_piece, right_piece, preferred_element_type=jnp.float32)
-                synthesis = term if synthesis is None else synthesis + term
+    step_high, step_low = split_parts(step)
+    step_stack = jnp.concatenate((step_high, step_high, step_low), 0)
+    synthesis = jnp.dot(backward_table, step_stack, preferred_element_type=jnp.float32)
     update = (synthesis * (1.0 / math.sqrt(kept_count))).astype(jnp.bfloat16)
     update = update.reshape(ang_count, 2, block, col_count)
     back = lax.all_to_all(update, ANG, split_axis=0, concat_axis=0, tiled=True)

time: 327 us -> 310 us (0.948)
  other arithmetic: 34.4 us -> 58.7 us
  waiting for transfers between devices: 86.5 us -> 62.7 us
  matrix products: 52.1 us -> 34.1 us
    concatenate x0 -> x2, other arithmetic: none -> 27.6 us  [the longest x1 20.5 us: body(): jnp.concatenate((backward_high, backward_low, backward_high), 1)]
    all_to_all x1, waiting for transfers between devices: 69.1 us -> 45.3 us  [body(): moved = lax.all_to_all(send, ANG, split_axis=0, concat_axis=0, tiled=True)]
    dot_general x5 -> x2, matrix products: 52.1 us -> 34.1 us  [the longest x1 20 us: body(): jnp.dot(backward_table, step_stack, preferred_element_type=jnp.float32)]
    convert_element_type x2, other arithmetic: 14.9 us -> 11.1 us  [split_parts(): low = (value - high.astype(jnp.float32)).astype(jnp.bfloat16)]
    unnamed x12 -> x8, local copies, waits for them, and re-layouts: 22.9 us -> 22.9 us
  transfers between devices with their start and end apart: 8 -> 8, of which waited for: 8 -> 8; matrix products, arithmetic and copies ran while one was open for 10% -> 19% of each run, Pallas kernels for 0% -> 0%
where the time goes in v4:
time: 310 us; the launch traced here: 309 us
  blocking collectives  108 us (35%)
  waiting for transfers between devices  62.7 us (20%)
  other arithmetic  58.7 us (19%)
  matrix products  34.1 us (11%)
  local copies, waits for them, and re-layouts  23 us (7%)
  starting transfers between devices  21.8 us (7%)
    all_to_all x1, blocking collectives, body(): back = lax.all_to_all(update, ANG, split_axis=0, concat_axis=0, tiled=True)  108 us
    all_to_all x1, waiting for transfers between devices, body(): moved = lax.all_to_all(send, ANG, split_axis=0, concat_axis=0, tiled=True)  45.3 us
    unnamed x8, local copies, waits for them, and re-layouts  22.9 us
    concatenate x1, other arithmetic, body(): jnp.concatenate((backward_high, backward_low, backward_high), 1)  20.5 us
    dot_general x1, matrix products, body(): jnp.dot(backward_table, step_stack, preferred_element_type=jnp.float32)  20 us
    ppermute x7, waiting for transfers between devices, global_sum(): value = value + lax.ppermute(value, axis, perm)  17.5 us
    dot_general x1, matrix products, body(): stacked = jnp.dot(forward_table, flat, preferred_element_type=jnp.float32)  14.1 us
    all_to_all x1, starting transfers between devices, body(): moved = lax.all_to_all(send, ANG, split_axis=0, concat_axis=0, tiled=True)  11.2 us
  transfers between devices with their start and end apart: 8, of which 8 were waited for; matrix products, arithmetic and copies ran while one was open for 19% of the time, Pallas kernels for 0%

profile of v4, /device:TPU:1, one launch (start us, length us, event | category | flops | bytes accessed | tf_op | source)
XLA Modules:
  0.0 309.3 jit_solution(11238450738544495234)
XLA Ops:
  0.6 11.3 %copy.14 = bf16[2,64,64,512]{3,1,0,2:T(8,128)(2,1)} copy(bf16[2,64,64,512]{3,2,1,0:T(8,128)(2,1)} %param.4) | data formatting | bytes 16777216 | tf_op args[0]
  12.0 11.2 %all-to-all-start = ((bf16[64,2,64,512]{3,2,1,0:T(8,128)(2,1)}), bf16[64,2,64,512]{3,2,1,0:T(8,128)(2,1)}, u32[]{:S(2)}, u32[]{:S(2)}) async-start(bf16[64,2,64,512]{3,2,1,0:T(8,128)(2,1)} %bitcast.22), calls=%async_computation | async-start | bytes 16777216 | tf_op jit(solution)/shard_map/all_to_all | solution.py:93
  24.5 1.7 multiply_add_fusion.1
  26.2 2.2 maximum_maximum_fusion
  28.4 3.7 %fusion.1 = (bf16[512,8192]{0,1:T(8,128)(2,1)S(1)}, bf16[512,8192]{0,1:T(8,128)(2,1)S(1)}) fusion(f32[512,64,2,64]{0,3,2,1:T(8,128)S(1)} %maximum_maximum_fusion), kind=kLoop, calls=%fused_computation.9 | loop fusion | flops 16777216 | bytes 33554432 | tf_op jit(solution)/shard_map/convert_element_type | solution.py:22
  32.2 5.8 %multiply_add_fusion = (f32[64,1,64,256]{3,2,1,0:T(8,128)}, f32[64,1,64,256]{3,2,1,0:T(8,128)}, f32[64,1,64,256]{3,2,1,0:T(8,128)}) fusion(f32[64,256]{1,0:T(8,128)S(1)} %get-tuple-element.24, f32[64,256]{1,0:T(8,128)S(1)} %get-tuple-element.21, f32[64,256]{1,0:T(8,128)S(1)} %get-tuple-element.25, f32[64,256]{1,0:T(8,128)S(1)} %get-tuple-element.20), kind=kLoop, calls=%fused_computation.12 | loop fusion | flops 7340032 | bytes 12845056 | tf_op jit(solution)/shard_map/add | solution.py:72
  38.0 7.5 %maximum_maximum_fusion.1 = f32[64,2,64,512]{3,2,1,0:T(8,128)S(1)} fusion(f32[64,1,64,256]{3,2,1,0:T(8,128)} %get-tuple-element.16, f32[64,1,64,256]{3,2,1,0:T(8,128)} %get-tuple-element.15, f32[64,1,64,256]{3,2,1,0:T(8,128)} %get-tuple-element.14), kind=kLoop, calls=%fused_computation.3 | loop fusion | flops 12582912 | bytes 29360128 | tf_op jit(solution)/shard_map/concatenate | solution.py:73
  45.5 7.2 %pad_maximum_fusion.1 = bf16[1024,8192]{0,1:T(8,128)(2,1)} fusion(bf16[512,8192]{0,1:T(8,128)(2,1)S(1)} %get-tuple-element.10, bf16[512,8192]{0,1:T(8,128)(2,1)S(1)} %get-tuple-element.11), kind=kLoop, calls=%fused_computation.2 | loop fusion | flops 33554432 | bytes 33554432 | tf_op jit(solution)/shard_map/concatenate | solution.py:99
  52.7 7.4 %fusion = (bf16[8192,512]{1,0:T(8,128)(2,1)}, bf16[8192,512]{1,0:T(8,128)(2,1)}) fusion(f32[64,2,64,512]{3,2,1,0:T(8,128)S(1)} %maximum_maximum_fusion.1), kind=kLoop, calls=%fused_computation.6 | loop fusion | flops 16777216 | bytes 33554432 | tf_op jit(solution)/shard_map/convert_element_type | solution.py:22
  60.1 20.5 %pad_maximum_fusion = bf16[8192,1536]{1,0:T(8,128)(2,1)} fusion(bf16[8192,512]{1,0:T(8,128)(2,1)} %get-tuple-element.9, bf16[8192,512]{1,0:T(8,128)(2,1)} %get-tuple-element.8), kind=kLoop, calls=%fused_computation | loop fusion | flops 75497472 | bytes 41943040 | tf_op jit(solution)/shard_map/concatenate | solution.py:100
  81.3 45.3 %all-to-all-done = bf16[64,2,64,512]{3,2,1,0:T(8,128)(2,1)} async-done(((bf16[64,2,64,512]{3,2,1,0:T(8,128)(2,1)}), bf16[64,2,64,512]{3,2,1,0:T(8,128)(2,1)}, u32[]{:S(2)}, u32[]{:S(2)}) %all-to-all-start) | async-done | bytes 8388640 | tf_op jit(solution)/shard_map/all_to_all | solution.py:93
  126.5 14.1 %fusion.41 = f32[1024,512]{1,0:T(8,128)S(1)} fusion(bf16[1024,8192]{0,1:T(8,128)(2,1)} %pad_maximum_fusion.1, bf16[8192,512]{1,0:T(8,128)(2,1)} %bitcast.3), kind=kOutput, calls=%fused_computation.80 | convolution fusion | flops 8589934592 | bytes 27262976 | tf_op jit(solution)/shard_map/dot_general | solution.py:103
  141.0 5.1 %collective-permute-start = (f32[256]{0:T(256)S(1)}, f32[256]{0:T(256)S(1)}, u32[]{:S(2)}, u32[]{:S(2)}) collective-permute-start(f32[256]{0:T(256)S(1)} %fusion.13), channel_id=1, source_target_pairs={{0,2},{2,0},{1,3},{3,1},{4,6},{6,4},{5,7},{7,5},{8,10},{10,8},{9,1... | collective-permute-start | bytes 3080 | tf_op jit(solution)/shard_map/ppermute | solution.py:46
  146.9 2.6 collective-permute-start.1
  149.6 1.3 collective-permute-done.1
  150.9 2.4 collective-permute-done.2
  153.3 3.6 %collective-permute-done.3 = f32[256]{0:T(256)S(1)} collective-permute-done((f32[256]{0:T(256)S(1)}, f32[256]{0:T(256)S(1)}, u32[]{:S(2)}, u32[]{:S(2)}) %collective-permute-start.3) | collective-permute-done | bytes 1056 | tf_op jit(solution)/shard_map/ppermute | solution.py:46
  156.9 3.9 %collective-permute-done.4 = f32[256]{0:T(256)S(1)} collective-permute-done((f32[256]{0:T(256)S(1)}, f32[256]{0:T(256)S(1)}, u32[]{:S(2)}, u32[]{:S(2)}) %collective-permute-start.4) | collective-permute-done | bytes 1056 | tf_op jit(solution)/shard_map/ppermute | solution.py:46
  160.9 2.2 collective-permute-start.5
  163.1 2.2 collective-permute-done.5
  166.0 3.2 %collective-permute-done.6 = f32[256]{0:T(256)S(1)} collective-permute-done((f32[256]{0:T(256)S(1)}, f32[256]{0:T(256)S(1)}, u32[]{:S(2)}, u32[]{:S(2)}) %collective-permute-start.6) | collective-permute-done | bytes 1056 | tf_op jit(solution)/shard_map/ppermute | solution.py:46
  169.6 20.0 %multiply_convert_fusion = bf16[8192,512]{1,0:T(8,128)(2,1)} fusion(bf16[8192,1536]{1,0:T(8,128)(2,1)} %pad_maximum_fusion, bf16[512,512]{1,0:T(8,128)(2,1)S(1)} %get-tuple-element.13, bf16[512,512]{1,0:T(8,128)(2,1)S(1)} %get-tuple-element.12), kind=kOutput, calls=%fused_computation.10 | convolution fusion | flops 12898009088 | bytes 34603008 | tf_op jit(solution)/shard_map/dot_general | solution.py:114
  189.7 108.1 %all_to_all.10 = bf16[64,2,64,512]{3,2,1,0:T(8,128)(2,1)} all-to-all(bf16[64,2,64,512]{3,2,1,0:T(8,128)(2,1)} %bitcast.24), channel_id=1, replica_groups=mesh['x'=4,'yl'=2,'z'=4,'c'=2,'pix'=2] {'x','yl','z','c'}, dimensions={0} | all-to-all | bytes 16777216 | tf_op jit(solution)/shard_map/all_to_all | solution.py:117
  297.8 11.5 %copy.12 = bf16[2,64,64,512]{3,2,1,0:T(8,128)(2,1)} copy(bf16[2,64,64,512]{3,1,0,2:T(8,128)(2,1)} %bitcast.23) | data formatting | bytes 16777216
  (27 shorter events, 4.4 us)
Async XLA Ops:
  12.0 11.2 %copy-start = (s32[4096]{0:T(1024)S(1)}, s32[4096]{0:T(1024)}, u32[]{:S(2)}) copy-start(s32[4096]{0:T(1024)} %param.5) | copy-start | bytes 49156
  12.0 11.4 %copy-start.1 = (s32[256]{0:T(256)S(1)}, s32[256]{0:T(256)}, u32[]{:S(2)}) copy-start(s32[256]{0:T(256)} %param.6) | copy-start | bytes 3076
  12.0 114.6 %all-to-all-start = ((bf16[64,2,64,512]{3,2,1,0:T(8,128)(2,1)}), bf16[64,2,64,512]{3,2,1,0:T(8,128)(2,1)}, u32[]{:S(2)}, u32[]{:S(2)}) async-start(bf16[64,2,64,512]{3,2,1,0:T(8,128)(2,1)} %bitcast.22), calls=%async_computation | async-start | bytes 16777216 | tf_op jit(solution)/shard_map/all_to_all | solution.py:93
  141.0 5.9 %collective-permute-start = (f32[256]{0:T(256)S(1)}, f32[256]{0:T(256)S(1)}, u32[]{:S(2)}, u32[]{:S(2)}) collective-permute-start(f32[256]{0:T(256)S(1)} %fusion.13), channel_id=1, source_target_pairs={{0,2},{2,0},{1,3},{3,1},{4,6},{6,4},{5,7},{7,5},{8,10},{10,8},{9,1... | collective-permute-start | bytes 3080 | tf_op jit(solution)/shard_map/ppermute | solution.py:46
  146.9 3.9 %collective-permute-start.1 = (f32[256]{0:T(256)S(1)}, f32[256]{0:T(256)S(1)}, u32[]{:S(2)}, u32[]{:S(2)}) collective-permute-start(f32[256]{0:T(256)S(1)} %add.137), channel_id=1, source_target_pairs={{0,1},{1,0},{2,3},{3,2},{4,5},{5,4},{6,7},{7,6},{8,9},{9,8},{10,11... | collective-permute-start | bytes 3080 | tf_op jit(solution)/shard_map/ppermute | solution.py:46
  150.9 2.4 collective-permute-start.2
  153.3 3.6 %collective-permute-start.3 = (f32[256]{0:T(256)S(1)}, f32[256]{0:T(256)S(1)}, u32[]{:S(2)}, u32[]{:S(2)}) collective-permute-start(f32[256]{0:T(256)S(1)} %add.139), channel_id=1, source_target_pairs={{0,32},{32,64},{64,96},{96,0},{1,33},{33,65},{65,97},{97,1},{2,34}... | collective-permute-start | bytes 3080 | tf_op jit(solution)/shard_map/ppermute | solution.py:46
  156.9 3.9 %collective-permute-start.4 = (f32[256]{0:T(256)S(1)}, f32[256]{0:T(256)S(1)}, u32[]{:S(2)}, u32[]{:S(2)}) collective-permute-start(f32[256]{0:T(256)S(1)} %add.140), channel_id=1, source_target_pairs={{0,64},{32,96},{64,0},{96,32},{1,65},{33,97},{65,1},{97,33},{2,66}... | collective-permute-start | bytes 3080 | tf_op jit(solution)/shard_map/ppermute | solution.py:46
  160.9 4.4 %collective-permute-start.5 = (f32[256]{0:T(256)S(1)}, f32[256]{0:T(256)S(1)}, u32[]{:S(2)}, u32[]{:S(2)}) collective-permute-start(f32[256]{0:T(256)S(1)} %add.141), channel_id=1, source_target_pairs={{0,4},{4,8},{8,12},{12,0},{1,5},{5,9},{9,13},{13,1},{2,6},{6,10},{... | collective-permute-start | bytes 3080 | tf_op jit(solution)/shard_map/ppermute | solution.py:46
  165.2 3.9 %collective-permute-start.6 = (f32[256]{0:T(256)S(1)}, f32[256]{0:T(256)S(1)}, u32[]{:S(2)}, u32[]{:S(2)}) collective-permute-start(f32[256]{0:T(256)S(1)} %add.142), channel_id=1, source_target_pairs={{0,8},{4,12},{8,0},{12,4},{1,9},{5,13},{9,1},{13,5},{2,10},{6,14},... | collective-permute-start | bytes 3080 | tf_op jit(solution)/shard_map/ppermute | solution.py:46
  169.2 20.5 %copy-start.2 = (f32[256]{0:T(256)}, f32[256]{0:T(256)S(1)}, u32[]{:S(2)}) copy-start(f32[256]{0:T(256)S(1)} %add_sqrt_fusion) | copy-start | bytes 3076

commit v5 on v4

--- a/solution.py
+++ b/solution.py
@@ -48,6 +48,9 @@
     return value
 
 
+HALVES = 2
+
+
 def phase_table(circle_pos, harmonics, ang_count, block):
     angle_count = circle_pos.shape[0]
     residues = circle_pos.reshape(ang_count, block)[:, 0]
@@ -89,10 +92,7 @@
     cell_count = float(row_pix * lax.axis_size("pix") * col_count)
     depth = ang_count * 2 * block
 
-    send = jnp.transpose(grads, (2, 0, 1, 3))
-    moved = lax.all_to_all(send, ANG, split_axis=0, concat_axis=0, tiled=True)
-    flat = moved.reshape(depth, col_count)
-
+    half = col_count // HALVES
     outer, inner = phase_table(circle_pos, harmonics, ang_count, block)
     forward_high, forward_low = split_parts(real_table(outer, inner, False).reshape(2 * kept_count, depth))
     backward_high, backward_low = split_parts(real_table(outer, inner, True).reshape(depth, 2 * kept_count))
@@ -100,8 +100,13 @@
     backward_table = jnp.concatenate((backward_high, backward_low, backward_high), 1)
     forward_table, backward_table = lax.optimization_barrier((forward_table, backward_table))
 
-    stacked = jnp.dot(forward_table, flat, preferred_element_type=jnp.float32)
-    coef = (stacked[: 2 * kept_count] + stacked[2 * kept_count:]) * (1.0 / math.sqrt(angle_count))
+    coefs = []
+    for h in range(HALVES):
+        send = jnp.transpose(grads[:, :, :, h * half:(h + 1) * half], (2, 0, 1, 3))
+        moved = lax.all_to_all(send, ANG, split_axis=0, concat_axis=0, tiled=True)
+        stacked = jnp.dot(forward_table, moved.reshape(depth, half), preferred_element_type=jnp.float32)
+        coefs.append((stacked[: 2 * kept_count] + stacked[2 * kept_count:]) * (1.0 / math.sqrt(angle_count)))
+    coef = jnp.concatenate(coefs, 1)
     coef_re = coef[:kept_count]
     coef_im = coef[kept_count:]
     square_sums = jnp.sum(weight[None, :] * (coef_re * coef_re + coef_im * coef_im), axis=1)

time: 310 us -> 308 us (level)
  waiting for transfers between devices: 62.7 us -> 36.8 us
  other arithmetic: 58.7 us -> 67.1 us
  starting transfers between devices: 21.8 us -> 27.2 us
  local copies, waits for them, and re-layouts: 23 us -> 27.9 us
  matrix products: 34.1 us -> 38.9 us
    all_to_all x1 -> x2, waiting for transfers between devices: 45.3 us -> 21 us  [body(): moved = lax.all_to_all(send, ANG, split_axis=0, concat_axis=0, tiled=True)]
    concatenate x1, other arithmetic: 7.15 us -> 16.9 us  [body(): forward_table = jnp.concatenate((forward_high, forward_low), 0)]
    all_to_all x1 -> x2, starting transfers between devices: 11.2 us -> 20.1 us  [body(): moved = lax.all_to_all(send, ANG, split_axis=0, concat_axis=0, tiled=True)]
    slice x0 -> x1, local copies, waits for them, and re-layouts: none -> 5.26 us  [body(): send = jnp.transpose(grads[:, :, :, h * half:(h + 1) * half], (2, 0, 1, 3))]
    dot_general x1 -> x2, matrix products: 14.1 us -> 18.7 us  [body(): jnp.dot(forward_table, moved.reshape(depth, half), preferred_element_type...]
    add x2, other arithmetic: 7.54 us -> 3.54 us  [real_table(): phase_sin = outer_sin * inner_cos + outer_cos * inner_sin]
    convert_element_type x2, other arithmetic: 11.1 us -> 14.9 us  [split_parts(): low = (value - high.astype(jnp.float32)).astype(jnp.bfloat16)]
    ppermute x7, starting transfers between devices: 10.7 us -> 7.13 us  [global_sum(): value = value + lax.ppermute(value, axis, perm)]
  transfers between devices with their start and end apart: 8 -> 9, of which waited for: 8 -> 8; matrix products, arithmetic and copies ran while one was open for 19% -> 27% of each run, Pallas kernels for 0% -> 0%
where the time goes in v5:
time: 308 us; the launch traced here: 307 us
  blocking collectives  109 us (35%)
  other arithmetic  67.1 us (22%)
  matrix products  38.9 us (13%)
  waiting for transfers between devices  36.8 us (12%)
  local copies, waits for them, and re-layouts  27.9 us (9%)
  starting transfers between devices  27.2 us (9%)
    all_to_all x1, blocking collectives, body(): back = lax.all_to_all(update, ANG, split_axis=0, concat_axis=0, tiled=True)  109 us
    unnamed x17, local copies, waits for them, and re-layouts  22.5 us
    all_to_all x2, waiting for transfers between devices, body(): moved = lax.all_to_all(send, ANG, split_axis=0, concat_axis=0, tiled=True)  21 us
    concatenate x1, other arithmetic, body(): jnp.concatenate((backward_high, backward_low, backward_high), 1)  20.7 us
    dot_general x1, matrix products, body(): jnp.dot(backward_table, step_stack, preferred_element_type=jnp.float32)  20.2 us
    all_to_all x2, starting transfers between devices, body(): moved = lax.all_to_all(send, ANG, split_axis=0, concat_axis=0, tiled=True)  20.1 us
    dot_general x2, matrix products, body(): jnp.dot(forward_table, moved.reshape(depth, half), preferred_element_type...  18.7 us
    concatenate x1, other arithmetic, body(): forward_table = jnp.concatenate((forward_high, forward_low), 0)  16.9 us
  transfers between devices with their start and end apart: 9, of which 8 were waited for; matrix products, arithmetic and copies ran while one was open for 27% of the time, Pallas kernels for 0%

profile of v5, /device:TPU:1, one launch (start us, length us, event | category | flops | bytes accessed | tf_op | source)
XLA Modules:
  0.0 307.5 jit_solution(2914991591204163790)
XLA Ops:
  0.6 5.3 %fusion.47 = (bf16[2,64,64,256]{3,2,1,0:T(8,128)(2,1)S(1)}, bf16[2,64,64,256]{3,2,1,0:T(8,128)(2,1)}) fusion(bf16[2,64,64,512]{3,2,1,0:T(8,128)(2,1)} %param.4), kind=kLoop, calls=%fused_computation.90 | loop fusion | bytes 16777216 | tf_op jit(solution)/shard_map/slice | solution.py:105
  5.9 4.4 %copy.20 = bf16[2,64,64,256]{3,1,0,2:T(8,128)(2,1)} copy(bf16[2,64,64,256]{3,2,1,0:T(8,128)(2,1)S(1)} %get-tuple-element.12) | data formatting | bytes 8388608
  10.3 11.0 %all-to-all-start.1 = ((bf16[64,2,64,256]{3,2,1,0:T(8,128)(2,1)}), bf16[64,2,64,256]{3,2,1,0:T(8,128)(2,1)}, u32[]{:S(2)}, u32[]{:S(2)}) async-start(bf16[64,2,64,256]{3,2,1,0:T(8,128)(2,1)} %bitcast.32), calls=%async_computation.1 | async-start | bytes 8388608 | tf_op jit(solution)/shard_map/all_to_all | solution.py:106
  22.6 1.8 multiply_add_fusion.1
  24.4 2.2 maximum_maximum_fusion
  26.7 7.4 %fusion.1 = (bf16[512,8192]{0,1:T(8,128)(2,1)}, bf16[512,8192]{0,1:T(8,128)(2,1)}) fusion(f32[512,64,2,64]{0,3,2,1:T(8,128)S(1)} %maximum_maximum_fusion), kind=kLoop, calls=%fused_computation.9 | loop fusion | flops 16777216 | bytes 33554432 | tf_op jit(solution)/shard_map/convert_element_type | solution.py:22
  34.1 1.8 multiply_add_fusion
  35.9 6.3 %maximum_maximum_fusion.1 = f32[64,2,64,512]{3,2,1,0:T(8,128)} fusion(f32[64,1,64,256]{3,2,1,0:T(8,128)S(1)} %get-tuple-element.18, f32[64,1,64,256]{3,2,1,0:T(8,128)S(1)} %get-tuple-element.17, f32[64,1,64,256]{3,2,1,0:T(8,128)S(1)} %get-tuple-element.16), kind=kLoop, calls=%fused_computation.3 | loop fusion | flops 12582912 | bytes 29360128 | tf_op jit(solution)/shard_map/concatenate | solution.py:76
  42.1 6.5 %copy.21 = bf16[2,64,64,256]{3,1,0,2:T(8,128)(2,1)} copy(bf16[2,64,64,256]{3,2,1,0:T(8,128)(2,1)} %get-tuple-element.13) | data formatting | bytes 8388608
  48.7 16.9 %pad_maximum_fusion.1 = bf16[1024,8192]{0,1:T(8,128)(2,1)} fusion(bf16[512,8192]{0,1:T(8,128)(2,1)} %get-tuple-element.10, bf16[512,8192]{0,1:T(8,128)(2,1)} %get-tuple-element.11), kind=kLoop, calls=%fused_computation.2 | loop fusion | flops 33554432 | bytes 33554432 | tf_op jit(solution)/shard_map/concatenate | solution.py:99
  65.6 7.4 %fusion = (bf16[8192,512]{1,0:T(8,128)(2,1)}, bf16[8192,512]{1,0:T(8,128)(2,1)}) fusion(f32[64,2,64,512]{3,2,1,0:T(8,128)S(1)} %bitcast.29), kind=kLoop, calls=%fused_computation.6 | loop fusion | flops 16777216 | bytes 33554432 | tf_op jit(solution)/shard_map/convert_element_type | solution.py:22
  73.1 9.0 %all-to-all-start = ((bf16[64,2,64,256]{3,2,1,0:T(8,128)(2,1)}), bf16[64,2,64,256]{3,2,1,0:T(8,128)(2,1)}, u32[]{:S(2)}, u32[]{:S(2)}) async-start(bf16[64,2,64,256]{3,2,1,0:T(8,128)(2,1)} %bitcast.31), calls=%async_computation | async-start | bytes 8388608 | tf_op jit(solution)/shard_map/all_to_all | solution.py:106
  82.1 20.7 %pad_maximum_fusion = bf16[8192,1536]{1,0:T(8,128)(2,1)} fusion(bf16[8192,512]{1,0:T(8,128)(2,1)} %get-tuple-element.9, bf16[8192,512]{1,0:T(8,128)(2,1)} %get-tuple-element.8), kind=kLoop, calls=%fused_computation | loop fusion | flops 75497472 | bytes 41943040 | tf_op jit(solution)/shard_map/concatenate | solution.py:100
  103.5 9.3 %fusion.49 = f32[1024,256]{0,1:T(8,128)S(1)} fusion(bf16[1024,8192]{0,1:T(8,128)(2,1)} %pad_maximum_fusion.1, bf16[8192,256]{1,0:T(8,128)(2,1)} %bitcast.5), kind=kOutput, calls=%fused_computation.92 | convolution fusion | flops 4294967296 | bytes 22020096 | tf_op jit(solution)/shard_map/dot_general | solution.py:107
  112.9 21.0 %all-to-all-done = bf16[64,2,64,256]{3,2,1,0:T(8,128)(2,1)} async-done(((bf16[64,2,64,256]{3,2,1,0:T(8,128)(2,1)}), bf16[64,2,64,256]{3,2,1,0:T(8,128)(2,1)}, u32[]{:S(2)}, u32[]{:S(2)}) %all-to-all-start) | async-done | bytes 4194336 | tf_op jit(solution)/shard_map/all_to_all | solution.py:106
  133.9 9.4 %fusion.48 = f32[1024,256]{0,1:T(8,128)S(1)} fusion(bf16[1024,8192]{0,1:T(8,128)(2,1)} %pad_maximum_fusion.1, bf16[8192,256]{1,0:T(8,128)(2,1)} %bitcast.3), kind=kOutput, calls=%fused_computation.91 | convolution fusion | flops 4294967296 | bytes 22020096 | tf_op jit(solution)/shard_map/dot_general | solution.py:107
  145.1 2.6 collective-permute-start.1
  152.0 3.1 %collective-permute-done.3 = f32[256]{0:T(256)S(1)} collective-permute-done((f32[256]{0:T(256)S(1)}, f32[256]{0:T(256)S(1)}, u32[]{:S(2)}, u32[]{:S(2)}) %collective-permute-start.3) | collective-permute-done | bytes 1056 | tf_op jit(solution)/shard_map/ppermute | solution.py:46
  155.3 3.7 %collective-permute-done.4 = f32[256]{0:T(256)S(1)} collective-permute-done((f32[256]{0:T(256)S(1)}, f32[256]{0:T(256)S(1)}, u32[]{:S(2)}, u32[]{:S(2)}) %collective-permute-start.4) | collective-permute-done | bytes 1056 | tf_op jit(solution)/shard_map/ppermute | solution.py:46
  159.5 3.1 %collective-permute-done.5 = f32[256]{0:T(256)S(1)} collective-permute-done((f32[256]{0:T(256)S(1)}, f32[256]{0:T(256)S(1)}, u32[]{:S(2)}, u32[]{:S(2)}) %collective-permute-start.5) | collective-permute-done | bytes 1056 | tf_op jit(solution)/shard_map/ppermute | solution.py:46
  164.2 2.3 collective-permute-done.6
  166.9 20.2 %multiply_convert_fusion = bf16[8192,512]{1,0:T(8,128)(2,1)} fusion(bf16[8192,1536]{1,0:T(8,128)(2,1)} %pad_maximum_fusion, bf16[512,512]{0,1:T(8,128)(2,1)S(1)} %get-tuple-element.15, bf16[512,512]{0,1:T(8,128)(2,1)S(1)} %get-tuple-element.14), kind=kOutput, calls=%fused_computation.10 | convolution fusion | flops 12898009088 | bytes 34603008 | tf_op jit(solution)/shard_map/dot_general | solution.py:119
  187.1 108.8 %all_to_all.15 = bf16[64,2,64,512]{3,2,1,0:T(8,128)(2,1)} all-to-all(bf16[64,2,64,512]{3,2,1,0:T(8,128)(2,1)} %bitcast.33), channel_id=1, replica_groups=mesh['x'=4,'yl'=2,'z'=4,'c'=2,'pix'=2] {'x','yl','z','c'}, dimensions={0} | all-to-all | bytes 16777216 | tf_op jit(solution)/shard_map/all_to_all | solution.py:122
  295.9 11.5 %copy.15 = bf16[2,64,64,512]{3,2,1,0:T(8,128)(2,1)} copy(bf16[2,64,64,512]{3,1,0,2:T(8,128)(2,1)} %bitcast.30) | data formatting | bytes 16777216
  (41 shorter events, 10.8 us)
Async XLA Ops:
  5.9 15.4 %copy-start = (s32[4096]{0:T(1024)S(1)}, s32[4096]{0:T(1024)}, u32[]{:S(2)}) copy-start(s32[4096]{0:T(1024)} %param.5) | copy-start | bytes 49156
  5.9 15.6 %copy-start.1 = (s32[256]{0:T(256)S(1)}, s32[256]{0:T(256)}, u32[]{:S(2)}) copy-start(s32[256]{0:T(256)} %param.6) | copy-start | bytes 3076
  10.3 62.8 %all-to-all-start.1 = ((bf16[64,2,64,256]{3,2,1,0:T(8,128)(2,1)}), bf16[64,2,64,256]{3,2,1,0:T(8,128)(2,1)}, u32[]{:S(2)}, u32[]{:S(2)}) async-start(bf16[64,2,64,256]{3,2,1,0:T(8,128)(2,1)} %bitcast.32), calls=%async_computation.1 | async-start | bytes 8388608 | tf_op jit(solution)/shard_map/all_to_all | solution.py:106
  48.7 16.9 %slice-start = ((s8[16777216]{0:T(1024)(128)(4,1)}), s8[4194304]{0:T(1024)(128)(4,1)S(1)}, s32[]{:S(2)}) async-start(s8[16777216]{0:T(1024)(128)(4,1)} %bitcast.28), calls=%async_computation.3 | async-start | bytes 8388608
  48.7 16.9 %slice-start.1 = ((s8[16777216]{0:T(1024)(128)(4,1)}), s8[4194304]{0:T(1024)(128)(4,1)S(1)}, s32[]{:S(2)}) async-start(s8[16777216]{0:T(1024)(128)(4,1)} %bitcast.28), calls=%async_computation.4 | async-start | bytes 8388608
  48.7 16.9 %slice-start.2 = ((s8[16777216]{0:T(1024)(128)(4,1)}), s8[4194304]{0:T(1024)(128)(4,1)S(1)}, s32[]{:S(2)}) async-start(s8[16777216]{0:T(1024)(128)(4,1)} %bitcast.28), calls=%async_computation.5 | async-start | bytes 8388608
  48.7 16.9 %slice-start.3 = ((s8[16777216]{0:T(1024)(128)(4,1)}), s8[4194304]{0:T(1024)(128)(4,1)S(1)}, s32[]{:S(2)}) async-start(s8[16777216]{0:T(1024)(128)(4,1)} %bitcast.28), calls=%async_computation.6 | async-start | bytes 8388608
  73.1 60.8 %all-to-all-start = ((bf16[64,2,64,256]{3,2,1,0:T(8,128)(2,1)}), bf16[64,2,64,256]{3,2,1,0:T(8,128)(2,1)}, u32[]{:S(2)}, u32[]{:S(2)}) async-start(bf16[64,2,64,256]{3,2,1,0:T(8,128)(2,1)} %bitcast.31), calls=%async_computation | async-start | bytes 8388608 | tf_op jit(solution)/shard_map/all_to_all | solution.py:106
  143.6 1.5 collective-permute-start
  145.1 3.9 %collective-permute-start.1 = (f32[256]{0:T(256)S(1)}, f32[256]{0:T(256)S(1)}, u32[]{:S(2)}, u32[]{:S(2)}) collective-permute-start(f32[256]{0:T(256)S(1)} %add.141), channel_id=1, source_target_pairs={{0,1},{1,0},{2,3},{3,2},{4,5},{5,4},{6,7},{7,6},{8,9},{9,8},{10,11... | collective-permute-start | bytes 3080 | tf_op jit(solution)/shard_map/ppermute | solution.py:46
  149.0 2.4 collective-permute-start.2
  151.4 3.6 %collective-permute-start.3 = (f32[256]{0:T(256)S(1)}, f32[256]{0:T(256)S(1)}, u32[]{:S(2)}, u32[]{:S(2)}) collective-permute-start(f32[256]{0:T(256)S(1)} %add.143), channel_id=1, source_target_pairs={{0,32},{32,64},{64,96},{96,0},{1,33},{33,65},{65,97},{97,1},{2,34}... | collective-permute-start | bytes 3080 | tf_op jit(solution)/shard_map/ppermute | solution.py:46
  155.1 3.9 %collective-permute-start.4 = (f32[256]{0:T(256)S(1)}, f32[256]{0:T(256)S(1)}, u32[]{:S(2)}, u32[]{:S(2)}) collective-permute-start(f32[256]{0:T(256)S(1)} %add.144), channel_id=1, source_target_pairs={{0,64},{32,96},{64,0},{96,32},{1,65},{33,97},{65,1},{97,33},{2,66}... | collective-permute-start | bytes 3080 | tf_op jit(solution)/shard_map/ppermute | solution.py:46
  159.0 3.6 %collective-permute-start.5 = (f32[256]{0:T(256)S(1)}, f32[256]{0:T(256)S(1)}, u32[]{:S(2)}, u32[]{:S(2)}) collective-permute-start(f32[256]{0:T(256)S(1)} %add.145), channel_id=1, source_target_pairs={{0,4},{4,8},{8,12},{12,0},{1,5},{5,9},{9,13},{13,1},{2,6},{6,10},{... | collective-permute-start | bytes 3080 | tf_op jit(solution)/shard_map/ppermute | solution.py:46
  162.6 3.9 %collective-permute-start.6 = (f32[256]{0:T(256)S(1)}, f32[256]{0:T(256)S(1)}, u32[]{:S(2)}, u32[]{:S(2)}) collective-permute-start(f32[256]{0:T(256)S(1)} %add.146), channel_id=1, source_target_pairs={{0,8},{4,12},{8,0},{12,4},{1,9},{5,13},{9,1},{13,5},{2,10},{6,14},... | collective-permute-start | bytes 3080 | tf_op jit(solution)/shard_map/ppermute | solution.py:46
  166.6 20.5 %copy-start.2 = (f32[256]{0:T(256)}, f32[256]{0:T(256)S(1)}, u32[]{:S(2)}) copy-start(f32[256]{0:T(256)S(1)} %add_sqrt_fusion) | copy-start | bytes 3076

commit v6 on v5

--- a/solution.py
+++ b/solution.py
@@ -95,16 +95,21 @@
     half = col_count // HALVES
     outer, inner = phase_table(circle_pos, harmonics, ang_count, block)
     forward_high, forward_low = split_parts(real_table(outer, inner, False).reshape(2 * kept_count, depth))
-    backward_high, backward_low = split_parts(real_table(outer, inner, True).reshape(depth, 2 * kept_count))
-    forward_table = jnp.concatenate((forward_high, forward_low), 0)
-    backward_table = jnp.concatenate((backward_high, backward_low, backward_high), 1)
-    forward_table, backward_table = lax.optimization_barrier((forward_table, backward_table))
+    forward_table = lax.optimization_barrier(jnp.concatenate((forward_high, forward_low), 0))
 
     coefs = []
     for h in range(HALVES):
         send = jnp.transpose(grads[:, :, :, h * half:(h + 1) * half], (2, 0, 1, 3))
         moved = lax.all_to_all(send, ANG, split_axis=0, concat_axis=0, tiled=True)
+        if h == 1:
+            moved, backward_table = lax.optimization_barrier((moved, backward_table))
         stacked = jnp.dot(forward_table, moved.reshape(depth, half), preferred_element_type=jnp.float32)
+        if h == 0:
+            outer, inner, stacked = lax.optimization_barrier((outer, inner, stacked))
+            backward_high, backward_low = split_parts(
+                real_table(outer, inner, True).reshape(depth, 2 * kept_count)
+            )
+            backward_table = jnp.concatenate((backward_high, backward_low, backward_high), 1)
         coefs.append((stacked[: 2 * kept_count] + stacked[2 * kept_count:]) * (1.0 / math.sqrt(angle_count)))
     coef = jnp.concatenate(coefs, 1)
     coef_re = coef[:kept_count]

time: 308 us -> 307 us (level)
  other arithmetic: 67.1 us -> 55.2 us
  waiting for transfers between devices: 36.8 us -> 48.5 us
    all_to_all x2, waiting for transfers between devices: 21 us -> 32.7 us  [body(): moved = lax.all_to_all(send, ANG, split_axis=0, concat_axis=0, tiled=True)]
    concatenate x1, other arithmetic: 16.9 us -> 7.19 us  [body(): jnp.concatenate((forward_high, forward_low), 0)]
    unnamed x17 -> x9, local copies, waits for them, and re-layouts: 22.5 us -> 22.5 us
  transfers between devices with their start and end apart: 9 -> 9, of which waited for: 8 -> 9; matrix products, arithmetic and copies ran while one was open for 27% -> 23% of each run, Pallas kernels for 0% -> 0%
where the time goes in v6:
time: 307 us; the launch traced here: 306 us
  blocking collectives  109 us (36%)
  other arithmetic  55.2 us (18%)
  waiting for transfers between devices  48.5 us (16%)
  matrix products  38.7 us (13%)
  local copies, waits for them, and re-layouts  28 us (9%)
  starting transfers between devices  26.4 us (9%)
    all_to_all x1, blocking collectives, body(): back = lax.all_to_all(update, ANG, split_axis=0, concat_axis=0, tiled=True)  109 us
    all_to_all x2, waiting for transfers between devices, body(): moved = lax.all_to_all(send, ANG, split_axis=0, concat_axis=0, tiled=True)  32.7 us
    unnamed x9, local copies, waits for them, and re-layouts  22.5 us
    dot_general x1, matrix products, body(): jnp.dot(backward_table, step_stack, preferred_element_type=jnp.float32)  20 us
    concatenate x1, other arithmetic, body(): jnp.concatenate((backward_high, backward_low, backward_high), 1)  19.4 us
    all_to_all x2, starting transfers between devices, body(): moved = lax.all_to_all(send, ANG, split_axis=0, concat_axis=0, tiled=True)  19.2 us
    dot_general x2, matrix products, body(): jnp.dot(forward_table, moved.reshape(depth, half), preferred_element_type...  18.7 us
    ppermute x7, waiting for transfers between devices, global_sum(): value = value + lax.ppermute(value, axis, perm)  15.8 us
  transfers between devices with their start and end apart: 9, of which 9 were waited for; matrix products, arithmetic and copies ran while one was open for 23% of the time, Pallas kernels for 0%

profile of v6, /device:TPU:1, one launch (start us, length us, event | category | flops | bytes accessed | tf_op | source)
XLA Modules:
  0.0 306.3 jit_solution(3089628186028106908)
XLA Ops:
  0.6 5.2 %fusion.33 = (bf16[2,64,64,256]{3,2,1,0:T(8,128)(2,1)S(1)}, bf16[2,64,64,256]{3,2,1,0:T(8,128)(2,1)}) fusion(bf16[2,64,64,512]{3,2,1,0:T(8,128)(2,1)} %param.4), kind=kLoop, calls=%fused_computation.68 | loop fusion | bytes 16777216 | tf_op jit(solution)/shard_map/slice | solution.py:102
  5.9 4.4 %copy.33 = bf16[2,64,64,256]{3,1,0,2:T(8,128)(2,1)} copy(bf16[2,64,64,256]{3,2,1,0:T(8,128)(2,1)S(1)} %get-tuple-element.22) | data formatting | bytes 8388608
  10.3 11.0 %all-to-all-start.1 = ((bf16[64,2,64,256]{3,2,1,0:T(8,128)(2,1)}), bf16[64,2,64,256]{3,2,1,0:T(8,128)(2,1)}, u32[]{:S(2)}, u32[]{:S(2)}) async-start(bf16[64,2,64,256]{3,2,1,0:T(8,128)(2,1)} %bitcast.34), calls=%async_computation.1 | async-start | bytes 8388608 | tf_op jit(solution)/shard_map/all_to_all | solution.py:103
  23.8 6.3 %maximum_maximum_fusion = f32[512,64,2,64]{0,3,2,1:T(8,128)} fusion(f32[256,64,1,64]{0,3,2,1:T(8,128)S(1)} %get-tuple-element.31, f32[256,64,1,64]{0,3,2,1:T(8,128)S(1)} %get-tuple-element.30, f32[256,64,1,64]{0,3,2,1:T(8,128)S(1)} %get-tuple-element.29), kind=kLoop, calls=%fused_computation.1 | loop fusion | flops 12582912 | bytes 29360128 | tf_op jit(solution)/shard_map/concatenate | solution.py:76
  30.1 6.6 %copy.34 = bf16[2,64,64,256]{3,1,0,2:T(8,128)(2,1)} copy(bf16[2,64,64,256]{3,2,1,0:T(8,128)(2,1)} %get-tuple-element.23) | data formatting | bytes 8388608
  36.7 7.2 %fusion.1 = (bf16[512,8192]{0,1:T(8,128)(2,1)S(1)}, bf16[512,8192]{0,1:T(8,128)(2,1)S(1)}) fusion(f32[512,64,2,64]{0,3,2,1:T(8,128)} %maximum_maximum_fusion), kind=kLoop, calls=%fused_computation.9 | loop fusion | flops 16777216 | bytes 33554432 | tf_op jit(solution)/shard_map/convert_element_type | solution.py:22
  43.9 7.2 %pad_maximum_fusion.1 = bf16[1024,8192]{0,1:T(8,128)(2,1)} fusion(bf16[512,8192]{0,1:T(8,128)(2,1)S(1)} %get-tuple-element.20, bf16[512,8192]{0,1:T(8,128)(2,1)S(1)} %get-tuple-element.21), kind=kLoop, calls=%fused_computation.2 | loop fusion | flops 33554432 | bytes 33554432 | tf_op jit(solution)/shard_map/concatenate | solution.py:98
  51.8 21.2 %all-to-all-done.1 = bf16[64,2,64,256]{3,2,1,0:T(8,128)(2,1)} async-done(((bf16[64,2,64,256]{3,2,1,0:T(8,128)(2,1)}), bf16[64,2,64,256]{3,2,1,0:T(8,128)(2,1)}, u32[]{:S(2)}, u32[]{:S(2)}) %all-to-all-start.1) | async-done | bytes 4194336 | tf_op jit(solution)/shard_map/all_to_all | solution.py:103
  73.1 8.2 %all-to-all-start = ((bf16[64,2,64,256]{3,2,1,0:T(8,128)(2,1)}), bf16[64,2,64,256]{3,2,1,0:T(8,128)(2,1)}, u32[]{:S(2)}, u32[]{:S(2)}) async-start(bf16[64,2,64,256]{3,2,1,0:T(8,128)(2,1)} %bitcast.33), calls=%async_computation | async-start | bytes 8388608 | tf_op jit(solution)/shard_map/all_to_all | solution.py:103
  81.3 9.4 %fusion.34 = f32[1024,256]{1,0:T(8,128)S(1)} fusion(bf16[1024,8192]{0,1:T(8,128)(2,1)} %pad_maximum_fusion.1, bf16[8192,256]{1,0:T(8,128)(2,1)} %bitcast.3), kind=kOutput, calls=%fused_computation.69 | convolution fusion | flops 4294967296 | bytes 22020096 | tf_op jit(solution)/shard_map/dot_general | solution.py:106
  90.6 1.7 multiply_add_fusion
  92.4 2.2 maximum_maximum_fusion.1
  94.6 7.5 %fusion = (bf16[8192,512]{1,0:T(8,128)(2,1)}, bf16[8192,512]{1,0:T(8,128)(2,1)}) fusion(f32[64,2,64,512]{3,2,1,0:T(8,128)S(1)} %maximum_maximum_fusion.1), kind=kLoop, calls=%fused_computation.6 | loop fusion | flops 16777216 | bytes 33554432 | tf_op jit(solution)/shard_map/convert_element_type | solution.py:22
  102.1 19.4 %pad_maximum_fusion = bf16[8192,1536]{1,0:T(8,128)(2,1)} fusion(bf16[8192,512]{1,0:T(8,128)(2,1)} %get-tuple-element.19, bf16[8192,512]{1,0:T(8,128)(2,1)} %get-tuple-element.18), kind=kLoop, calls=%fused_computation | loop fusion | flops 75497472 | bytes 41943040 | tf_op jit(solution)/shard_map/concatenate | solution.py:112
  121.5 11.5 %all-to-all-done = bf16[64,2,64,256]{3,2,1,0:T(8,128)(2,1)} async-done(((bf16[64,2,64,256]{3,2,1,0:T(8,128)(2,1)}), bf16[64,2,64,256]{3,2,1,0:T(8,128)(2,1)}, u32[]{:S(2)}, u32[]{:S(2)}) %all-to-all-start) | async-done | bytes 4194336 | tf_op jit(solution)/shard_map/all_to_all | solution.py:103
  133.0 9.3 %fusion.35 = f32[1024,256]{1,0:T(8,128)S(1)} fusion(bf16[1024,8192]{0,1:T(8,128)(2,1)} %pad_maximum_fusion.1, bf16[8192,256]{1,0:T(8,128)(2,1)} %bitcast.9), kind=kOutput, calls=%fused_computation.70 | convolution fusion | flops 4294967296 | bytes 22020096 | tf_op jit(solution)/shard_map/dot_general | solution.py:106
  144.2 2.6 collective-permute-start.1
  151.0 3.1 %collective-permute-done.3 = f32[256]{0:T(256)S(1)} collective-permute-done((f32[256]{0:T(256)S(1)}, f32[256]{0:T(256)S(1)}, u32[]{:S(2)}, u32[]{:S(2)}) %collective-permute-start.3) | collective-permute-done | bytes 1056 | tf_op jit(solution)/shard_map/ppermute | solution.py:46
  154.3 3.7 %collective-permute-done.4 = f32[256]{0:T(256)S(1)} collective-permute-done((f32[256]{0:T(256)S(1)}, f32[256]{0:T(256)S(1)}, u32[]{:S(2)}, u32[]{:S(2)}) %collective-permute-start.4) | collective-permute-done | bytes 1056 | tf_op jit(solution)/shard_map/ppermute | solution.py:46
  158.6 3.1 %collective-permute-done.5 = f32[256]{0:T(256)S(1)} collective-permute-done((f32[256]{0:T(256)S(1)}, f32[256]{0:T(256)S(1)}, u32[]{:S(2)}, u32[]{:S(2)}) %collective-permute-start.5) | collective-permute-done | bytes 1056 | tf_op jit(solution)/shard_map/ppermute | solution.py:46
  163.3 2.3 collective-permute-done.6
  165.9 20.0 %multiply_convert_fusion = bf16[8192,512]{1,0:T(8,128)(2,1)} fusion(bf16[8192,1536]{1,0:T(8,128)(2,1)} %pad_maximum_fusion, bf16[512,512]{1,0:T(8,128)(2,1)S(1)} %get-tuple-element.25, bf16[512,512]{1,0:T(8,128)(2,1)S(1)} %get-tuple-element.24), kind=kOutput, calls=%fused_computation.10 | convolution fusion | flops 12898009088 | bytes 34603008 | tf_op jit(solution)/shard_map/dot_general | solution.py:124
  186.0 108.8 %all_to_all.15 = bf16[64,2,64,512]{3,2,1,0:T(8,128)(2,1)} all-to-all(bf16[64,2,64,512]{3,2,1,0:T(8,128)(2,1)} %bitcast.35), channel_id=1, replica_groups=mesh['x'=4,'yl'=2,'z'=4,'c'=2,'pix'=2] {'x','yl','z','c'}, dimensions={0} | all-to-all | bytes 16777216 | tf_op jit(solution)/shard_map/all_to_all | solution.py:127
  294.8 11.5 %copy.27 = bf16[2,64,64,512]{3,2,1,0:T(8,128)(2,1)} copy(bf16[2,64,64,512]{3,1,0,2:T(8,128)(2,1)} %bitcast.32) | data formatting | bytes 16777216
  (31 shorter events, 11.8 us)
Async XLA Ops:
  5.9 15.5 %copy-start = (s32[4096]{0:T(1024)S(1)}, s32[4096]{0:T(1024)}, u32[]{:S(2)}) copy-start(s32[4096]{0:T(1024)} %param.5) | copy-start | bytes 49156
  5.9 15.6 %copy-start.2 = (s32[256]{0:T(256)S(1)}, s32[256]{0:T(256)}, u32[]{:S(2)}) copy-start(s32[256]{0:T(256)} %param.6) | copy-start | bytes 3076
  10.3 62.8 %all-to-all-start.1 = ((bf16[64,2,64,256]{3,2,1,0:T(8,128)(2,1)}), bf16[64,2,64,256]{3,2,1,0:T(8,128)(2,1)}, u32[]{:S(2)}, u32[]{:S(2)}) async-start(bf16[64,2,64,256]{3,2,1,0:T(8,128)(2,1)} %bitcast.34), calls=%async_computation.1 | async-start | bytes 8388608 | tf_op jit(solution)/shard_map/all_to_all | solution.py:103
  73.1 60.0 %all-to-all-start = ((bf16[64,2,64,256]{3,2,1,0:T(8,128)(2,1)}), bf16[64,2,64,256]{3,2,1,0:T(8,128)(2,1)}, u32[]{:S(2)}, u32[]{:S(2)}) async-start(bf16[64,2,64,256]{3,2,1,0:T(8,128)(2,1)} %bitcast.33), calls=%async_computation | async-start | bytes 8388608 | tf_op jit(solution)/shard_map/all_to_all | solution.py:103
  142.7 1.5 collective-permute-start
  144.2 3.9 %collective-permute-start.1 = (f32[256]{0:T(256)S(1)}, f32[256]{0:T(256)S(1)}, u32[]{:S(2)}, u32[]{:S(2)}) collective-permute-start(f32[256]{0:T(256)S(1)} %add.117), channel_id=1, source_target_pairs={{0,1},{1,0},{2,3},{3,2},{4,5},{5,4},{6,7},{7,6},{8,9},{9,8},{10,11... | collective-permute-start | bytes 3080 | tf_op jit(solution)/shard_map/ppermute | solution.py:46
  148.1 2.4 collective-permute-start.2
  150.5 3.6 %collective-permute-start.3 = (f32[256]{0:T(256)S(1)}, f32[256]{0:T(256)S(1)}, u32[]{:S(2)}, u32[]{:S(2)}) collective-permute-start(f32[256]{0:T(256)S(1)} %add.119), channel_id=1, source_target_pairs={{0,32},{32,64},{64,96},{96,0},{1,33},{33,65},{65,97},{97,1},{2,34}... | collective-permute-start | bytes 3080 | tf_op jit(solution)/shard_map/ppermute | solution.py:46
  154.1 3.9 %collective-permute-start.4 = (f32[256]{0:T(256)S(1)}, f32[256]{0:T(256)S(1)}, u32[]{:S(2)}, u32[]{:S(2)}) collective-permute-start(f32[256]{0:T(256)S(1)} %add.120), channel_id=1, source_target_pairs={{0,64},{32,96},{64,0},{96,32},{1,65},{33,97},{65,1},{97,33},{2,66}... | collective-permute-start | bytes 3080 | tf_op jit(solution)/shard_map/ppermute | solution.py:46
  158.1 3.6 %collective-permute-start.5 = (f32[256]{0:T(256)S(1)}, f32[256]{0:T(256)S(1)}, u32[]{:S(2)}, u32[]{:S(2)}) collective-permute-start(f32[256]{0:T(256)S(1)} %add.121), channel_id=1, source_target_pairs={{0,4},{4,8},{8,12},{12,0},{1,5},{5,9},{9,13},{13,1},{2,6},{6,10},{... | collective-permute-start | bytes 3080 | tf_op jit(solution)/shard_map/ppermute | solution.py:46
  161.7 3.9 %collective-permute-start.6 = (f32[256]{0:T(256)S(1)}, f32[256]{0:T(256)S(1)}, u32[]{:S(2)}, u32[]{:S(2)}) collective-permute-start(f32[256]{0:T(256)S(1)} %add.122), channel_id=1, source_target_pairs={{0,8},{4,12},{8,0},{12,4},{1,9},{5,13},{9,1},{13,5},{2,10},{6,14},... | collective-permute-start | bytes 3080 | tf_op jit(solution)/shard_map/ppermute | solution.py:46
  165.6 20.3 %copy-start.1 = (f32[256]{0:T(256)}, f32[256]{0:T(256)S(1)}, u32[]{:S(2)}) copy-start(f32[256]{0:T(256)S(1)} %add_sqrt_fusion) | copy-start | bytes 3076

commit v7 on v6

--- a/solution.py
+++ b/solution.py
@@ -40,11 +40,17 @@
 def global_sum(value):
     for axis in ("c", "pix", "yl", "x", "z"):
         size = lax.axis_size(axis)
-        shift = 1
-        while shift < size:
-            perm = [(i, (i + shift) % size) for i in range(size)]
-            value = value + lax.ppermute(value, axis, perm)
-            shift *= 2
+        if size == 2:
+            value = value + lax.ppermute(value, axis, [(0, 1), (1, 0)])
+            continue
+        parts = [value] + [
+            lax.ppermute(value, axis, [(i, (i + shift) % size) for i in range(size)]) for shift in range(1, size)
+        ]
+        order = (lax.axis_index(axis) - jnp.arange(size)) % size
+        ordered = jnp.stack(parts)[order]
+        value = ordered[0]
+        for position in range(1, size):
+            value = value + ordered[position]
     return value
 
 

time: 307 us -> 305 us (level)
  waiting for transfers between devices: 48.5 us -> 42.1 us
  starting transfers between devices: 26.4 us -> 30.3 us
    ppermute x7 -> x9, waiting for transfers between devices: 15.8 us -> 10.1 us  [the longest x6 6.66 us: global_sum(): lax.ppermute(value, axis, [(i, (i + shift) % size) for i in range(size)])]
    ppermute x7 -> x9, starting transfers between devices: 7.14 us -> 11.1 us  [the longest x6 6.76 us: global_sum(): lax.ppermute(value, axis, [(i, (i + shift) % size) for i in range(size)])]
  transfers between devices with their start and end apart: 9 -> 11, of which waited for: 9 -> 9; matrix products, arithmetic and copies ran while one was open for 23% -> 23% of each run, Pallas kernels for 0% -> 0%
where the time goes in v7:
time: 305 us; the launch traced here: 304 us
  blocking collectives  107 us (35%)
  other arithmetic  56 us (18%)
  waiting for transfers between devices  42.1 us (14%)
  matrix products  38.7 us (13%)
  starting transfers between devices  30.3 us (10%)
  local copies, waits for them, and re-layouts  29.1 us (10%)
    all_to_all x1, blocking collectives, body(): back = lax.all_to_all(update, ANG, split_axis=0, concat_axis=0, tiled=True)  107 us
    all_to_all x2, waiting for transfers between devices, body(): moved = lax.all_to_all(send, ANG, split_axis=0, concat_axis=0, tiled=True)  32 us
    unnamed x9, local copies, waits for them, and re-layouts  22.6 us
    concatenate x1, other arithmetic, body(): jnp.concatenate((backward_high, backward_low, backward_high), 1)  20.2 us
    dot_general x1, matrix products, body(): jnp.dot(backward_table, step_stack, preferred_element_type=jnp.float32)  20 us
    all_to_all x2, starting transfers between devices, body(): moved = lax.all_to_all(send, ANG, split_axis=0, concat_axis=0, tiled=True)  19.2 us
    dot_general x2, matrix products, body(): jnp.dot(forward_table, moved.reshape(depth, half), preferred_element_type...  18.7 us
    convert_element_type x2, other arithmetic, split_parts(): low = (value - high.astype(jnp.float32)).astype(jnp.bfloat16)  14.7 us
  transfers between devices with their start and end apart: 11, of which 9 were waited for; matrix products, arithmetic and copies ran while one was open for 23% of the time, Pallas kernels for 0%

profile of v7, /device:TPU:1, one launch (start us, length us, event | category | flops | bytes accessed | tf_op | source)
XLA Modules:
  0.0 304.4 jit_solution(10591346041519196624)
XLA Ops:
  0.6 5.2 %fusion.38 = (bf16[2,64,64,256]{3,2,1,0:T(8,128)(2,1)S(1)}, bf16[2,64,64,256]{3,2,1,0:T(8,128)(2,1)}) fusion(bf16[2,64,64,512]{3,2,1,0:T(8,128)(2,1)} %param.4), kind=kLoop, calls=%fused_computation.93 | loop fusion | bytes 16777216 | tf_op jit(solution)/shard_map/slice | solution.py:108
  5.9 4.4 %copy.33 = bf16[2,64,64,256]{3,1,0,2:T(8,128)(2,1)} copy(bf16[2,64,64,256]{3,2,1,0:T(8,128)(2,1)S(1)} %get-tuple-element.22) | data formatting | bytes 8388608
  10.3 11.0 %all-to-all-start.1 = ((bf16[64,2,64,256]{3,2,1,0:T(8,128)(2,1)}), bf16[64,2,64,256]{3,2,1,0:T(8,128)(2,1)}, u32[]{:S(2)}, u32[]{:S(2)}) async-start(bf16[64,2,64,256]{3,2,1,0:T(8,128)(2,1)} %bitcast.47), calls=%async_computation.1 | async-start | bytes 8388608 | tf_op jit(solution)/shard_map/all_to_all | solution.py:109
  23.8 6.3 %maximum_maximum_fusion = f32[512,64,2,64]{0,3,2,1:T(8,128)} fusion(f32[256,64,1,64]{0,3,2,1:T(8,128)S(1)} %get-tuple-element.31, f32[256,64,1,64]{0,3,2,1:T(8,128)S(1)} %get-tuple-element.30, f32[256,64,1,64]{0,3,2,1:T(8,128)S(1)} %get-tuple-element.29), kind=kLoop, calls=%fused_computation.3 | loop fusion | flops 12582912 | bytes 29360128 | tf_op jit(solution)/shard_map/concatenate | solution.py:82
  30.1 6.6 %copy.34 = bf16[2,64,64,256]{3,1,0,2:T(8,128)(2,1)} copy(bf16[2,64,64,256]{3,2,1,0:T(8,128)(2,1)} %get-tuple-element.23) | data formatting | bytes 8388608
  36.7 7.2 %fusion.1 = (bf16[512,8192]{0,1:T(8,128)(2,1)S(1)}, bf16[512,8192]{0,1:T(8,128)(2,1)S(1)}) fusion(f32[512,64,2,64]{0,3,2,1:T(8,128)} %maximum_maximum_fusion), kind=kLoop, calls=%fused_computation.11 | loop fusion | flops 16777216 | bytes 33554432 | tf_op jit(solution)/shard_map/convert_element_type | solution.py:22
  44.0 7.2 %pad_maximum_fusion.1 = bf16[1024,8192]{0,1:T(8,128)(2,1)} fusion(bf16[512,8192]{0,1:T(8,128)(2,1)S(1)} %get-tuple-element.20, bf16[512,8192]{0,1:T(8,128)(2,1)S(1)} %get-tuple-element.21), kind=kLoop, calls=%fused_computation.4 | loop fusion | flops 33554432 | bytes 33554432 | tf_op jit(solution)/shard_map/concatenate | solution.py:104
  51.9 21.2 %all-to-all-done.1 = bf16[64,2,64,256]{3,2,1,0:T(8,128)(2,1)} async-done(((bf16[64,2,64,256]{3,2,1,0:T(8,128)(2,1)}), bf16[64,2,64,256]{3,2,1,0:T(8,128)(2,1)}, u32[]{:S(2)}, u32[]{:S(2)}) %all-to-all-start.1) | async-done | bytes 4194336 | tf_op jit(solution)/shard_map/all_to_all | solution.py:109
  73.1 8.2 %all-to-all-start = ((bf16[64,2,64,256]{3,2,1,0:T(8,128)(2,1)}), bf16[64,2,64,256]{3,2,1,0:T(8,128)(2,1)}, u32[]{:S(2)}, u32[]{:S(2)}) async-start(bf16[64,2,64,256]{3,2,1,0:T(8,128)(2,1)} %bitcast.46), calls=%async_computation | async-start | bytes 8388608 | tf_op jit(solution)/shard_map/all_to_all | solution.py:109
  81.3 9.4 %fusion.39 = f32[1024,256]{1,0:T(8,128)S(1)} fusion(bf16[1024,8192]{0,1:T(8,128)(2,1)} %pad_maximum_fusion.1, bf16[8192,256]{1,0:T(8,128)(2,1)} %bitcast.3), kind=kOutput, calls=%fused_computation.94 | convolution fusion | flops 4294967296 | bytes 22020096 | tf_op jit(solution)/shard_map/dot_general | solution.py:112
  90.6 1.7 multiply_add_fusion
  92.4 2.2 maximum_maximum_fusion.1
  94.6 7.4 %fusion = (bf16[8192,512]{1,0:T(8,128)(2,1)}, bf16[8192,512]{1,0:T(8,128)(2,1)}) fusion(f32[64,2,64,512]{3,2,1,0:T(8,128)S(1)} %maximum_maximum_fusion.1), kind=kLoop, calls=%fused_computation.8 | loop fusion | flops 16777216 | bytes 33554432 | tf_op jit(solution)/shard_map/convert_element_type | solution.py:22
  102.0 20.2 %pad_maximum_fusion = bf16[8192,1536]{1,0:T(8,128)(2,1)} fusion(bf16[8192,512]{1,0:T(8,128)(2,1)} %get-tuple-element.19, bf16[8192,512]{1,0:T(8,128)(2,1)} %get-tuple-element.18), kind=kLoop, calls=%fused_computation.2 | loop fusion | flops 75497472 | bytes 41943040 | tf_op jit(solution)/shard_map/concatenate | solution.py:118
  122.2 10.8 %all-to-all-done = bf16[64,2,64,256]{3,2,1,0:T(8,128)(2,1)} async-done(((bf16[64,2,64,256]{3,2,1,0:T(8,128)(2,1)}), bf16[64,2,64,256]{3,2,1,0:T(8,128)(2,1)}, u32[]{:S(2)}, u32[]{:S(2)}) %all-to-all-start) | async-done | bytes 4194336 | tf_op jit(solution)/shard_map/all_to_all | solution.py:109
  133.0 9.3 %fusion.40 = f32[1024,256]{1,0:T(8,128)S(1)} fusion(bf16[1024,8192]{0,1:T(8,128)(2,1)} %pad_maximum_fusion.1, bf16[8192,256]{1,0:T(8,128)(2,1)} %bitcast.9), kind=kOutput, calls=%fused_computation.95 | convolution fusion | flops 4294967296 | bytes 22020096 | tf_op jit(solution)/shard_map/dot_general | solution.py:112
  144.2 2.6 collective-permute-start.1
  150.5 1.9 collective-permute-start.5
  153.2 3.2 %collective-permute-done.4 = f32[256]{0:T(256)S(1)} collective-permute-done((f32[256]{0:T(256)S(1)}, f32[256]{0:T(256)S(1)}, u32[]{:S(2)}, u32[]{:S(2)}) %collective-permute-start.4) | collective-permute-done | bytes 1056 | tf_op jit(solution)/shard_map/ppermute | solution.py:47
  157.0 3.6 %collective-permute-start.8 = (f32[256]{0:T(256)S(1)}, f32[256]{0:T(256)S(1)}, u32[]{:S(2)}, u32[]{:S(2)}) collective-permute-start(f32[256]{0:T(256)S(1)} %bitcast.58), channel_id=1, source_target_pairs={{0,12},{4,0},{8,4},{12,8},{1,13},{5,1},{9,5},{13,9},{2,14},{6,2},{... | collective-permute-start | bytes 3080 | tf_op jit(solution)/shard_map/ppermute | solution.py:47
  161.3 3.2 %collective-permute-done.7 = f32[256]{0:T(256)S(1)} collective-permute-done((f32[256]{0:T(256)S(1)}, f32[256]{0:T(256)S(1)}, u32[]{:S(2)}, u32[]{:S(2)}) %collective-permute-start.7) | collective-permute-done | bytes 1056 | tf_op jit(solution)/shard_map/ppermute | solution.py:47
  165.4 20.0 %multiply_convert_fusion = bf16[8192,512]{1,0:T(8,128)(2,1)} fusion(bf16[8192,1536]{1,0:T(8,128)(2,1)} %pad_maximum_fusion, bf16[512,512]{1,0:T(8,128)(2,1)S(1)} %get-tuple-element.25, bf16[512,512]{1,0:T(8,128)(2,1)S(1)} %get-tuple-element.24), kind=kOutput, calls=%fused_computation.12 | convolution fusion | flops 12898009088 | bytes 34603008 | tf_op jit(solution)/shard_map/dot_general | solution.py:130
  185.5 107.4 %all_to_all.15 = bf16[64,2,64,512]{3,2,1,0:T(8,128)(2,1)} all-to-all(bf16[64,2,64,512]{3,2,1,0:T(8,128)(2,1)} %bitcast.48), channel_id=1, replica_groups=mesh['x'=4,'yl'=2,'z'=4,'c'=2,'pix'=2] {'x','yl','z','c'}, dimensions={0} | all-to-all | bytes 16777216 | tf_op jit(solution)/shard_map/all_to_all | solution.py:133
  292.9 11.5 %copy.27 = bf16[2,64,64,512]{3,2,1,0:T(8,128)(2,1)} copy(bf16[2,64,64,512]{3,1,0,2:T(8,128)(2,1)} %bitcast.45) | data formatting | bytes 16777216
  (41 shorter events, 11.7 us)
Async XLA Ops:
  5.9 15.5 %copy-start = (s32[4096]{0:T(1024)S(1)}, s32[4096]{0:T(1024)}, u32[]{:S(2)}) copy-start(s32[4096]{0:T(1024)} %param.5) | copy-start | bytes 49156
  5.9 15.6 %copy-start.2 = (s32[256]{0:T(256)S(1)}, s32[256]{0:T(256)}, u32[]{:S(2)}) copy-start(s32[256]{0:T(256)} %param.6) | copy-start | bytes 3076
  10.3 62.8 %all-to-all-start.1 = ((bf16[64,2,64,256]{3,2,1,0:T(8,128)(2,1)}), bf16[64,2,64,256]{3,2,1,0:T(8,128)(2,1)}, u32[]{:S(2)}, u32[]{:S(2)}) async-start(bf16[64,2,64,256]{3,2,1,0:T(8,128)(2,1)} %bitcast.47), calls=%async_computation.1 | async-start | bytes 8388608 | tf_op jit(solution)/shard_map/all_to_all | solution.py:109
  73.1 60.0 %all-to-all-start = ((bf16[64,2,64,256]{3,2,1,0:T(8,128)(2,1)}), bf16[64,2,64,256]{3,2,1,0:T(8,128)(2,1)}, u32[]{:S(2)}, u32[]{:S(2)}) async-start(bf16[64,2,64,256]{3,2,1,0:T(8,128)(2,1)} %bitcast.46), calls=%async_computation | async-start | bytes 8388608 | tf_op jit(solution)/shard_map/all_to_all | solution.py:109
  142.7 1.5 collective-permute-start
  144.2 3.9 %collective-permute-start.1 = (f32[256]{0:T(256)S(1)}, f32[256]{0:T(256)S(1)}, u32[]{:S(2)}, u32[]{:S(2)}) collective-permute-start(f32[256]{0:T(256)S(1)} %add.194), channel_id=1, source_target_pairs={{0,1},{1,0},{2,3},{3,2},{4,5},{5,4},{6,7},{7,6},{8,9},{9,8},{10,11... | collective-permute-start | bytes 3080 | tf_op jit(solution)/shard_map/ppermute | solution.py:44
  148.1 2.4 collective-permute-start.2
  150.5 2.7 collective-permute-start.5
  152.4 3.9 %collective-permute-start.4 = (f32[256]{0:T(256)S(1)}, f32[256]{0:T(256)S(1)}, u32[]{:S(2)}, u32[]{:S(2)}) collective-permute-start(f32[256]{0:T(256)S(1)} %add.196), channel_id=1, source_target_pairs={{0,64},{32,96},{64,0},{96,32},{1,65},{33,97},{65,1},{97,33},{2,66}... | collective-permute-start | bytes 3080 | tf_op jit(solution)/shard_map/ppermute | solution.py:47
  152.8 3.6 %collective-permute-start.3 = (f32[256]{0:T(256)S(1)}, f32[256]{0:T(256)S(1)}, u32[]{:S(2)}, u32[]{:S(2)}) collective-permute-start(f32[256]{0:T(256)S(1)} %add.196), channel_id=1, source_target_pairs={{0,32},{32,64},{64,96},{96,0},{1,33},{33,65},{65,97},{97,1},{2,34}... | collective-permute-start | bytes 3080 | tf_op jit(solution)/shard_map/ppermute | solution.py:47
  157.0 4.3 %collective-permute-start.8 = (f32[256]{0:T(256)S(1)}, f32[256]{0:T(256)S(1)}, u32[]{:S(2)}, u32[]{:S(2)}) collective-permute-start(f32[256]{0:T(256)S(1)} %bitcast.58), channel_id=1, source_target_pairs={{0,12},{4,0},{8,4},{12,8},{1,13},{5,1},{9,5},{13,9},{2,14},{6,2},{... | collective-permute-start | bytes 3080 | tf_op jit(solution)/shard_map/ppermute | solution.py:47
  160.6 3.9 %collective-permute-start.7 = (f32[256]{0:T(256)S(1)}, f32[256]{0:T(256)S(1)}, u32[]{:S(2)}, u32[]{:S(2)}) collective-permute-start(f32[256]{0:T(256)S(1)} %bitcast.59), channel_id=1, source_target_pairs={{0,8},{4,12},{8,0},{12,4},{1,9},{5,13},{9,1},{13,5},{2,10},{6,14},... | collective-permute-start | bytes 3080 | tf_op jit(solution)/shard_map/ppermute | solution.py:47
  160.6 3.9 %collective-permute-start.6 = (f32[256]{0:T(256)S(1)}, f32[256]{0:T(256)S(1)}, u32[]{:S(2)}, u32[]{:S(2)}) collective-permute-start(f32[256]{0:T(256)S(1)} %bitcast.60), channel_id=1, source_target_pairs={{0,4},{4,8},{8,12},{12,0},{1,5},{5,9},{9,13},{13,1},{2,6},{6,10},{... | collective-permute-start | bytes 3080 | tf_op jit(solution)/shard_map/ppermute | solution.py:47
  165.1 20.3 %copy-start.1 = (f32[1,256]{1,0:T(1,128)}, f32[1,256]{1,0:T(1,128)S(1)}, u32[]{:S(2)}) copy-start(f32[1,256]{1,0:T(1,128)S(1)} %add_sqrt_fusion) | copy-start | bytes 3076

commit v8 on v7

--- a/solution.py
+++ b/solution.py
@@ -38,7 +38,7 @@
 
 
 def global_sum(value):
-    for axis in ("c", "pix", "yl", "x", "z"):
+    for axis in (("c",), ("yl", "pix"), ("x",), ("z",)):
         size = lax.axis_size(axis)
         if size == 2:
             value = value + lax.ppermute(value, axis, [(0, 1), (1, 0)])

time: 305 us -> 305 us (level)
  other arithmetic: 56 us -> 48.4 us
  waiting for transfers between devices: 42.1 us -> 48.4 us
    all_to_all x2, waiting for transfers between devices: 32 us -> 39.5 us  [body(): moved = lax.all_to_all(send, ANG, split_axis=0, concat_axis=0, tiled=True)]
    ppermute x6 -> x9, starting transfers between devices: 6.76 us -> 11.4 us  [global_sum(): lax.ppermute(value, axis, [(i, (i + shift) % size) for i in range(size)])]
    concatenate x2, other arithmetic: 8.54 us -> 4.48 us  [real_table(): jnp.concatenate((jnp.concatenate((phase_cos, phase_sin), axis_ri), jnp.co...]
    ppermute x3 -> x1, starting transfers between devices: 4.33 us -> 0.64 us  [global_sum(): value = value + lax.ppermute(value, axis, [(0, 1), (1, 0)])]
    convert_element_type x2, other arithmetic: 14.7 us -> 11.2 us  [split_parts(): low = (value - high.astype(jnp.float32)).astype(jnp.bfloat16)]
    ppermute x6 -> x9, waiting for transfers between devices: 6.66 us -> 8.05 us  [global_sum(): lax.ppermute(value, axis, [(i, (i + shift) % size) for i in range(size)])]
  transfers between devices with their start and end apart: 11 -> 12, of which waited for: 9 -> 8; matrix products, arithmetic and copies ran while one was open for 23% -> 21% of each run, Pallas kernels for 0% -> 0%
where the time goes in v8:
time: 305 us; the launch traced here: 304 us
  blocking collectives  107 us (35%)
  other arithmetic  48.4 us (16%)
  waiting for transfers between devices  48.4 us (16%)
  matrix products  38.7 us (13%)
  starting transfers between devices  31.4 us (10%)
  local copies, waits for them, and re-layouts  29.6 us (10%)
    all_to_all x1, blocking collectives, body(): back = lax.all_to_all(update, ANG, split_axis=0, concat_axis=0, tiled=True)  107 us
    all_to_all x2, waiting for transfers between devices, body(): moved = lax.all_to_all(send, ANG, split_axis=0, concat_axis=0, tiled=True)  39.5 us
    unnamed x9, local copies, waits for them, and re-layouts  22.5 us
    concatenate x1, other arithmetic, body(): jnp.concatenate((backward_high, backward_low, backward_high), 1)  20.2 us
    dot_general x1, matrix products, body(): jnp.dot(backward_table, step_stack, preferred_element_type=jnp.float32)  20 us
    all_to_all x2, starting transfers between devices, body(): moved = lax.all_to_all(send, ANG, split_axis=0, concat_axis=0, tiled=True)  19.4 us
    dot_general x2, matrix products, body(): jnp.dot(forward_table, moved.reshape(depth, half), preferred_element_type...  18.7 us
    ppermute x9, starting transfers between devices, global_sum(): lax.ppermute(value, axis, [(i, (i + shift) % size) for i in range(size)])  11.4 us
  transfers between devices with their start and end apart: 12, of which 8 were waited for; matrix products, arithmetic and copies ran while one was open for 21% of the time, Pallas kernels for 0%

profile of v8, /device:TPU:1, one launch (start us, length us, event | category | flops | bytes accessed | tf_op | source)
XLA Modules:
  0.0 304.1 jit_solution(7895200824277533296)
XLA Ops:
  0.6 5.2 %fusion.40 = (bf16[2,64,64,256]{3,2,1,0:T(8,128)(2,1)S(1)}, bf16[2,64,64,256]{3,2,1,0:T(8,128)(2,1)}) fusion(bf16[2,64,64,512]{3,2,1,0:T(8,128)(2,1)} %param.4), kind=kLoop, calls=%fused_computation.105 | loop fusion | bytes 16777216 | tf_op jit(solution)/shard_map/slice | solution.py:108
  5.9 4.4 %copy.33 = bf16[2,64,64,256]{3,1,0,2:T(8,128)(2,1)} copy(bf16[2,64,64,256]{3,2,1,0:T(8,128)(2,1)S(1)} %get-tuple-element.22) | data formatting | bytes 8388608
  10.2 11.2 %all-to-all-start.1 = ((bf16[64,2,64,256]{3,2,1,0:T(8,128)(2,1)}), bf16[64,2,64,256]{3,2,1,0:T(8,128)(2,1)}, u32[]{:S(2)}, u32[]{:S(2)}) async-start(bf16[64,2,64,256]{3,2,1,0:T(8,128)(2,1)} %bitcast.53), calls=%async_computation.1 | async-start | bytes 8388608 | tf_op jit(solution)/shard_map/all_to_all | solution.py:109
  21.4 6.6 %copy.34 = bf16[2,64,64,256]{3,1,0,2:T(8,128)(2,1)} copy(bf16[2,64,64,256]{3,2,1,0:T(8,128)(2,1)} %get-tuple-element.23) | data formatting | bytes 8388608
  30.5 2.2 maximum_maximum_fusion
  32.8 3.7 %fusion.1 = (bf16[512,8192]{0,1:T(8,128)(2,1)S(1)}, bf16[512,8192]{0,1:T(8,128)(2,1)S(1)}) fusion(f32[512,64,2,64]{0,3,2,1:T(8,128)S(1)} %maximum_maximum_fusion), kind=kLoop, calls=%fused_computation.12 | loop fusion | flops 16777216 | bytes 33554432 | tf_op jit(solution)/shard_map/convert_element_type | solution.py:22
  36.5 7.2 %pad_maximum_fusion.1 = bf16[1024,8192]{0,1:T(8,128)(2,1)} fusion(bf16[512,8192]{0,1:T(8,128)(2,1)S(1)} %get-tuple-element.20, bf16[512,8192]{0,1:T(8,128)(2,1)S(1)} %get-tuple-element.21), kind=kLoop, calls=%fused_computation.5 | loop fusion | flops 33554432 | bytes 33554432 | tf_op jit(solution)/shard_map/concatenate | solution.py:104
  44.5 28.7 %all-to-all-done.1 = bf16[64,2,64,256]{3,2,1,0:T(8,128)(2,1)} async-done(((bf16[64,2,64,256]{3,2,1,0:T(8,128)(2,1)}), bf16[64,2,64,256]{3,2,1,0:T(8,128)(2,1)}, u32[]{:S(2)}, u32[]{:S(2)}) %all-to-all-start.1) | async-done | bytes 4194336 | tf_op jit(solution)/shard_map/all_to_all | solution.py:109
  73.2 8.2 %all-to-all-start = ((bf16[64,2,64,256]{3,2,1,0:T(8,128)(2,1)}), bf16[64,2,64,256]{3,2,1,0:T(8,128)(2,1)}, u32[]{:S(2)}, u32[]{:S(2)}) async-start(bf16[64,2,64,256]{3,2,1,0:T(8,128)(2,1)} %bitcast.52), calls=%async_computation | async-start | bytes 8388608 | tf_op jit(solution)/shard_map/all_to_all | solution.py:109
  81.4 9.4 %fusion.41 = f32[1024,256]{1,0:T(8,128)S(1)} fusion(bf16[1024,8192]{0,1:T(8,128)(2,1)} %pad_maximum_fusion.1, bf16[8192,256]{1,0:T(8,128)(2,1)} %bitcast.3), kind=kOutput, calls=%fused_computation.106 | convolution fusion | flops 4294967296 | bytes 22020096 | tf_op jit(solution)/shard_map/dot_general | solution.py:112
  92.5 2.2 maximum_maximum_fusion.1
  94.7 7.4 %fusion = (bf16[8192,512]{1,0:T(8,128)(2,1)}, bf16[8192,512]{1,0:T(8,128)(2,1)}) fusion(f32[64,2,64,512]{3,2,1,0:T(8,128)S(1)} %maximum_maximum_fusion.1), kind=kLoop, calls=%fused_computation.9 | loop fusion | flops 16777216 | bytes 33554432 | tf_op jit(solution)/shard_map/convert_element_type | solution.py:22
  102.1 20.2 %pad_maximum_fusion = bf16[8192,1536]{1,0:T(8,128)(2,1)} fusion(bf16[8192,512]{1,0:T(8,128)(2,1)} %get-tuple-element.19, bf16[8192,512]{1,0:T(8,128)(2,1)} %get-tuple-element.18), kind=kLoop, calls=%fused_computation.3 | loop fusion | flops 75497472 | bytes 41943040 | tf_op jit(solution)/shard_map/concatenate | solution.py:118
  122.3 10.8 %all-to-all-done = bf16[64,2,64,256]{3,2,1,0:T(8,128)(2,1)} async-done(((bf16[64,2,64,256]{3,2,1,0:T(8,128)(2,1)}), bf16[64,2,64,256]{3,2,1,0:T(8,128)(2,1)}, u32[]{:S(2)}, u32[]{:S(2)}) %all-to-all-start) | async-done | bytes 4194336 | tf_op jit(solution)/shard_map/all_to_all | solution.py:109
  133.1 9.3 %fusion.42 = f32[1024,256]{1,0:T(8,128)S(1)} fusion(bf16[1024,8192]{0,1:T(8,128)(2,1)} %pad_maximum_fusion.1, bf16[8192,256]{1,0:T(8,128)(2,1)} %bitcast.9), kind=kOutput, calls=%fused_computation.107 | convolution fusion | flops 4294967296 | bytes 22020096 | tf_op jit(solution)/shard_map/dot_general | solution.py:112
  144.3 2.5 collective-permute-start.3
  146.8 2.1 collective-permute-start.1
  151.0 2.4 collective-permute-start.6
  154.1 3.2 %collective-permute-done.5 = f32[256]{0:T(256)S(1)} collective-permute-done((f32[256]{0:T(256)S(1)}, f32[256]{0:T(256)S(1)}, u32[]{:S(2)}, u32[]{:S(2)}) %collective-permute-start.5) | collective-permute-done | bytes 1056 | tf_op jit(solution)/shard_map/ppermute | solution.py:47
  158.0 3.1 %collective-permute-start.9 = (f32[256]{0:T(256)S(1)}, f32[256]{0:T(256)S(1)}, u32[]{:S(2)}, u32[]{:S(2)}) collective-permute-start(f32[256]{0:T(256)S(1)} %bitcast.67), channel_id=1, source_target_pairs={{0,12},{4,0},{8,4},{12,8},{1,13},{5,1},{9,5},{13,9},{2,14},{6,2},{... | collective-permute-start | bytes 3080 | tf_op jit(solution)/shard_map/ppermute | solution.py:47
  161.7 3.2 %collective-permute-done.8 = f32[256]{0:T(256)S(1)} collective-permute-done((f32[256]{0:T(256)S(1)}, f32[256]{0:T(256)S(1)}, u32[]{:S(2)}, u32[]{:S(2)}) %collective-permute-start.8) | collective-permute-done | bytes 1056 | tf_op jit(solution)/shard_map/ppermute | solution.py:47
  165.8 20.0 %multiply_convert_fusion = bf16[8192,512]{1,0:T(8,128)(2,1)} fusion(bf16[8192,1536]{1,0:T(8,128)(2,1)} %pad_maximum_fusion, bf16[512,512]{1,0:T(8,128)(2,1)S(1)} %get-tuple-element.25, bf16[512,512]{1,0:T(8,128)(2,1)S(1)} %get-tuple-element.24), kind=kOutput, calls=%fused_computation.13 | convolution fusion | flops 12898009088 | bytes 34603008 | tf_op jit(solution)/shard_map/dot_general | solution.py:130
  185.9 106.7 %all_to_all.15 = bf16[64,2,64,512]{3,2,1,0:T(8,128)(2,1)} all-to-all(bf16[64,2,64,512]{3,2,1,0:T(8,128)(2,1)} %bitcast.54), channel_id=1, replica_groups=mesh['x'=4,'yl'=2,'z'=4,'c'=2,'pix'=2] {'x','yl','z','c'}, dimensions={0} | all-to-all | bytes 16777216 | tf_op jit(solution)/shard_map/all_to_all | solution.py:133
  292.6 11.5 %copy.27 = bf16[2,64,64,512]{3,2,1,0:T(8,128)(2,1)} copy(bf16[2,64,64,512]{3,1,0,2:T(8,128)(2,1)} %bitcast.51) | data formatting | bytes 16777216
  (46 shorter events, 11.7 us)
Async XLA Ops:
  10.2 17.8 %copy-start = (s32[4096]{0:T(1024)S(1)}, s32[4096]{0:T(1024)}, u32[]{:S(2)}) copy-start(s32[4096]{0:T(1024)} %param.5) | copy-start | bytes 49156
  10.2 18.0 %copy-start.2 = (s32[256]{0:T(256)S(1)}, s32[256]{0:T(256)}, u32[]{:S(2)}) copy-start(s32[256]{0:T(256)} %param.6) | copy-start | bytes 3076
  10.2 62.9 %all-to-all-start.1 = ((bf16[64,2,64,256]{3,2,1,0:T(8,128)(2,1)}), bf16[64,2,64,256]{3,2,1,0:T(8,128)(2,1)}, u32[]{:S(2)}, u32[]{:S(2)}) async-start(bf16[64,2,64,256]{3,2,1,0:T(8,128)(2,1)} %bitcast.53), calls=%async_computation.1 | async-start | bytes 8388608 | tf_op jit(solution)/shard_map/all_to_all | solution.py:109
  73.2 60.0 %all-to-all-start = ((bf16[64,2,64,256]{3,2,1,0:T(8,128)(2,1)}), bf16[64,2,64,256]{3,2,1,0:T(8,128)(2,1)}, u32[]{:S(2)}, u32[]{:S(2)}) async-start(bf16[64,2,64,256]{3,2,1,0:T(8,128)(2,1)} %bitcast.52), calls=%async_computation | async-start | bytes 8388608 | tf_op jit(solution)/shard_map/all_to_all | solution.py:109
  142.8 1.5 collective-permute-start
  144.3 4.7 %collective-permute-start.3 = (f32[256]{0:T(256)S(1)}, f32[256]{0:T(256)S(1)}, u32[]{:S(2)}, u32[]{:S(2)}) collective-permute-start(f32[256]{0:T(256)S(1)} %add.229), channel_id=1, source_target_pairs={{0,17},{1,0},{16,1},{17,16},{2,19},{3,2},{18,3},{19,18},{4,21},{5,... | collective-permute-start | bytes 3080 | tf_op jit(solution)/shard_map/ppermute | solution.py:47
  146.8 2.5 collective-permute-start.2
  146.8 3.6 %collective-permute-start.1 = (f32[256]{0:T(256)S(1)}, f32[256]{0:T(256)S(1)}, u32[]{:S(2)}, u32[]{:S(2)}) collective-permute-start(f32[256]{0:T(256)S(1)} %add.229), channel_id=1, source_target_pairs={{0,1},{1,16},{16,17},{17,0},{2,3},{3,18},{18,19},{19,2},{4,5},{5,2... | collective-permute-start | bytes 3080 | tf_op jit(solution)/shard_map/ppermute | solution.py:47
  151.0 3.1 %collective-permute-start.6 = (f32[256]{0:T(256)S(1)}, f32[256]{0:T(256)S(1)}, u32[]{:S(2)}, u32[]{:S(2)}) collective-permute-start(f32[256]{0:T(256)S(1)} %bitcast.64), channel_id=1, source_target_pairs={{0,96},{32,0},{64,32},{96,64},{1,97},{33,1},{65,33},{97,65},{2,98}... | collective-permute-start | bytes 3080 | tf_op jit(solution)/shard_map/ppermute | solution.py:47
  153.4 3.9 %collective-permute-start.5 = (f32[256]{0:T(256)S(1)}, f32[256]{0:T(256)S(1)}, u32[]{:S(2)}, u32[]{:S(2)}) collective-permute-start(f32[256]{0:T(256)S(1)} %bitcast.65), channel_id=1, source_target_pairs={{0,64},{32,96},{64,0},{96,32},{1,65},{33,97},{65,1},{97,33},{2,66}... | collective-permute-start | bytes 3080 | tf_op jit(solution)/shard_map/ppermute | solution.py:47
  153.7 3.6 %collective-permute-start.4 = (f32[256]{0:T(256)S(1)}, f32[256]{0:T(256)S(1)}, u32[]{:S(2)}, u32[]{:S(2)}) collective-permute-start(f32[256]{0:T(256)S(1)} %bitcast.66), channel_id=1, source_target_pairs={{0,32},{32,64},{64,96},{96,0},{1,33},{33,65},{65,97},{97,1},{2,34}... | collective-permute-start | bytes 3080 | tf_op jit(solution)/shard_map/ppermute | solution.py:47
  158.0 3.8 %collective-permute-start.9 = (f32[256]{0:T(256)S(1)}, f32[256]{0:T(256)S(1)}, u32[]{:S(2)}, u32[]{:S(2)}) collective-permute-start(f32[256]{0:T(256)S(1)} %bitcast.67), channel_id=1, source_target_pairs={{0,12},{4,0},{8,4},{12,8},{1,13},{5,1},{9,5},{13,9},{2,14},{6,2},{... | collective-permute-start | bytes 3080 | tf_op jit(solution)/shard_map/ppermute | solution.py:47
  161.0 3.9 %collective-permute-start.8 = (f32[256]{0:T(256)S(1)}, f32[256]{0:T(256)S(1)}, u32[]{:S(2)}, u32[]{:S(2)}) collective-permute-start(f32[256]{0:T(256)S(1)} %bitcast.68), channel_id=1, source_target_pairs={{0,8},{4,12},{8,0},{12,4},{1,9},{5,13},{9,1},{13,5},{2,10},{6,14},... | collective-permute-start | bytes 3080 | tf_op jit(solution)/shard_map/ppermute | solution.py:47
  161.2 3.7 %collective-permute-start.7 = (f32[256]{0:T(256)S(1)}, f32[256]{0:T(256)S(1)}, u32[]{:S(2)}, u32[]{:S(2)}) collective-permute-start(f32[256]{0:T(256)S(1)} %bitcast.69), channel_id=1, source_target_pairs={{0,4},{4,8},{8,12},{12,0},{1,5},{5,9},{9,13},{13,1},{2,6},{6,10},{... | collective-permute-start | bytes 3080 | tf_op jit(solution)/shard_map/ppermute | solution.py:47
  165.5 20.3 %copy-start.1 = (f32[1,256]{1,0:T(1,128)}, f32[1,256]{1,0:T(1,128)S(1)}, u32[]{:S(2)}) copy-start(f32[1,256]{1,0:T(1,128)S(1)} %add_sqrt_fusion) | copy-start | bytes 3076

commit v9 on v7

--- a/solution.py
+++ b/solution.py
@@ -105,7 +105,8 @@
 
     coefs = []
     for h in range(HALVES):
-        send = jnp.transpose(grads[:, :, :, h * half:(h + 1) * half], (2, 0, 1, 3))
+        source = grads if h == 0 else lax.optimization_barrier(grads)
+        send = jnp.transpose(source[:, :, :, h * half:(h + 1) * half], (2, 0, 1, 3))
         moved = lax.all_to_all(send, ANG, split_axis=0, concat_axis=0, tiled=True)
         if h == 1:
             moved, backward_table = lax.optimization_barrier((moved, backward_table))

time: 305 us -> 302 us (level)
  transfers between devices with their start and end apart: 11 -> 11, of which waited for: 9 -> 10; matrix products, arithmetic and copies ran while one was open for 23% -> 23% of each run, Pallas kernels for 0% -> 0%
where the time goes in v9:
time: 302 us; the launch traced here: 301 us
  blocking collectives  108 us (36%)
  other arithmetic  56.6 us (19%)
  waiting for transfers between devices  39.1 us (13%)
  matrix products  38.7 us (13%)
  starting transfers between devices  31.9 us (11%)
  local copies, waits for them, and re-layouts  26.1 us (9%)
    all_to_all x1, blocking collectives, body(): back = lax.all_to_all(update, ANG, split_axis=0, concat_axis=0, tiled=True)  108 us
    all_to_all x2, waiting for transfers between devices, body(): moved = lax.all_to_all(send, ANG, split_axis=0, concat_axis=0, tiled=True)  31.4 us
    concatenate x1, other arithmetic, body(): jnp.concatenate((backward_high, backward_low, backward_high), 1)  20.9 us
    unnamed x9, local copies, waits for them, and re-layouts  20.4 us
    dot_general x1, matrix products, body(): jnp.dot(backward_table, step_stack, preferred_element_type=jnp.float32)  20 us
    all_to_all x2, starting transfers between devices, body(): moved = lax.all_to_all(send, ANG, split_axis=0, concat_axis=0, tiled=True)  19.2 us
    dot_general x2, matrix products, body(): jnp.dot(forward_table, moved.reshape(depth, half), preferred_element_type...  18.7 us
    convert_element_type x2, other arithmetic, split_parts(): low = (value - high.astype(jnp.float32)).astype(jnp.bfloat16)  14.7 us
  transfers between devices with their start and end apart: 11, of which 10 were waited for; matrix products, arithmetic and copies ran while one was open for 23% of the time, Pallas kernels for 0%

profile of v9, /device:TPU:1, one launch (start us, length us, event | category | flops | bytes accessed | tf_op | source)
XLA Modules:
  0.0 301.2 jit_solution(17288108814145974578)
XLA Ops:
  0.6 2.2 slice-done
  2.8 4.4 %copy.33 = bf16[2,64,64,256]{3,1,0,2:T(8,128)(2,1)} copy(bf16[2,64,64,256]{3,2,1,0:T(8,128)(2,1)S(1)} %slice-done) | data formatting | bytes 8388608
  7.3 11.0 %all-to-all-start.1 = ((bf16[64,2,64,256]{3,2,1,0:T(8,128)(2,1)}), bf16[64,2,64,256]{3,2,1,0:T(8,128)(2,1)}, u32[]{:S(2)}, u32[]{:S(2)}) async-start(bf16[64,2,64,256]{3,2,1,0:T(8,128)(2,1)} %bitcast.46), calls=%async_computation.1 | async-start | bytes 8388608 | tf_op jit(solution)/shard_map/all_to_all | solution.py:110
  19.1 1.7 multiply_add_fusion.1
  20.8 6.3 %maximum_maximum_fusion = f32[512,64,2,64]{0,3,2,1:T(8,128)} fusion(f32[256,64,1,64]{0,3,2,1:T(8,128)S(1)} %get-tuple-element.29, f32[256,64,1,64]{0,3,2,1:T(8,128)S(1)} %get-tuple-element.28, f32[256,64,1,64]{0,3,2,1:T(8,128)S(1)} %get-tuple-element.27), kind=kLoop, calls=%fused_computation.3 | loop fusion | flops 12582912 | bytes 29360128 | tf_op jit(solution)/shard_map/concatenate | solution.py:82
  27.1 7.2 %fusion.1 = (bf16[512,8192]{0,1:T(8,128)(2,1)S(1)}, bf16[512,8192]{0,1:T(8,128)(2,1)S(1)}) fusion(f32[512,64,2,64]{0,3,2,1:T(8,128)} %maximum_maximum_fusion), kind=kLoop, calls=%fused_computation.11 | loop fusion | flops 16777216 | bytes 33554432 | tf_op jit(solution)/shard_map/convert_element_type | solution.py:22
  34.3 7.2 %pad_maximum_fusion.1 = bf16[1024,8192]{0,1:T(8,128)(2,1)} fusion(bf16[512,8192]{0,1:T(8,128)(2,1)S(1)} %get-tuple-element.20, bf16[512,8192]{0,1:T(8,128)(2,1)S(1)} %get-tuple-element.21), kind=kLoop, calls=%fused_computation.4 | loop fusion | flops 33554432 | bytes 33554432 | tf_op jit(solution)/shard_map/concatenate | solution.py:104
  41.5 2.2 slice-done.1
  43.7 4.4 %copy.34 = bf16[2,64,64,256]{3,1,0,2:T(8,128)(2,1)} copy(bf16[2,64,64,256]{3,2,1,0:T(8,128)(2,1)S(1)} %slice-done.1) | data formatting | bytes 8388608
  48.8 21.2 %all-to-all-done.1 = bf16[64,2,64,256]{3,2,1,0:T(8,128)(2,1)} async-done(((bf16[64,2,64,256]{3,2,1,0:T(8,128)(2,1)}), bf16[64,2,64,256]{3,2,1,0:T(8,128)(2,1)}, u32[]{:S(2)}, u32[]{:S(2)}) %all-to-all-start.1) | async-done | bytes 4194336 | tf_op jit(solution)/shard_map/all_to_all | solution.py:110
  70.1 8.2 %all-to-all-start = ((bf16[64,2,64,256]{3,2,1,0:T(8,128)(2,1)}), bf16[64,2,64,256]{3,2,1,0:T(8,128)(2,1)}, u32[]{:S(2)}, u32[]{:S(2)}) async-start(bf16[64,2,64,256]{3,2,1,0:T(8,128)(2,1)} %bitcast.47), calls=%async_computation | async-start | bytes 8388608 | tf_op jit(solution)/shard_map/all_to_all | solution.py:110
  78.3 9.4 %fusion.38 = f32[1024,256]{1,0:T(8,128)S(1)} fusion(bf16[1024,8192]{0,1:T(8,128)(2,1)} %pad_maximum_fusion.1, bf16[8192,256]{1,0:T(8,128)(2,1)} %bitcast.3), kind=kOutput, calls=%fused_computation.93 | convolution fusion | flops 4294967296 | bytes 22020096 | tf_op jit(solution)/shard_map/dot_general | solution.py:113
  87.6 1.7 multiply_add_fusion
  89.3 2.2 maximum_maximum_fusion.1
  91.6 7.4 %fusion = (bf16[8192,512]{1,0:T(8,128)(2,1)}, bf16[8192,512]{1,0:T(8,128)(2,1)}) fusion(f32[64,2,64,512]{3,2,1,0:T(8,128)S(1)} %maximum_maximum_fusion.1), kind=kLoop, calls=%fused_computation.8 | loop fusion | flops 16777216 | bytes 33554432 | tf_op jit(solution)/shard_map/convert_element_type | solution.py:22
  99.0 20.9 %pad_maximum_fusion = bf16[8192,1536]{1,0:T(8,128)(2,1)} fusion(bf16[8192,512]{1,0:T(8,128)(2,1)} %get-tuple-element.19, bf16[8192,512]{1,0:T(8,128)(2,1)} %get-tuple-element.18), kind=kLoop, calls=%fused_computation.2 | loop fusion | flops 75497472 | bytes 41943040 | tf_op jit(solution)/shard_map/concatenate | solution.py:119
  119.9 10.1 %all-to-all-done = bf16[64,2,64,256]{3,2,1,0:T(8,128)(2,1)} async-done(((bf16[64,2,64,256]{3,2,1,0:T(8,128)(2,1)}), bf16[64,2,64,256]{3,2,1,0:T(8,128)(2,1)}, u32[]{:S(2)}, u32[]{:S(2)}) %all-to-all-start) | async-done | bytes 4194336 | tf_op jit(solution)/shard_map/all_to_all | solution.py:110
  130.0 9.3 %fusion.39 = f32[1024,256]{1,0:T(8,128)S(1)} fusion(bf16[1024,8192]{0,1:T(8,128)(2,1)} %pad_maximum_fusion.1, bf16[8192,256]{1,0:T(8,128)(2,1)} %bitcast.9), kind=kOutput, calls=%fused_computation.94 | convolution fusion | flops 4294967296 | bytes 22020096 | tf_op jit(solution)/shard_map/dot_general | solution.py:113
  141.1 2.6 collective-permute-start.1
  148.0 2.6 collective-permute-start.4
  155.1 3.2 %collective-permute-start.7 = (f32[256]{0:T(256)S(1)}, f32[256]{0:T(256)S(1)}, u32[]{:S(2)}, u32[]{:S(2)}) collective-permute-start(f32[256]{0:T(256)S(1)} %bitcast.59), channel_id=1, source_target_pairs={{0,8},{4,12},{8,0},{12,4},{1,9},{5,13},{9,1},{13,5},{2,10},{6,14},... | collective-permute-start | bytes 3080 | tf_op jit(solution)/shard_map/ppermute | solution.py:47
  161.7 20.0 %multiply_convert_fusion = bf16[8192,512]{1,0:T(8,128)(2,1)} fusion(bf16[8192,1536]{1,0:T(8,128)(2,1)} %pad_maximum_fusion, bf16[512,512]{1,0:T(8,128)(2,1)S(1)} %get-tuple-element.23, bf16[512,512]{1,0:T(8,128)(2,1)S(1)} %get-tuple-element.22), kind=kOutput, calls=%fused_computation.12 | convolution fusion | flops 12898009088 | bytes 34603008 | tf_op jit(solution)/shard_map/dot_general | solution.py:131
  181.7 108.0 %all_to_all.15 = bf16[64,2,64,512]{3,2,1,0:T(8,128)(2,1)} all-to-all(bf16[64,2,64,512]{3,2,1,0:T(8,128)(2,1)} %bitcast.48), channel_id=1, replica_groups=mesh['x'=4,'yl'=2,'z'=4,'c'=2,'pix'=2] {'x','yl','z','c'}, dimensions={0} | all-to-all | bytes 16777216 | tf_op jit(solution)/shard_map/all_to_all | solution.py:134
  289.7 11.5 %copy.27 = bf16[2,64,64,512]{3,2,1,0:T(8,128)(2,1)} copy(bf16[2,64,64,512]{3,1,0,2:T(8,128)(2,1)} %bitcast.45) | data formatting | bytes 16777216
  (44 shorter events, 15.3 us)
Async XLA Ops:
  0.6 2.2 slice-start
  2.8 15.5 %copy-start = (s32[4096]{0:T(1024)S(1)}, s32[4096]{0:T(1024)}, u32[]{:S(2)}) copy-start(s32[4096]{0:T(1024)} %param.5) | copy-start | bytes 49156
  2.8 15.7 %copy-start.2 = (s32[256]{0:T(256)S(1)}, s32[256]{0:T(256)}, u32[]{:S(2)}) copy-start(s32[256]{0:T(256)} %param.6) | copy-start | bytes 3076
  7.3 62.8 %all-to-all-start.1 = ((bf16[64,2,64,256]{3,2,1,0:T(8,128)(2,1)}), bf16[64,2,64,256]{3,2,1,0:T(8,128)(2,1)}, u32[]{:S(2)}, u32[]{:S(2)}) async-start(bf16[64,2,64,256]{3,2,1,0:T(8,128)(2,1)} %bitcast.46), calls=%async_computation.1 | async-start | bytes 8388608 | tf_op jit(solution)/shard_map/all_to_all | solution.py:110
  41.5 2.2 slice-start.1
  70.1 60.0 %all-to-all-start = ((bf16[64,2,64,256]{3,2,1,0:T(8,128)(2,1)}), bf16[64,2,64,256]{3,2,1,0:T(8,128)(2,1)}, u32[]{:S(2)}, u32[]{:S(2)}) async-start(bf16[64,2,64,256]{3,2,1,0:T(8,128)(2,1)} %bitcast.47), calls=%async_computation | async-start | bytes 8388608 | tf_op jit(solution)/shard_map/all_to_all | solution.py:110
  139.7 1.5 collective-permute-start
  141.1 3.9 %collective-permute-start.1 = (f32[256]{0:T(256)S(1)}, f32[256]{0:T(256)S(1)}, u32[]{:S(2)}, u32[]{:S(2)}) collective-permute-start(f32[256]{0:T(256)S(1)} %add.194), channel_id=1, source_target_pairs={{0,1},{1,0},{2,3},{3,2},{4,5},{5,4},{6,7},{7,6},{8,9},{9,8},{10,11... | collective-permute-start | bytes 3080 | tf_op jit(solution)/shard_map/ppermute | solution.py:44
  145.1 2.4 collective-permute-start.2
  147.5 3.6 %collective-permute-start.3 = (f32[256]{0:T(256)S(1)}, f32[256]{0:T(256)S(1)}, u32[]{:S(2)}, u32[]{:S(2)}) collective-permute-start(f32[256]{0:T(256)S(1)} %add.196), channel_id=1, source_target_pairs={{0,32},{32,64},{64,96},{96,0},{1,33},{33,65},{65,97},{97,1},{2,34}... | collective-permute-start | bytes 3080 | tf_op jit(solution)/shard_map/ppermute | solution.py:47
  148.0 3.9 %collective-permute-start.4 = (f32[256]{0:T(256)S(1)}, f32[256]{0:T(256)S(1)}, u32[]{:S(2)}, u32[]{:S(2)}) collective-permute-start(f32[256]{0:T(256)S(1)} %add.196), channel_id=1, source_target_pairs={{0,64},{32,96},{64,0},{96,32},{1,65},{33,97},{65,1},{97,33},{2,66}... | collective-permute-start | bytes 3080 | tf_op jit(solution)/shard_map/ppermute | solution.py:47
  150.6 2.4 collective-permute-start.5
  153.6 5.1 %collective-permute-start.6 = (f32[256]{0:T(256)S(1)}, f32[256]{0:T(256)S(1)}, u32[]{:S(2)}, u32[]{:S(2)}) collective-permute-start(f32[256]{0:T(256)S(1)} %bitcast.58), channel_id=1, source_target_pairs={{0,4},{4,8},{8,12},{12,0},{1,5},{5,9},{9,13},{13,1},{2,6},{6,10},{... | collective-permute-start | bytes 3080 | tf_op jit(solution)/shard_map/ppermute | solution.py:47
  155.1 4.2 %collective-permute-start.7 = (f32[256]{0:T(256)S(1)}, f32[256]{0:T(256)S(1)}, u32[]{:S(2)}, u32[]{:S(2)}) collective-permute-start(f32[256]{0:T(256)S(1)} %bitcast.59), channel_id=1, source_target_pairs={{0,8},{4,12},{8,0},{12,4},{1,9},{5,13},{9,1},{13,5},{2,10},{6,14},... | collective-permute-start | bytes 3080 | tf_op jit(solution)/shard_map/ppermute | solution.py:47
  158.3 2.4 collective-permute-start.8
  161.4 20.3 %copy-start.1 = (f32[1,256]{1,0:T(1,128)}, f32[1,256]{1,0:T(1,128)S(1)}, u32[]{:S(2)}) copy-start(f32[1,256]{1,0:T(1,128)S(1)} %add_sqrt_fusion) | copy-start | bytes 3076

commit v10 on v9

--- a/solution.py
+++ b/solution.py
@@ -46,11 +46,7 @@
         parts = [value] + [
             lax.ppermute(value, axis, [(i, (i + shift) % size) for i in range(size)]) for shift in range(1, size)
         ]
-        order = (lax.axis_index(axis) - jnp.arange(size)) % size
-        ordered = jnp.stack(parts)[order]
-        value = ordered[0]
-        for position in range(1, size):
-            value = value + ordered[position]
+        value = (parts[0] + parts[2]) + (parts[1] + parts[3])
     return value
 
 

time: 302 us -> 301 us (level)
  transfers between devices with their start and end apart: 11 -> 11, of which waited for: 10 -> 9; matrix products, arithmetic and copies ran while one was open for 23% -> 23% of each run, Pallas kernels for 0% -> 0%
where the time goes in v10:
time: 301 us
  blocking collectives  108 us (36%)
  other arithmetic  56.6 us (19%)
  matrix products  38.7 us (13%)
  waiting for transfers between devices  38.2 us (13%)
  starting transfers between devices  33.3 us (11%)
  local copies, waits for them, and re-layouts  24.9 us (8%)
    all_to_all x1, blocking collectives, body(): back = lax.all_to_all(update, ANG, split_axis=0, concat_axis=0, tiled=True)  108 us
    all_to_all x2, waiting for transfers between devices, body(): moved = lax.all_to_all(send, ANG, split_axis=0, concat_axis=0, tiled=True)  31.4 us
    concatenate x1, other arithmetic, body(): jnp.concatenate((backward_high, backward_low, backward_high), 1)  20.9 us
    unnamed x9, local copies, waits for them, and re-layouts  20.4 us
    dot_general x1, matrix products, body(): jnp.dot(backward_table, step_stack, preferred_element_type=jnp.float32)  20 us
    all_to_all x2, starting transfers between devices, body(): moved = lax.all_to_all(send, ANG, split_axis=0, concat_axis=0, tiled=True)  19.2 us
    dot_general x2, matrix products, body(): jnp.dot(forward_table, moved.reshape(depth, half), preferred_element_type...  18.7 us
    convert_element_type x2, other arithmetic, split_parts(): low = (value - high.astype(jnp.float32)).astype(jnp.bfloat16)  14.7 us
  transfers between devices with their start and end apart: 11, of which 9 were waited for; matrix products, arithmetic and copies ran while one was open for 23% of the time, Pallas kernels for 0%

profile of v10, /device:TPU:1, one launch (start us, length us, event | category | flops | bytes accessed | tf_op | source)
XLA Modules:
  0.0 300.7 jit_solution(17722259516002636861)
XLA Ops:
  0.6 2.2 slice-done
  2.8 4.4 %copy.33 = bf16[2,64,64,256]{3,1,0,2:T(8,128)(2,1)} copy(bf16[2,64,64,256]{3,2,1,0:T(8,128)(2,1)S(1)} %slice-done) | data formatting | bytes 8388608
  7.3 11.0 %all-to-all-start.1 = ((bf16[64,2,64,256]{3,2,1,0:T(8,128)(2,1)}), bf16[64,2,64,256]{3,2,1,0:T(8,128)(2,1)}, u32[]{:S(2)}, u32[]{:S(2)}) async-start(bf16[64,2,64,256]{3,2,1,0:T(8,128)(2,1)} %bitcast.33), calls=%async_computation.1 | async-start | bytes 8388608 | tf_op jit(solution)/shard_map/all_to_all | solution.py:106
  19.1 1.7 multiply_add_fusion.1
  20.8 6.3 %maximum_maximum_fusion = f32[512,64,2,64]{0,3,2,1:T(8,128)} fusion(f32[256,64,1,64]{0,3,2,1:T(8,128)S(1)} %get-tuple-element.29, f32[256,64,1,64]{0,3,2,1:T(8,128)S(1)} %get-tuple-element.28, f32[256,64,1,64]{0,3,2,1:T(8,128)S(1)} %get-tuple-element.27), kind=kLoop, calls=%fused_computation.1 | loop fusion | flops 12582912 | bytes 29360128 | tf_op jit(solution)/shard_map/concatenate | solution.py:78
  27.1 7.2 %fusion.1 = (bf16[512,8192]{0,1:T(8,128)(2,1)S(1)}, bf16[512,8192]{0,1:T(8,128)(2,1)S(1)}) fusion(f32[512,64,2,64]{0,3,2,1:T(8,128)} %maximum_maximum_fusion), kind=kLoop, calls=%fused_computation.9 | loop fusion | flops 16777216 | bytes 33554432 | tf_op jit(solution)/shard_map/convert_element_type | solution.py:22
  34.3 7.2 %pad_maximum_fusion.1 = bf16[1024,8192]{0,1:T(8,128)(2,1)} fusion(bf16[512,8192]{0,1:T(8,128)(2,1)S(1)} %get-tuple-element.20, bf16[512,8192]{0,1:T(8,128)(2,1)S(1)} %get-tuple-element.21), kind=kLoop, calls=%fused_computation.2 | loop fusion | flops 33554432 | bytes 33554432 | tf_op jit(solution)/shard_map/concatenate | solution.py:100
  41.5 2.2 slice-done.1
  43.7 4.4 %copy.34 = bf16[2,64,64,256]{3,1,0,2:T(8,128)(2,1)} copy(bf16[2,64,64,256]{3,2,1,0:T(8,128)(2,1)S(1)} %slice-done.1) | data formatting | bytes 8388608
  48.8 21.2 %all-to-all-done.1 = bf16[64,2,64,256]{3,2,1,0:T(8,128)(2,1)} async-done(((bf16[64,2,64,256]{3,2,1,0:T(8,128)(2,1)}), bf16[64,2,64,256]{3,2,1,0:T(8,128)(2,1)}, u32[]{:S(2)}, u32[]{:S(2)}) %all-to-all-start.1) | async-done | bytes 4194336 | tf_op jit(solution)/shard_map/all_to_all | solution.py:106
  70.1 8.2 %all-to-all-start = ((bf16[64,2,64,256]{3,2,1,0:T(8,128)(2,1)}), bf16[64,2,64,256]{3,2,1,0:T(8,128)(2,1)}, u32[]{:S(2)}, u32[]{:S(2)}) async-start(bf16[64,2,64,256]{3,2,1,0:T(8,128)(2,1)} %bitcast.34), calls=%async_computation | async-start | bytes 8388608 | tf_op jit(solution)/shard_map/all_to_all | solution.py:106
  78.3 9.4 %fusion.33 = f32[1024,256]{1,0:T(8,128)S(1)} fusion(bf16[1024,8192]{0,1:T(8,128)(2,1)} %pad_maximum_fusion.1, bf16[8192,256]{1,0:T(8,128)(2,1)} %bitcast.3), kind=kOutput, calls=%fused_computation.69 | convolution fusion | flops 4294967296 | bytes 22020096 | tf_op jit(solution)/shard_map/dot_general | solution.py:109
  87.6 1.7 multiply_add_fusion
  89.3 2.2 maximum_maximum_fusion.1
  91.6 7.4 %fusion = (bf16[8192,512]{1,0:T(8,128)(2,1)}, bf16[8192,512]{1,0:T(8,128)(2,1)}) fusion(f32[64,2,64,512]{3,2,1,0:T(8,128)S(1)} %maximum_maximum_fusion.1), kind=kLoop, calls=%fused_computation.6 | loop fusion | flops 16777216 | bytes 33554432 | tf_op jit(solution)/shard_map/convert_element_type | solution.py:22
  99.0 20.9 %pad_maximum_fusion = bf16[8192,1536]{1,0:T(8,128)(2,1)} fusion(bf16[8192,512]{1,0:T(8,128)(2,1)} %get-tuple-element.19, bf16[8192,512]{1,0:T(8,128)(2,1)} %get-tuple-element.18), kind=kLoop, calls=%fused_computation | loop fusion | flops 75497472 | bytes 41943040 | tf_op jit(solution)/shard_map/concatenate | solution.py:115
  119.9 10.1 %all-to-all-done = bf16[64,2,64,256]{3,2,1,0:T(8,128)(2,1)} async-done(((bf16[64,2,64,256]{3,2,1,0:T(8,128)(2,1)}), bf16[64,2,64,256]{3,2,1,0:T(8,128)(2,1)}, u32[]{:S(2)}, u32[]{:S(2)}) %all-to-all-start) | async-done | bytes 4194336 | tf_op jit(solution)/shard_map/all_to_all | solution.py:106
  130.0 9.3 %fusion.34 = f32[1024,256]{1,0:T(8,128)S(1)} fusion(bf16[1024,8192]{0,1:T(8,128)(2,1)} %pad_maximum_fusion.1, bf16[8192,256]{1,0:T(8,128)(2,1)} %bitcast.9), kind=kOutput, calls=%fused_computation.70 | convolution fusion | flops 4294967296 | bytes 22020096 | tf_op jit(solution)/shard_map/dot_general | solution.py:109
  141.1 2.6 collective-permute-start.1
  152.4 3.2 %collective-permute-start.6 = (f32[256]{0:T(256)S(1)}, f32[256]{0:T(256)S(1)}, u32[]{:S(2)}, u32[]{:S(2)}) collective-permute-start(f32[256]{0:T(256)S(1)} %add_add_fusion), channel_id=1, source_target_pairs={{0,8},{4,12},{8,0},{12,4},{1,9},{5,13},{9,1},{13,5},{2,10},{6,14},... | collective-permute-start | bytes 3080 | tf_op jit(solution)/shard_map/ppermute | solution.py:47
  155.6 2.3 collective-permute-start.7
  160.9 20.0 %multiply_convert_fusion = bf16[8192,512]{1,0:T(8,128)(2,1)} fusion(bf16[8192,1536]{1,0:T(8,128)(2,1)} %pad_maximum_fusion, bf16[512,512]{1,0:T(8,128)(2,1)S(1)} %get-tuple-element.23, bf16[512,512]{1,0:T(8,128)(2,1)S(1)} %get-tuple-element.22), kind=kOutput, calls=%fused_computation.10 | convolution fusion | flops 12898009088 | bytes 34603008 | tf_op jit(solution)/shard_map/dot_general | solution.py:127
  180.9 108.2 %all_to_all.15 = bf16[64,2,64,512]{3,2,1,0:T(8,128)(2,1)} all-to-all(bf16[64,2,64,512]{3,2,1,0:T(8,128)(2,1)} %bitcast.35), channel_id=1, replica_groups=mesh['x'=4,'yl'=2,'z'=4,'c'=2,'pix'=2] {'x','yl','z','c'}, dimensions={0} | all-to-all | bytes 16777216 | tf_op jit(solution)/shard_map/all_to_all | solution.py:130
  289.1 11.5 %copy.27 = bf16[2,64,64,512]{3,2,1,0:T(8,128)(2,1)} copy(bf16[2,64,64,512]{3,1,0,2:T(8,128)(2,1)} %bitcast.32) | data formatting | bytes 16777216
  (36 shorter events, 14.9 us)
Async XLA Ops:
  0.6 2.2 slice-start
  2.8 15.5 %copy-start = (s32[4096]{0:T(1024)S(1)}, s32[4096]{0:T(1024)}, u32[]{:S(2)}) copy-start(s32[4096]{0:T(1024)} %param.5) | copy-start | bytes 49156
  2.8 15.7 %copy-start.2 = (s32[256]{0:T(256)S(1)}, s32[256]{0:T(256)}, u32[]{:S(2)}) copy-start(s32[256]{0:T(256)} %param.6) | copy-start | bytes 3076
  7.3 62.8 %all-to-all-start.1 = ((bf16[64,2,64,256]{3,2,1,0:T(8,128)(2,1)}), bf16[64,2,64,256]{3,2,1,0:T(8,128)(2,1)}, u32[]{:S(2)}, u32[]{:S(2)}) async-start(bf16[64,2,64,256]{3,2,1,0:T(8,128)(2,1)} %bitcast.33), calls=%async_computation.1 | async-start | bytes 8388608 | tf_op jit(solution)/shard_map/all_to_all | solution.py:106
  41.5 2.2 slice-start.1
  70.1 60.0 %all-to-all-start = ((bf16[64,2,64,256]{3,2,1,0:T(8,128)(2,1)}), bf16[64,2,64,256]{3,2,1,0:T(8,128)(2,1)}, u32[]{:S(2)}, u32[]{:S(2)}) async-start(bf16[64,2,64,256]{3,2,1,0:T(8,128)(2,1)} %bitcast.34), calls=%async_computation | async-start | bytes 8388608 | tf_op jit(solution)/shard_map/all_to_all | solution.py:106
  139.7 1.5 collective-permute-start
  141.1 3.9 %collective-permute-start.1 = (f32[256]{0:T(256)S(1)}, f32[256]{0:T(256)S(1)}, u32[]{:S(2)}, u32[]{:S(2)}) collective-permute-start(f32[256]{0:T(256)S(1)} %add.123), channel_id=1, source_target_pairs={{0,1},{1,0},{2,3},{3,2},{4,5},{5,4},{6,7},{7,6},{8,9},{9,8},{10,11... | collective-permute-start | bytes 3080 | tf_op jit(solution)/shard_map/ppermute | solution.py:44
  145.1 2.4 collective-permute-start.2
  147.5 3.9 %collective-permute-start.3 = (f32[256]{0:T(256)S(1)}, f32[256]{0:T(256)S(1)}, u32[]{:S(2)}, u32[]{:S(2)}) collective-permute-start(f32[256]{0:T(256)S(1)} %add.125), channel_id=1, source_target_pairs={{0,64},{32,96},{64,0},{96,32},{1,65},{33,97},{65,1},{97,33},{2,66}... | collective-permute-start | bytes 3080 | tf_op jit(solution)/shard_map/ppermute | solution.py:47
  148.7 3.6 %collective-permute-start.4 = (f32[256]{0:T(256)S(1)}, f32[256]{0:T(256)S(1)}, u32[]{:S(2)}, u32[]{:S(2)}) collective-permute-start(f32[256]{0:T(256)S(1)} %add.125), channel_id=1, source_target_pairs={{0,32},{32,64},{64,96},{96,0},{1,33},{33,65},{65,97},{97,1},{2,34}... | collective-permute-start | bytes 3080 | tf_op jit(solution)/shard_map/ppermute | solution.py:47
  150.0 2.4 collective-permute-start.5
  152.4 5.9 %collective-permute-start.6 = (f32[256]{0:T(256)S(1)}, f32[256]{0:T(256)S(1)}, u32[]{:S(2)}, u32[]{:S(2)}) collective-permute-start(f32[256]{0:T(256)S(1)} %add_add_fusion), channel_id=1, source_target_pairs={{0,8},{4,12},{8,0},{12,4},{1,9},{5,13},{9,1},{13,5},{2,10},{6,14},... | collective-permute-start | bytes 3080 | tf_op jit(solution)/shard_map/ppermute | solution.py:47
  155.6 3.6 %collective-permute-start.7 = (f32[256]{0:T(256)S(1)}, f32[256]{0:T(256)S(1)}, u32[]{:S(2)}, u32[]{:S(2)}) collective-permute-start(f32[256]{0:T(256)S(1)} %add_add_fusion), channel_id=1, source_target_pairs={{0,4},{4,8},{8,12},{12,0},{1,5},{5,9},{9,13},{13,1},{2,6},{6,10},{... | collective-permute-start | bytes 3080 | tf_op jit(solution)/shard_map/ppermute | solution.py:47
  157.9 2.7 collective-permute-start.8
  160.6 20.3 %copy-start.1 = (f32[256]{0:T(256)}, f32[256]{0:T(256)S(1)}, u32[]{:S(2)}) copy-start(f32[256]{0:T(256)S(1)} %add_sqrt_fusion) | copy-start | bytes 3076

commit v11 on v10

--- a/solution.py
+++ b/solution.py
@@ -38,7 +38,7 @@
 
 
 def global_sum(value):
-    for axis in ("c", "pix", "yl", "x", "z"):
+    for axis in (("c",), ("yl", "pix"), ("x",), ("z",)):
         size = lax.axis_size(axis)
         if size == 2:
             value = value + lax.ppermute(value, axis, [(0, 1), (1, 0)])

time: 301 us -> 302 us (level)
    ppermute x3 -> x1, starting transfers between devices: 4.33 us -> 0.64 us  [global_sum(): value = value + lax.ppermute(value, axis, [(0, 1), (1, 0)])]
    ppermute x6 -> x9, waiting for transfers between devices: 3.34 us -> 6.63 us  [global_sum(): lax.ppermute(value, axis, [(i, (i + shift) % size) for i in range(size)])]
    ppermute x6 -> x9, starting transfers between devices: 9.74 us -> 12.4 us  [global_sum(): lax.ppermute(value, axis, [(i, (i + shift) % size) for i in range(size)])]
  transfers between devices with their start and end apart: 11 -> 12, of which waited for: 9 -> 9; matrix products, arithmetic and copies ran while one was open for 23% -> 23% of each run, Pallas kernels for 0% -> 0%
where the time goes in v11:
time: 302 us; the launch traced here: 301 us
  blocking collectives  109 us (36%)
  other arithmetic  56.7 us (19%)
  matrix products  38.7 us (13%)
  waiting for transfers between devices  38.6 us (13%)
  starting transfers between devices  32.3 us (11%)
  local copies, waits for them, and re-layouts  24.9 us (8%)
    all_to_all x1, blocking collectives, body(): back = lax.all_to_all(update, ANG, split_axis=0, concat_axis=0, tiled=True)  109 us
    all_to_all x2, waiting for transfers between devices, body(): moved = lax.all_to_all(send, ANG, split_axis=0, concat_axis=0, tiled=True)  31.2 us
    concatenate x1, other arithmetic, body(): jnp.concatenate((backward_high, backward_low, backward_high), 1)  21.1 us
    unnamed x9, local copies, waits for them, and re-layouts  20.4 us
    dot_general x1, matrix products, body(): jnp.dot(backward_table, step_stack, preferred_element_type=jnp.float32)  20 us
    all_to_all x2, starting transfers between devices, body(): moved = lax.all_to_all(send, ANG, split_axis=0, concat_axis=0, tiled=True)  19.2 us
    dot_general x2, matrix products, body(): jnp.dot(forward_table, moved.reshape(depth, half), preferred_element_type...  18.7 us
    convert_element_type x2, other arithmetic, split_parts(): low = (value - high.astype(jnp.float32)).astype(jnp.bfloat16)  14.7 us
  transfers between devices with their start and end apart: 12, of which 9 were waited for; matrix products, arithmetic and copies ran while one was open for 23% of the time, Pallas kernels for 0%

profile of v11, /device:TPU:1, one launch (start us, length us, event | category | flops | bytes accessed | tf_op | source)
XLA Modules:
  0.0 300.8 jit_solution(14213185053089837300)
XLA Ops:
  0.6 2.2 slice-done
  2.8 4.4 %copy.33 = bf16[2,64,64,256]{3,1,0,2:T(8,128)(2,1)} copy(bf16[2,64,64,256]{3,2,1,0:T(8,128)(2,1)S(1)} %slice-done) | data formatting | bytes 8388608
  7.3 11.0 %all-to-all-start.1 = ((bf16[64,2,64,256]{3,2,1,0:T(8,128)(2,1)}), bf16[64,2,64,256]{3,2,1,0:T(8,128)(2,1)}, u32[]{:S(2)}, u32[]{:S(2)}) async-start(bf16[64,2,64,256]{3,2,1,0:T(8,128)(2,1)} %bitcast.33), calls=%async_computation.1 | async-start | bytes 8388608 | tf_op jit(solution)/shard_map/all_to_all | solution.py:106
  20.8 6.3 %maximum_maximum_fusion = f32[512,64,2,64]{0,3,2,1:T(8,128)} fusion(f32[256,64,1,64]{0,3,2,1:T(8,128)S(1)} %get-tuple-element.29, f32[256,64,1,64]{0,3,2,1:T(8,128)S(1)} %get-tuple-element.28, f32[256,64,1,64]{0,3,2,1:T(8,128)S(1)} %get-tuple-element.27), kind=kLoop, calls=%fused_computation.1 | loop fusion | flops 12582912 | bytes 29360128 | tf_op jit(solution)/shard_map/concatenate | solution.py:78
  27.1 7.2 %fusion.1 = (bf16[512,8192]{0,1:T(8,128)(2,1)S(1)}, bf16[512,8192]{0,1:T(8,128)(2,1)S(1)}) fusion(f32[512,64,2,64]{0,3,2,1:T(8,128)} %maximum_maximum_fusion), kind=kLoop, calls=%fused_computation.9 | loop fusion | flops 16777216 | bytes 33554432 | tf_op jit(solution)/shard_map/convert_element_type | solution.py:22
  34.3 7.2 %pad_maximum_fusion.1 = bf16[1024,8192]{0,1:T(8,128)(2,1)} fusion(bf16[512,8192]{0,1:T(8,128)(2,1)S(1)} %get-tuple-element.20, bf16[512,8192]{0,1:T(8,128)(2,1)S(1)} %get-tuple-element.21), kind=kLoop, calls=%fused_computation.2 | loop fusion | flops 33554432 | bytes 33554432 | tf_op jit(solution)/shard_map/concatenate | solution.py:100
  41.5 2.2 slice-done.1
  43.7 4.4 %copy.34 = bf16[2,64,64,256]{3,1,0,2:T(8,128)(2,1)} copy(bf16[2,64,64,256]{3,2,1,0:T(8,128)(2,1)S(1)} %slice-done.1) | data formatting | bytes 8388608
  48.8 21.2 %all-to-all-done.1 = bf16[64,2,64,256]{3,2,1,0:T(8,128)(2,1)} async-done(((bf16[64,2,64,256]{3,2,1,0:T(8,128)(2,1)}), bf16[64,2,64,256]{3,2,1,0:T(8,128)(2,1)}, u32[]{:S(2)}, u32[]{:S(2)}) %all-to-all-start.1) | async-done | bytes 4194336 | tf_op jit(solution)/shard_map/all_to_all | solution.py:106
  70.1 8.2 %all-to-all-start = ((bf16[64,2,64,256]{3,2,1,0:T(8,128)(2,1)}), bf16[64,2,64,256]{3,2,1,0:T(8,128)(2,1)}, u32[]{:S(2)}, u32[]{:S(2)}) async-start(bf16[64,2,64,256]{3,2,1,0:T(8,128)(2,1)} %bitcast.34), calls=%async_computation | async-start | bytes 8388608 | tf_op jit(solution)/shard_map/all_to_all | solution.py:106
  78.3 9.4 %fusion.33 = f32[1024,256]{1,0:T(8,128)S(1)} fusion(bf16[1024,8192]{0,1:T(8,128)(2,1)} %pad_maximum_fusion.1, bf16[8192,256]{1,0:T(8,128)(2,1)} %bitcast.3), kind=kOutput, calls=%fused_computation.70 | convolution fusion | flops 4294967296 | bytes 22020096 | tf_op jit(solution)/shard_map/dot_general | solution.py:109
  87.6 1.7 multiply_add_fusion
  89.3 2.2 maximum_maximum_fusion.1
  91.6 7.4 %fusion = (bf16[8192,512]{1,0:T(8,128)(2,1)}, bf16[8192,512]{1,0:T(8,128)(2,1)}) fusion(f32[64,2,64,512]{3,2,1,0:T(8,128)S(1)} %maximum_maximum_fusion.1), kind=kLoop, calls=%fused_computation.6 | loop fusion | flops 16777216 | bytes 33554432 | tf_op jit(solution)/shard_map/convert_element_type | solution.py:22
  99.0 21.1 %pad_maximum_fusion = bf16[8192,1536]{1,0:T(8,128)(2,1)} fusion(bf16[8192,512]{1,0:T(8,128)(2,1)} %get-tuple-element.19, bf16[8192,512]{1,0:T(8,128)(2,1)} %get-tuple-element.18), kind=kLoop, calls=%fused_computation | loop fusion | flops 75497472 | bytes 41943040 | tf_op jit(solution)/shard_map/concatenate | solution.py:115
  120.1 10.0 %all-to-all-done = bf16[64,2,64,256]{3,2,1,0:T(8,128)(2,1)} async-done(((bf16[64,2,64,256]{3,2,1,0:T(8,128)(2,1)}), bf16[64,2,64,256]{3,2,1,0:T(8,128)(2,1)}, u32[]{:S(2)}, u32[]{:S(2)}) %all-to-all-start) | async-done | bytes 4194336 | tf_op jit(solution)/shard_map/all_to_all | solution.py:106
  130.0 9.3 %fusion.34 = f32[1024,256]{1,0:T(8,128)S(1)} fusion(bf16[1024,8192]{0,1:T(8,128)(2,1)} %pad_maximum_fusion.1, bf16[8192,256]{1,0:T(8,128)(2,1)} %bitcast.9), kind=kOutput, calls=%fused_computation.71 | convolution fusion | flops 4294967296 | bytes 22020096 | tf_op jit(solution)/shard_map/dot_general | solution.py:109
  142.2 2.6 collective-permute-start.2
  145.8 2.9 collective-permute-done.3
  154.1 1.7 collective-permute-start.7
  155.8 2.0 collective-permute-start.8
  160.5 20.0 %multiply_convert_fusion = bf16[8192,512]{1,0:T(8,128)(2,1)} fusion(bf16[8192,1536]{1,0:T(8,128)(2,1)} %pad_maximum_fusion, bf16[512,512]{1,0:T(8,128)(2,1)S(1)} %get-tuple-element.23, bf16[512,512]{1,0:T(8,128)(2,1)S(1)} %get-tuple-element.22), kind=kOutput, calls=%fused_computation.10 | convolution fusion | flops 12898009088 | bytes 34603008 | tf_op jit(solution)/shard_map/dot_general | solution.py:127
  180.6 108.7 %all_to_all.15 = bf16[64,2,64,512]{3,2,1,0:T(8,128)(2,1)} all-to-all(bf16[64,2,64,512]{3,2,1,0:T(8,128)(2,1)} %bitcast.35), channel_id=1, replica_groups=mesh['x'=4,'yl'=2,'z'=4,'c'=2,'pix'=2] {'x','yl','z','c'}, dimensions={0} | all-to-all | bytes 16777216 | tf_op jit(solution)/shard_map/all_to_all | solution.py:130
  289.3 11.5 %copy.27 = bf16[2,64,64,512]{3,2,1,0:T(8,128)(2,1)} copy(bf16[2,64,64,512]{3,1,0,2:T(8,128)(2,1)} %bitcast.32) | data formatting | bytes 16777216
  (37 shorter events, 15.1 us)
Async XLA Ops:
  0.6 2.2 slice-start
  2.8 15.5 %copy-start = (s32[4096]{0:T(1024)S(1)}, s32[4096]{0:T(1024)}, u32[]{:S(2)}) copy-start(s32[4096]{0:T(1024)} %param.5) | copy-start | bytes 49156
  2.8 15.7 %copy-start.2 = (s32[256]{0:T(256)S(1)}, s32[256]{0:T(256)}, u32[]{:S(2)}) copy-start(s32[256]{0:T(256)} %param.6) | copy-start | bytes 3076
  7.3 62.8 %all-to-all-start.1 = ((bf16[64,2,64,256]{3,2,1,0:T(8,128)(2,1)}), bf16[64,2,64,256]{3,2,1,0:T(8,128)(2,1)}, u32[]{:S(2)}, u32[]{:S(2)}) async-start(bf16[64,2,64,256]{3,2,1,0:T(8,128)(2,1)} %bitcast.33), calls=%async_computation.1 | async-start | bytes 8388608 | tf_op jit(solution)/shard_map/all_to_all | solution.py:106
  41.5 2.2 slice-start.1
  70.1 60.0 %all-to-all-start = ((bf16[64,2,64,256]{3,2,1,0:T(8,128)(2,1)}), bf16[64,2,64,256]{3,2,1,0:T(8,128)(2,1)}, u32[]{:S(2)}, u32[]{:S(2)}) async-start(bf16[64,2,64,256]{3,2,1,0:T(8,128)(2,1)} %bitcast.34), calls=%async_computation | async-start | bytes 8388608 | tf_op jit(solution)/shard_map/all_to_all | solution.py:106
  139.7 1.5 collective-permute-start
  141.1 3.7 %collective-permute-start.1 = (f32[256]{0:T(256)S(1)}, f32[256]{0:T(256)S(1)}, u32[]{:S(2)}, u32[]{:S(2)}) collective-permute-start(f32[256]{0:T(256)S(1)} %add.126), channel_id=1, source_target_pairs={{0,16},{1,17},{16,0},{17,1},{2,18},{3,19},{18,2},{19,3},{4,20},{5,... | collective-permute-start | bytes 3080 | tf_op jit(solution)/shard_map/ppermute | solution.py:47
  142.2 3.6 %collective-permute-start.2 = (f32[256]{0:T(256)S(1)}, f32[256]{0:T(256)S(1)}, u32[]{:S(2)}, u32[]{:S(2)}) collective-permute-start(f32[256]{0:T(256)S(1)} %add.126), channel_id=1, source_target_pairs={{0,1},{1,16},{16,17},{17,0},{2,3},{3,18},{18,19},{19,2},{4,5},{5,2... | collective-permute-start | bytes 3080 | tf_op jit(solution)/shard_map/ppermute | solution.py:47
  144.8 3.9 %collective-permute-start.3 = (f32[256]{0:T(256)S(1)}, f32[256]{0:T(256)S(1)}, u32[]{:S(2)}, u32[]{:S(2)}) collective-permute-start(f32[256]{0:T(256)S(1)} %add.126), channel_id=1, source_target_pairs={{0,17},{1,0},{16,1},{17,16},{2,19},{3,2},{18,3},{19,18},{4,21},{5,... | collective-permute-start | bytes 3080 | tf_op jit(solution)/shard_map/ppermute | solution.py:47
  148.8 4.3 %collective-permute-start.4 = (f32[256]{0:T(256)S(1)}, f32[256]{0:T(256)S(1)}, u32[]{:S(2)}, u32[]{:S(2)}) collective-permute-start(f32[256]{0:T(256)S(1)} %add_add_fusion.1), channel_id=1, source_target_pairs={{0,64},{32,96},{64,0},{96,32},{1,65},{33,97},{65,1},{97,33},{2,66}... | collective-permute-start | bytes 3080 | tf_op jit(solution)/shard_map/ppermute | solution.py:47
  150.4 3.6 %collective-permute-start.5 = (f32[256]{0:T(256)S(1)}, f32[256]{0:T(256)S(1)}, u32[]{:S(2)}, u32[]{:S(2)}) collective-permute-start(f32[256]{0:T(256)S(1)} %add_add_fusion.1), channel_id=1, source_target_pairs={{0,32},{32,64},{64,96},{96,0},{1,33},{33,65},{65,97},{97,1},{2,34}... | collective-permute-start | bytes 3080 | tf_op jit(solution)/shard_map/ppermute | solution.py:47
  151.7 2.4 collective-permute-start.6
  154.1 4.4 %collective-permute-start.7 = (f32[256]{0:T(256)S(1)}, f32[256]{0:T(256)S(1)}, u32[]{:S(2)}, u32[]{:S(2)}) collective-permute-start(f32[256]{0:T(256)S(1)} %add_add_fusion), channel_id=1, source_target_pairs={{0,8},{4,12},{8,0},{12,4},{1,9},{5,13},{9,1},{13,5},{2,10},{6,14},... | collective-permute-start | bytes 3080 | tf_op jit(solution)/shard_map/ppermute | solution.py:47
  155.8 3.6 %collective-permute-start.8 = (f32[256]{0:T(256)S(1)}, f32[256]{0:T(256)S(1)}, u32[]{:S(2)}, u32[]{:S(2)}) collective-permute-start(f32[256]{0:T(256)S(1)} %add_add_fusion), channel_id=1, source_target_pairs={{0,4},{4,8},{8,12},{12,0},{1,5},{5,9},{9,13},{13,1},{2,6},{6,10},{... | collective-permute-start | bytes 3080 | tf_op jit(solution)/shard_map/ppermute | solution.py:47
  157.8 2.4 collective-permute-start.9
  160.2 20.3 %copy-start.1 = (f32[256]{0:T(256)}, f32[256]{0:T(256)S(1)}, u32[]{:S(2)}) copy-start(f32[256]{0:T(256)S(1)} %add_sqrt_fusion) | copy-start | bytes 3076
